TPU v7x, 128 devices: a whole 4x4x4 slice. The times are simulated.
128 devices in a mesh: leaf: 16 (over z, x), panel: 8 (over y, core).
Axes of the slice: x: 4, y: 4, z: 4, core: 2. Of those that a mesh axis runs over, the one named last changes fastest.
Arguments:
- child_front: float32 [16, 2048, 2048], P('leaf', 'panel'), as said below
- child_panel: bfloat16 [16, 2048, 4096], P('leaf'), may hold values from -0.03125 to 0.03125
- parent_front: float32 [4096, 4096], P('leaf', 'panel'), as said below
- tile_map: int32 [16, 8], P('leaf'), may hold values from 0 to 15, as said below
- tile_count: int32 [16], P('leaf'), may hold values from 2 to 8, as said below
Outputs:
- eliminated: float32 [4096, 4096], P('leaf', 'panel')
Inputs may be any that keep to these rules, and one draw needn't show every extreme that they name: `tile_count`: some child has 8 live tiles and some child has 2. `tile_map`: for child c the first tile_count[c] entries are distinct and rising; the other entries are 0. Each child's block is symmetric, and child_front[c] - child_panel[c] child_panel[c]^T is positive definite. `parent_front`: symmetric positive definite.
All inputs are finite; a program needn't handle non-finite values.
Results may differ from a plain program's by a relative error of at most 0.0003.
Values sent between devices are 32-bit elements; how exact they have to be, the bound alone decides.
No kernel may reach another device: no remote copies, remote signals or barrier semaphores. Data moves between devices by JAX's collectives and lax.ppermute only.
A program may use at most 128 MiB of HBM per device.

v0:
```python
import jax
import jax.numpy as jnp
from jax import lax
from jax.sharding import PartitionSpec as P

TILE = 256
NF = 4096
CB = 2048
STEPS = 4


def spread(array, axis, root):
    mine = lax.axis_index(axis) == root
    return lax.psum(jnp.where(mine, array, jnp.zeros_like(array)), axis)


def finish_rows(block, row_index, factor, pivot_start):
    solved = lax.linalg.triangular_solve(
        factor, block, left_side=False, lower=True, transpose_a=True
    )
    offset = jnp.clip(row_index - pivot_start, 0, TILE - 1)
    own_rows = jnp.take(factor, offset, axis=0)
    inside = (row_index >= pivot_start) & (row_index < pivot_start + TILE)
    kept = jnp.where(inside[:, None], own_rows, solved)
    return jnp.where(row_index[:, None] < pivot_start, 0.0, kept)


def shards(child_front, child_panel, parent_front, tile_map, tile_count):
    highest = lax.Precision.HIGHEST
    panel_count = lax.axis_size("panel")
    leaf_id = lax.axis_index("leaf")
    panel_id = lax.axis_index("panel")
    tiles_child = CB // TILE
    tiles_front = NF // TILE
    pivot_span = STEPS * TILE
    child_rows = child_front.shape[1]
    height = parent_front.shape[0]
    col_width = parent_front.shape[1]
    panel_all = child_panel[0]
    own_panel = lax.dynamic_slice_in_dim(panel_all, panel_id * child_rows, child_rows, 0)
    update = child_front[0] - lax.dot_general(
        own_panel, panel_all, (((1,), (1,)), ((), ())), preferred_element_type=jnp.float32
    )
    mapped = tile_map[0]
    live_tiles = jnp.arange(tiles_child, dtype=jnp.int32) < tile_count[0]
    everywhere = jnp.arange(tiles_front, dtype=jnp.int32)
    chosen = ((mapped[None, :] == everywhere[:, None]) & live_tiles[None, :]).astype(jnp.float32)
    placed = jnp.einsum(
        "rtb,ft->rfb", update.reshape(child_rows, tiles_child, TILE), chosen, precision=highest
    )
    placed = placed.reshape(child_rows, panel_count, col_width)
    moved_cols = lax.all_to_all(placed, "panel", split_axis=1, concat_axis=0, tiled=True)
    column_tiles = moved_cols.reshape(tiles_child, TILE, col_width)
    targets = jnp.arange(lax.axis_size("leaf") * height // TILE, dtype=jnp.int32)
    picked = ((mapped[None, :] == targets[:, None]) & live_tiles[None, :]).astype(jnp.float32)
    front_block = parent_front + lax.psum_scatter(
        jnp.einsum("ft,tbc->fbc", picked, column_tiles, precision=highest).reshape(
            lax.axis_size("leaf") * height, col_width
        ),
        "leaf",
        scatter_dimension=0,
        tiled=True,
    )
    global_rows = leaf_id * height + jnp.arange(height, dtype=jnp.int32)
    global_cols = panel_id * col_width + jnp.arange(col_width, dtype=jnp.int32)
    col_tiles = col_width // TILE
    for pivot_step in range(STEPS):
        source_panel = pivot_step // col_tiles
        local_start = pivot_step % col_tiles * TILE
        pivot_start = pivot_step * TILE
        source = front_block[:, local_start : local_start + TILE]
        column = spread(source, "panel", source_panel)
        full_column = lax.all_gather(column, "leaf", axis=0, tiled=True)
        factor = jnp.linalg.cholesky(full_column[pivot_start : pivot_start + TILE])
        own_factor = finish_rows(column, global_rows, factor, pivot_start)
        col_factor = finish_rows(
            lax.dynamic_slice_in_dim(full_column, panel_id * col_width, col_width, 0),
            global_cols,
            factor,
            pivot_start,
        )
        front_block = front_block - lax.dot_general(
            own_factor,
            col_factor,
            (((1,), (1,)), ((), ())),
            precision=highest,
            preferred_element_type=jnp.float32,
        )
        replaced = jnp.where(
            panel_id == source_panel, own_factor, front_block[:, local_start : local_start + TILE]
        )
        front_block = front_block.at[:, local_start : local_start + TILE].set(replaced)
    upper_zone = (global_rows[:, None] < pivot_span) & (global_cols[None, :] >= pivot_span)
    return jnp.where(upper_zone, 0.0, front_block)


def solution(mesh):
    placed = (
        P("leaf", "panel", None),
        P("leaf", None, None),
        P("leaf", "panel"),
        P("leaf", None),
        P("leaf"),
    )
    return jax.shard_map(
        shards, mesh=mesh, in_specs=placed, out_specs=P("leaf", "panel"), check_vma=False
    )
```

profile of v0, /device:TPU:1, one launch (start us, length us, event | category | flops | bytes accessed | tf_op | source)
XLA Modules:
  0.0 963.8 jit_solution(7068307118465232745)
XLA Ops:
  6.5 11.5 %fusion.2 = f32[256,2048]{1,0:T(8,128)S(1)} fusion(bf16[1,2048,4096]{2,1,0:T(8,128)(2,1)} %param.23, f32[1,256,2048]{2,1,0:T(8,128)} %param.22, s32[]{:T(128)S(6)} %select_n.120), kind=kOutput, calls=%fused_computation.18 | convolution fusion | flops 4295491584 | bytes 23068676 | tf_op jit(solution)/shard_map/dot_general | solution.py:41
  19.6 3.6 convolution_bitcast_fusion
  23.2 5.2 reshape.226
  28.4 4.6 copy.25
  33.0 54.7 %all_to_all.15 = f32[256,8,512]{2,0,1:T(8,128)} all-to-all(f32[256,8,512]{2,0,1:T(8,128)S(1)} %copy.25), channel_id=1, replica_groups=mesh['leaf'=16,'panel'=8] {'panel'}, dimensions={1} | all-to-all | bytes 8388608 | tf_op jit(solution)/shard_map/all_to_all | solution.py:52
  87.7 5.5 copy.46
  93.2 5.5 fusion.118
  98.7 11.3 %copy.54 = f32[64,8,16,256]{3,1,2,0:T(8,128)} copy(f32[64,8,16,256]{3,2,1,0:T(8,128)S(1)} %bitcast.200) | data formatting | bytes 16777216
  111.3 84.5 %reduce-scatter.2.cloned.1.call-done = f32[256,512]{0,1:T(8,128)} async-done(((f32[4096,512]{0,1:T(8,128)}), f32[256,512]{0,1:T(8,128)}) %reduce-scatter.2.cloned.1.call-update) | async-done | bytes 524304 | tf_op jit(solution)/shard_map/reduce_scatter | solution.py:56
  195.8 1.1 add.140
  197.7 59.3 %all-reduce.6.cloned.1.call-done = f32[256,256]{0,1:T(8,128)} async-done(((f32[256,256]{0,1:T(8,128)}), f32[256,256]{0,1:T(8,128)}) %all-reduce.6.cloned.1.call-update) | async-done | bytes 262160 | tf_op jit(solution)/shard_map/psum | solution.py:14
  258.0 57.9 %all-gather.5.cloned.1.call-done = f32[4096,256]{0,1:T(8,128)} async-done(((f32[256,256]{0,1:T(8,128)}), f32[4096,256]{0,1:T(8,128)}) %all-gather.5.cloned.1.call-update) | async-done | bytes 4194320 | tf_op jit(solution)/shard_map/all_gather | solution.py:73
  318.0 11.7 %cholesky.214 = f32[128,128]{1,0:T(8,128)S(1)} custom-call(f32[128,128]{1,0:T(8,128)S(1)} %cholesky.346), custom_call_target="Cholesky" | custom-call | tf_op jit(solution)/shard_map/jit(cholesky)/cholesky | solution.py:74
  329.8 9.8 %custom-call.23 = f32[1,128,128]{1,2,0:T(8,128)S(1)} custom-call(f32[1,128,128]{2,1,0:T(8,128)S(1)} %get-tuple-element.181), custom_call_target="InvertDiagBlocksLowerTriangular" | custom-call | tf_op jit(solution)/shard_map/jit(cholesky)/cholesky | solution.py:74
  340.1 11.7 %cholesky.231 = f32[128,128]{1,0:T(8,128)S(1)} custom-call(f32[128,128]{1,0:T(8,128)S(1)} %convolution_subtract_fusion.15), custom_call_target="Cholesky" | custom-call | tf_op jit(solution)/shard_map/jit(cholesky)/cholesky | solution.py:74
  354.0 4.2 while.20
  354.7 1.4 bitcast_dynamic-update-slice_fusion.8
  356.8 1.4 bitcast_dynamic-update-slice_fusion.8
  358.2 20.1 %custom-call.24 = f32[2,128,128]{1,2,0:T(8,128)S(1)} custom-call(f32[2,128,128]{2,1,0:T(8,128)S(1)} %get-tuple-element.110), custom_call_target="InvertDiagBlocksLowerTriangular" | custom-call | tf_op jit(solution)/shard_map/triangular_solve/custom-call.0 | solution.py:18
  379.2 1.4 fusion.37
  380.6 1.3 convolution_subtract_fusion.7
  382.3 1.6 gather_fusion.1
  385.2 1.0 convolution_subtract_fusion.3
  387.8 58.9 %all-reduce.8.cloned.1.call-done = f32[256,256]{0,1:T(8,128)} async-done(((f32[256,256]{0,1:T(8,128)}), f32[256,256]{0,1:T(8,128)}) %all-reduce.8.cloned.1.call-update) | async-done | bytes 262160 | tf_op jit(solution)/shard_map/psum | solution.py:14
  447.1 58.4 %all-gather.7.cloned.1.call-done = f32[4096,256]{0,1:T(8,128)} async-done(((f32[256,256]{0,1:T(8,128)}), f32[4096,256]{0,1:T(8,128)}) %all-gather.7.cloned.1.call-update) | async-done | bytes 4194320 | tf_op jit(solution)/shard_map/all_gather | solution.py:73
  507.6 11.7 %cholesky.248 = f32[128,128]{1,0:T(8,128)S(1)} custom-call(f32[128,128]{1,0:T(8,128)S(1)} %cholesky.349), custom_call_target="Cholesky" | custom-call | tf_op jit(solution)/shard_map/jit(cholesky)/cholesky | solution.py:74
  519.4 9.8 %custom-call.26 = f32[1,128,128]{1,2,0:T(8,128)S(1)} custom-call(f32[1,128,128]{2,1,0:T(8,128)S(1)} %get-tuple-element.177), custom_call_target="InvertDiagBlocksLowerTriangular" | custom-call | tf_op jit(solution)/shard_map/jit(cholesky)/cholesky | solution.py:74
  529.7 11.7 %cholesky.265 = f32[128,128]{1,0:T(8,128)S(1)} custom-call(f32[128,128]{1,0:T(8,128)S(1)} %convolution_subtract_fusion.14), custom_call_target="Cholesky" | custom-call | tf_op jit(solution)/shard_map/jit(cholesky)/cholesky | solution.py:74
  544.2 4.4 while.21
  545.1 1.4 bitcast_dynamic-update-slice_fusion.9
  547.2 1.4 bitcast_dynamic-update-slice_fusion.9
  548.6 19.7 %custom-call.27 = f32[2,128,128]{1,2,0:T(8,128)S(1)} custom-call(f32[2,128,128]{2,1,0:T(8,128)S(1)} %get-tuple-element.112), custom_call_target="InvertDiagBlocksLowerTriangular" | custom-call | tf_op jit(solution)/shard_map/triangular_solve/custom-call.0 | solution.py:18
  569.2 1.4 fusion.35
  570.6 1.3 convolution_subtract_fusion.6
  572.4 1.6 gather_fusion.3
  575.3 1.0 convolution_subtract_fusion.2
  577.2 58.9 %all-reduce.10.cloned.1.call-done = f32[256,256]{0,1:T(8,128)} async-done(((f32[256,256]{0,1:T(8,128)}), f32[256,256]{0,1:T(8,128)}) %all-reduce.10.cloned.1.call-update) | async-done | bytes 262160 | tf_op jit(solution)/shard_map/psum | solution.py:14
  636.5 58.5 %all-gather.9.cloned.1.call-done = f32[4096,256]{0,1:T(8,128)} async-done(((f32[256,256]{0,1:T(8,128)}), f32[4096,256]{0,1:T(8,128)}) %all-gather.9.cloned.1.call-update) | async-done | bytes 4194320 | tf_op jit(solution)/shard_map/all_gather | solution.py:73
  697.1 11.7 %cholesky.282 = f32[128,128]{1,0:T(8,128)S(1)} custom-call(f32[128,128]{1,0:T(8,128)S(1)} %cholesky.352), custom_call_target="Cholesky" | custom-call | tf_op jit(solution)/shard_map/jit(cholesky)/cholesky | solution.py:74
  708.9 9.8 %custom-call.29 = f32[1,128,128]{1,2,0:T(8,128)S(1)} custom-call(f32[1,128,128]{2,1,0:T(8,128)S(1)} %get-tuple-element.173), custom_call_target="InvertDiagBlocksLowerTriangular" | custom-call | tf_op jit(solution)/shard_map/jit(cholesky)/cholesky | solution.py:74
  719.2 11.7 %cholesky.299 = f32[128,128]{1,0:T(8,128)S(1)} custom-call(f32[128,128]{1,0:T(8,128)S(1)} %convolution_subtract_fusion.13), custom_call_target="Cholesky" | custom-call | tf_op jit(solution)/shard_map/jit(cholesky)/cholesky | solution.py:74
  733.7 4.6 while.22
  734.8 1.4 bitcast_dynamic-update-slice_fusion.10
  736.9 1.4 bitcast_dynamic-update-slice_fusion.10
  738.3 19.7 %custom-call.30 = f32[2,128,128]{1,2,0:T(8,128)S(1)} custom-call(f32[2,128,128]{2,1,0:T(8,128)S(1)} %get-tuple-element.114), custom_call_target="InvertDiagBlocksLowerTriangular" | custom-call | tf_op jit(solution)/shard_map/triangular_solve/custom-call.0 | solution.py:18
  758.9 1.4 fusion.32
  760.3 1.3 convolution_subtract_fusion.5
  762.1 1.6 gather_fusion.5
  765.0 1.0 convolution_subtract_fusion.1
  767.7 58.7 %all-reduce.12.cloned.1.call-done = f32[256,256]{0,1:T(8,128)} async-done(((f32[256,256]{0,1:T(8,128)}), f32[256,256]{0,1:T(8,128)}) %all-reduce.12.cloned.1.call-update) | async-done | bytes 262160 | tf_op jit(solution)/shard_map/psum | solution.py:14
  826.5 58.8 %all-gather.11.cloned.1.call-done = f32[4096,256]{0,1:T(8,128)} async-done(((f32[256,256]{0,1:T(8,128)}), f32[4096,256]{0,1:T(8,128)}) %all-gather.11.cloned.1.call-update) | async-done | bytes 4194320 | tf_op jit(solution)/shard_map/all_gather | solution.py:73
  886.5 1.0 fusion.43
  887.5 11.7 %cholesky.316 = f32[128,128]{1,0:T(8,128)S(1)} custom-call(f32[128,128]{1,0:T(8,128)S(1)} %cholesky.355), custom_call_target="Cholesky" | custom-call | tf_op jit(solution)/shard_map/jit(cholesky)/cholesky | solution.py:74
  899.2 9.8 %custom-call.32 = f32[1,128,128]{1,2,0:T(8,128)S(1)} custom-call(f32[1,128,128]{2,1,0:T(8,128)S(1)} %get-tuple-element.169), custom_call_target="InvertDiagBlocksLowerTriangular" | custom-call | tf_op jit(solution)/shard_map/jit(cholesky)/cholesky | solution.py:74
  909.5 11.7 %cholesky.333 = f32[128,128]{1,0:T(8,128)S(1)} custom-call(f32[128,128]{1,0:T(8,128)S(1)} %convolution_subtract_fusion.12), custom_call_target="Cholesky" | custom-call | tf_op jit(solution)/shard_map/jit(cholesky)/cholesky | solution.py:74
  923.9 4.2 while.23
  924.7 1.4 bitcast_dynamic-update-slice_fusion.11
  926.7 1.4 bitcast_dynamic-update-slice_fusion.11
  928.1 19.7 %custom-call.33 = f32[2,128,128]{1,2,0:T(8,128)S(1)} custom-call(f32[2,128,128]{2,1,0:T(8,128)S(1)} %get-tuple-element.116), custom_call_target="InvertDiagBlocksLowerTriangular" | custom-call | tf_op jit(solution)/shard_map/triangular_solve/custom-call.0 | solution.py:18
  948.7 1.4 fusion.30
  950.1 1.3 convolution_subtract_fusion.4
  951.9 1.6 gather_fusion.7
  954.8 1.0 convolution_subtract_fusion
  956.0 1.0 copy.45
  (170 shorter events, 39.1 us)
Async XLA Ops:
  6.5 189.2 %reduce-scatter.2.cloned.1.call-start = ((), (), s32[]{:S(2)}) async-start(), calls=%async_computation.2 | async-start | bytes 8912896 | tf_op jit(solution)/shard_map/reduce_scatter | solution.py:56
  18.0 1.6 copy-start.5
  110.0 1.0 copy-start.4
  110.1 146.9 %all-reduce.6.cloned.1.call-start = ((), (), s32[]{:S(2)}) async-start(), calls=%async_computation.3 | async-start | bytes 524288 | tf_op jit(solution)/shard_map/psum | solution.py:14
  197.6 118.3 %all-gather.5.cloned.1.call-start = ((), (), s32[]{:S(2)}) async-start(), calls=%async_computation.4 | async-start | bytes 4456448 | tf_op jit(solution)/shard_map/all_gather | solution.py:73
  257.0 121.3 %copy-start = (f32[256,256]{0,1:T(8,128)S(1)}, f32[256,256]{0,1:T(8,128)}, u32[]{:S(2)}) copy-start(f32[256,256]{0,1:T(8,128)} %all-reduce.6.cloned.1.call-done) | copy-start | bytes 786436
  257.0 189.7 %all-reduce.8.cloned.1.call-start = ((), (), s32[]{:S(2)}) async-start(), calls=%async_computation.5 | async-start | bytes 524288 | tf_op jit(solution)/shard_map/psum | solution.py:14
  387.7 117.8 %all-gather.7.cloned.1.call-start = ((), (), s32[]{:S(2)}) async-start(), calls=%async_computation.6 | async-start | bytes 4456448 | tf_op jit(solution)/shard_map/all_gather | solution.py:73
  446.7 121.6 %copy-start.2 = (f32[256,256]{0,1:T(8,128)S(1)}, f32[256,256]{0,1:T(8,128)}, u32[]{:S(2)}) copy-start(f32[256,256]{0,1:T(8,128)} %all-reduce.8.cloned.1.call-done) | copy-start | bytes 786436
  446.7 189.3 %all-reduce.10.cloned.1.call-start = ((), (), s32[]{:S(2)}) async-start(), calls=%async_computation.7 | async-start | bytes 524288 | tf_op jit(solution)/shard_map/psum | solution.py:14
  577.1 117.9 %all-gather.9.cloned.1.call-start = ((), (), s32[]{:S(2)}) async-start(), calls=%async_computation.8 | async-start | bytes 4456448 | tf_op jit(solution)/shard_map/all_gather | solution.py:73
  636.0 122.0 %copy-start.3 = (f32[256,256]{0,1:T(8,128)S(1)}, f32[256,256]{0,1:T(8,128)}, u32[]{:S(2)}) copy-start(f32[256,256]{0,1:T(8,128)} %all-reduce.10.cloned.1.call-done) | copy-start | bytes 786436
  636.1 190.3 %all-reduce.12.cloned.1.call-start = ((), (), s32[]{:S(2)}) async-start(), calls=%async_computation.9 | async-start | bytes 524288 | tf_op jit(solution)/shard_map/psum | solution.py:14
  767.5 117.9 %all-gather.11.cloned.1.call-start = ((), (), s32[]{:S(2)}) async-start(), calls=%async_computation.10 | async-start | bytes 4456448 | tf_op jit(solution)/shard_map/all_gather | solution.py:73
  826.4 121.4 %copy-start.1 = (f32[256,256]{0,1:T(8,128)S(1)}, f32[256,256]{0,1:T(8,128)}, u32[]{:S(2)}) copy-start(f32[256,256]{0,1:T(8,128)} %all-reduce.12.cloned.1.call-done) | copy-start | bytes 786436
Sparse Core Ops, SparseCore 0:
  110.2 85.5 reduce-scatter.1
  198.1 58.8 all-reduce.5
  259.1 56.7 all-gather.4
  387.8 58.8 all-reduce.7
  448.7 56.7 all-gather.6
  577.2 58.7 all-reduce.9
  638.1 56.7 all-gather.8
  767.6 58.7 all-reduce.11
  828.5 56.7 all-gather.10
where the time goes:
time: 972 us; the launch traced here: 964 us
  waiting for transfers between devices  554 us (57%)
  other arithmetic  228 us (23%)
  local copies, waits for them, and re-layouts  62 us (6%)
  blocking collectives  54.7 us (6%)
  matrix products  42.7 us (4%)
  between operations  20.3 us (2%)
    psum x4, waiting for transfers between devices, spread(): return lax.psum(jnp.where(mine, array, jnp.zeros_like(array)), axis)  236 us
    all_gather x4, waiting for transfers between devices, shards(): full_column = lax.all_gather(column, 'leaf', axis=0, tiled=True)  234 us
    another operation x27, other arithmetic, shards(): factor = jnp.linalg.cholesky(full_column[pivot_start:pivot_start + TILE])  138 us
    reduce_scatter x1, waiting for transfers between devices, shards(): lax.psum_scatter(jnp.einsum('ft,tbc->fbc', picked, column_tiles, precisio...  84.5 us
    another operation x9, other arithmetic, finish_rows(): lax.linalg.triangular_solve(factor, block, left_side=False, lower=True, t...  79.3 us
    all_to_all x1, blocking collectives, shards(): lax.all_to_all(placed, 'panel', split_axis=1, concat_axis=0, tiled=True)  54.7 us
  transfers between devices with their start and end apart: 9, of which 9 were waited for; matrix products, arithmetic and copies ran while one was open for 0% of the time, Pallas kernels for 0%

commit v1 on v0

v1 whole, which is shorter than its diff:
```python
import jax
import jax.numpy as jnp
from jax import lax
from jax.sharding import PartitionSpec as P

TILE = 256
NF = 4096
CB = 2048
STEPS = 4


def shards(child_front, child_panel, parent_front, tile_map, tile_count):
    highest = lax.Precision.HIGHEST
    panel_count = lax.axis_size("panel")
    leaf_count = lax.axis_size("leaf")
    leaf_id = lax.axis_index("leaf")
    panel_id = lax.axis_index("panel")
    tiles_child = CB // TILE
    tiles_front = NF // TILE
    pivot_span = STEPS * TILE
    child_rows = child_front.shape[1]
    height = parent_front.shape[0]
    col_width = parent_front.shape[1]
    slab = pivot_span // panel_count
    slabs_per_block = col_width // slab

    panel_all = child_panel[0]
    own_panel = lax.dynamic_slice_in_dim(panel_all, panel_id * child_rows, child_rows, 0)
    update = child_front[0] - lax.dot_general(
        own_panel, panel_all, (((1,), (1,)), ((), ())), preferred_element_type=jnp.float32
    )
    mapped = tile_map[0]
    live_tiles = jnp.arange(tiles_child, dtype=jnp.int32) < tile_count[0]
    everywhere = jnp.arange(tiles_front, dtype=jnp.int32)
    chosen = ((mapped[None, :] == everywhere[:, None]) & live_tiles[None, :]).astype(jnp.float32)
    placed = jnp.einsum(
        "rtb,ft->rfb", update.reshape(child_rows, tiles_child, TILE), chosen, precision=highest
    ).reshape(child_rows, NF)
    regular = placed.reshape(child_rows, panel_count, col_width).transpose(1, 0, 2)
    pivot_slabs = placed[:, :pivot_span].reshape(child_rows, panel_count, slab).transpose(1, 0, 2)
    parent_slabs = parent_front.reshape(height, slabs_per_block, slab).transpose(1, 0, 2)
    parent_slabs = jnp.tile(parent_slabs, (panel_count // slabs_per_block, 1, 1))
    dest = jnp.arange(panel_count, dtype=jnp.int32)
    parent_slabs = jnp.where(
        (dest // slabs_per_block == panel_id)[:, None, None], parent_slabs, 0.0
    )
    send = jnp.concatenate([regular, pivot_slabs, parent_slabs], axis=2)
    moved = lax.all_to_all(send, "panel", split_axis=0, concat_axis=0, tiled=True)
    child_part = moved[:, :, : col_width + slab]
    parent_slab = jnp.sum(moved[:, :, col_width + slab :], axis=0)
    targets = jnp.arange(leaf_count * height // TILE, dtype=jnp.int32)
    picked = ((mapped[None, :] == targets[:, None]) & live_tiles[None, :]).astype(jnp.float32)
    summed = jnp.einsum("ft,tbc->fbc", picked, child_part, precision=highest)
    own_parent = jnp.concatenate([parent_front, parent_slab], axis=1)
    summed = summed.at[leaf_id].add(own_parent)
    reduced = lax.psum_scatter(
        summed.reshape(leaf_count * height, col_width + slab),
        "leaf",
        scatter_dimension=0,
        tiled=True,
    )
    front_block = reduced[:, :col_width]
    my_slab = reduced[:, col_width:]

    gathered = lax.all_gather(my_slab, ("leaf", "panel"), axis=0, tiled=False)
    gathered = gathered.reshape(leaf_count, panel_count, height, slab)

    def rows_of(tiles):
        count = tiles.shape[0]
        return tiles.transpose(0, 2, 1, 3).reshape(count * height, panel_count * slab)

    top_tiles = pivot_span // height
    pivot_block = rows_of(gathered[:top_tiles])
    own_rows = rows_of(lax.dynamic_slice_in_dim(gathered, leaf_id, 1, 0))
    col_tiles = col_width // height
    col_rows = rows_of(lax.dynamic_slice_in_dim(gathered, panel_id * col_tiles, col_tiles, 0))

    factor = jnp.linalg.cholesky(pivot_block)
    solved = lax.linalg.triangular_solve(
        factor,
        jnp.concatenate([own_rows, col_rows], axis=0),
        left_side=False,
        lower=True,
        transpose_a=True,
    )
    factor_rows = lax.dynamic_slice_in_dim(
        factor, jnp.minimum(leaf_id, top_tiles - 1) * height, height, 0
    )
    row_part = jnp.where(leaf_id < top_tiles, factor_rows, solved[:height])
    col_part = solved[height:]
    rest = front_block - lax.dot_general(
        row_part,
        col_part,
        (((1,), (1,)), ((), ())),
        precision=highest,
        preferred_element_type=jnp.float32,
    )
    pivot_blocks = pivot_span // col_width
    pivot_out = lax.dynamic_slice_in_dim(
        row_part, jnp.minimum(panel_id, pivot_blocks - 1) * col_width, col_width, 1
    )
    upper = jnp.where(leaf_id < top_tiles, 0.0, rest)
    return jnp.where(panel_id < pivot_blocks, pivot_out, upper)


def solution(mesh):
    placed = (
        P("leaf", "panel", None),
        P("leaf", None, None),
        P("leaf", "panel"),
        P("leaf", None),
        P("leaf"),
    )
    return jax.shard_map(
        shards, mesh=mesh, in_specs=placed, out_specs=P("leaf", "panel"), check_vma=False
    )
```

time: 972 us -> 786 us (0.81)
  waiting for transfers between devices: 554 us -> 243 us
  local copies, waits for them, and re-layouts: 62 us -> 126 us
  matrix products: 42.7 us -> 100 us
  blocking collectives: 54.7 us -> 0 us
  other arithmetic: 228 us -> 280 us
    psum x4 -> x0, waiting for transfers between devices: 236 us -> none  [spread(): return lax.psum(jnp.where(mine, array, jnp.zeros_like(array)), axis)]
    all_gather x4 -> x1, waiting for transfers between devices: 234 us -> 82.1 us  [shards(): gathered = lax.all_gather(my_slab, ('leaf', 'panel'), axis=0, tiled=False)]
    all_to_all x0 -> x1, waiting for transfers between devices: none -> 70.3 us  [shards(): lax.all_to_all(send, 'panel', split_axis=0, concat_axis=0, tiled=True)]
    another operation x32 -> x29, matrix products: 18 us -> 73.8 us  [the longest x15 48.1 us: shards(): lax.linalg.triangular_solve(factor, jnp.concatenate([own_rows, col_rows],...]
    all_to_all x1 -> x0, blocking collectives: 54.7 us -> none  [shards(): lax.all_to_all(placed, 'panel', split_axis=1, concat_axis=0, tiled=True)]
    another operation x37 -> x35, other arithmetic: 218 us -> 268 us  [the longest x30 178 us: shards(): factor = jnp.linalg.cholesky(pivot_block)]
    another operation x37 -> x42, local copies, waits for them, and re-layouts: 16.5 us -> 52.7 us  [the longest x29 16.4 us: finish_rows(): lax.linalg.triangular_solve(factor, block, left_side=False, lower=True, t...]
    scatter-add x0 -> x2, local copies, waits for them, and re-layouts: none -> 25.6 us  [shards(): summed = summed.at[leaf_id].add(own_parent)]
  transfers between devices with their start and end apart: 9 -> 3, of which waited for: 9 -> 3; matrix products, arithmetic and copies ran while one was open for 0% -> 0% of each run, Pallas kernels for 0% -> 0%
where the time goes in v1:
time: 786 us; the launch traced here: 775 us
  other arithmetic  280 us (36%)
  waiting for transfers between devices  243 us (31%)
  local copies, waits for them, and re-layouts  126 us (16%)
  matrix products  100 us (13%)
  between operations  19.7 us (3%)
    another operation x30, other arithmetic, shards(): factor = jnp.linalg.cholesky(pivot_block)  178 us
    reduce_scatter x1, waiting for transfers between devices, shards(): lax.psum_scatter(summed.reshape(leaf_count * height, col_width + slab), '...  90.2 us
    another operation x3, other arithmetic, shards(): lax.linalg.triangular_solve(factor, jnp.concatenate([own_rows, col_rows],...  87 us
    all_gather x1, waiting for transfers between devices, shards(): gathered = lax.all_gather(my_slab, ('leaf', 'panel'), axis=0, tiled=False)  82.1 us
    all_to_all x1, waiting for transfers between devices, shards(): lax.all_to_all(send, 'panel', split_axis=0, concat_axis=0, tiled=True)  70.3 us
    another operation x15, matrix products, shards(): lax.linalg.triangular_solve(factor, jnp.concatenate([own_rows, col_rows],...  48.1 us
    another operation x24, local copies, waits for them, and re-layouts  27.4 us
    another operation x14, matrix products, shards(): factor = jnp.linalg.cholesky(pivot_block)  25.7 us
  transfers between devices with their start and end apart: 3, of which 3 were waited for; matrix products, arithmetic and copies ran while one was open for 0% of the time, Pallas kernels for 0%

profile of v1, /device:TPU:1, one launch (start us, length us, event | category | flops | bytes accessed | tf_op | source)
XLA Modules:
  0.0 774.9 jit_solution(14297250270212547966)
XLA Ops:
  7.2 12.8 %fusion.6 = f32[256,2048]{1,0:T(8,128)} fusion(bf16[1,2048,4096]{2,1,0:T(8,128)(2,1)} %param.8, f32[1,256,2048]{2,1,0:T(8,128)} %param.7, s32[]{:T(128)S(6)} %select_n.61), kind=kOutput, calls=%fused_computation.27 | convolution fusion | flops 4295491584 | bytes 23068676 | tf_op jit(solution)/shard_map/dot_general | solution.py:29
  20.1 2.5 copy.72
  22.5 3.6 convolution_bitcast_fusion
  26.2 5.2 copy.68
  31.4 5.3 reshape_reshape.3
  36.9 6.7 copy.79
  45.3 5.5 pad_maximum_fusion
  50.8 6.1 all-to-all-start
  57.8 70.3 %all-to-all-done = f32[8,256,768]{2,1,0:T(8,128)} async-done(((f32[8,256,768]{2,1,0:T(8,128)}), f32[8,256,768]{2,1,0:T(8,128)}, u32[]{:S(2)}, u32[]{:S(2)}) %all-to-all-start) | async-done | bytes 6291488 | tf_op jit(solution)/shard_map/all_to_all | solution.py:48
  129.5 2.9 slice.291
  132.4 7.0 fusion.2
  139.4 3.8 copy-done
  144.8 14.2 %scatter-add.4 = f32[16,256,640]{2,0,1:T(8,128)} dynamic-update-slice(f32[16,256,640]{2,0,1:T(8,128)} %copy-done, f32[1,256,640]{2,0,1:T(1,128)S(1)} %broadcast_select_fusion, s32[]{:T(128)} %select_n.64, s32[]{:T(128)} %copy.126, s32[]{:T(128)} %copy.126) | dynamic-update-slice | bytes 1310724 | tf_op jit(solution)/shard_map/scatter-add | solution.py:55
  159.0 11.3 %copy.53 = f32[16,256,640]{2,1,0:T(8,128)} copy(f32[16,256,640]{2,0,1:T(8,128)} %scatter-add.4) | data formatting | bytes 20971520 | tf_op jit(solution)/shard_map/scatter-add | solution.py:55
  170.4 90.2 %reduce-scatter.2.cloned.1.call-done = f32[256,640]{1,0:T(8,128)} async-done(((f32[4096,640]{1,0:T(8,128)}), f32[256,640]{1,0:T(8,128)}) %reduce-scatter.2.cloned.1.call-update) | async-done | bytes 655376 | tf_op jit(solution)/shard_map/reduce_scatter | solution.py:56
  262.2 82.1 %all-gather.3.cloned.1.call-done = f32[32768,128]{1,0:T(8,128)} async-done(((f32[256,128]{1,0:T(8,128)}), f32[32768,128]{1,0:T(8,128)}) %all-gather.3.cloned.1.call-update) | async-done | bytes 16777232 | tf_op jit(solution)/shard_map/all_gather | solution.py:65
  349.8 4.4 slice.294
  354.2 5.2 copy.54
  359.5 5.2 copy.73
  364.6 5.5 copy.55
  370.1 4.4 fusion.4
  376.5 11.7 %cholesky.223 = f32[128,128]{1,0:T(8,128)S(1)} custom-call(f32[128,128]{1,0:T(8,128)S(1)} %cholesky.580), custom_call_target="Cholesky" | custom-call | tf_op jit(solution)/shard_map/jit(cholesky)/cholesky | solution.py:78
  388.3 9.8 %custom-call.62 = f32[1,128,128]{1,2,0:T(8,128)S(1)} custom-call(f32[1,128,128]{2,1,0:T(8,128)S(1)} %get-tuple-element.75), custom_call_target="InvertDiagBlocksLowerTriangular" | custom-call | tf_op jit(solution)/shard_map/jit(cholesky)/cholesky | solution.py:78
  398.1 2.5 cholesky.255
  400.6 2.3 constant_dynamic-update-slice_fusion.25
  405.2 11.9 %cholesky.244 = f32[128,128]{1,0:T(8,128)S(1)} custom-call(f32[128,128]{1,0:T(8,128)S(1)} %cholesky.584), custom_call_target="Cholesky" | custom-call | tf_op jit(solution)/shard_map/jit(cholesky)/cholesky | solution.py:78
  417.8 9.8 %custom-call.63 = f32[1,128,128]{1,2,0:T(8,128)S(1)} custom-call(f32[1,128,128]{2,1,0:T(8,128)S(1)} %get-tuple-element.72), custom_call_target="InvertDiagBlocksLowerTriangular" | custom-call | tf_op jit(solution)/shard_map/jit(cholesky)/cholesky | solution.py:78
  432.6 13.2 %cholesky.468 = f32[128,128]{1,0:T(8,128)} custom-call(f32[128,128]{1,0:T(8,128)} %cholesky.589), custom_call_target="Cholesky" | custom-call | tf_op jit(solution)/shard_map/jit(cholesky)/cholesky | solution.py:78
  447.9 11.3 %custom-call.64 = f32[1,128,128]{1,2,0:T(8,128)} custom-call(f32[1,128,128]{2,1,0:T(8,128)} %get-tuple-element.69), custom_call_target="InvertDiagBlocksLowerTriangular" | custom-call | tf_op jit(solution)/shard_map/jit(cholesky)/cholesky | solution.py:78
  461.2 2.3 convolution_subtract_fusion.8
  463.6 12.7 %cholesky.487 = f32[128,128]{1,0:T(8,128)} custom-call(f32[128,128]{1,0:T(8,128)S(1)} %cholesky.594), custom_call_target="Cholesky" | custom-call | tf_op jit(solution)/shard_map/jit(cholesky)/cholesky | solution.py:78
  478.4 10.4 %custom-call.65 = f32[1,128,128]{1,2,0:T(8,128)} custom-call(f32[1,128,128]{2,1,0:T(8,128)S(1)} %get-tuple-element.66), custom_call_target="InvertDiagBlocksLowerTriangular" | custom-call | tf_op jit(solution)/shard_map/jit(cholesky)/cholesky | solution.py:78
  490.8 2.3 convolution_subtract_fusion.9
  493.1 11.7 %cholesky.506 = f32[128,128]{1,0:T(8,128)S(1)} custom-call(f32[128,128]{1,0:T(8,128)S(1)} %cholesky.599), custom_call_target="Cholesky" | custom-call | tf_op jit(solution)/shard_map/jit(cholesky)/cholesky | solution.py:78
  506.2 10.0 %custom-call.66 = f32[1,128,128]{1,2,0:T(8,128)S(1)} custom-call(f32[1,128,128]{2,1,0:T(8,128)S(1)} %get-tuple-element.63), custom_call_target="InvertDiagBlocksLowerTriangular" | custom-call | tf_op jit(solution)/shard_map/jit(cholesky)/cholesky | solution.py:78
  519.5 11.7 %cholesky.526 = f32[128,128]{1,0:T(8,128)S(1)} custom-call(f32[128,128]{1,0:T(8,128)S(1)} %cholesky.604), custom_call_target="Cholesky" | custom-call | tf_op jit(solution)/shard_map/jit(cholesky)/cholesky | solution.py:78
  532.5 9.8 %custom-call.67 = f32[1,128,128]{1,2,0:T(8,128)S(1)} custom-call(f32[1,128,128]{2,1,0:T(8,128)S(1)} %get-tuple-element.60), custom_call_target="InvertDiagBlocksLowerTriangular" | custom-call | tf_op jit(solution)/shard_map/jit(cholesky)/cholesky | solution.py:78
  545.4 11.9 %cholesky.546 = f32[128,128]{1,0:T(8,128)S(1)} custom-call(f32[128,128]{1,0:T(8,128)S(1)} %cholesky.609), custom_call_target="Cholesky" | custom-call | tf_op jit(solution)/shard_map/jit(cholesky)/cholesky | solution.py:78
  558.5 9.8 %custom-call.68 = f32[1,128,128]{1,2,0:T(8,128)S(1)} custom-call(f32[1,128,128]{2,1,0:T(8,128)S(1)} %get-tuple-element.57), custom_call_target="InvertDiagBlocksLowerTriangular" | custom-call | tf_op jit(solution)/shard_map/jit(cholesky)/cholesky | solution.py:78
  571.0 11.7 %cholesky.564 = f32[128,128]{1,0:T(8,128)S(1)} custom-call(f32[128,128]{1,0:T(8,128)S(1)} %convolution_subtract_fusion.12), custom_call_target="Cholesky" | custom-call | tf_op jit(solution)/shard_map/jit(cholesky)/cholesky | solution.py:78
  589.6 6.6 fusion.5
  596.2 27.4 %while.2 = (s32[]{:T(128)}, f32[1024,1024]{1,0:T(8,128)}, s32[8,2]{0,1:T(2,128)S(1)}, f32[8,128,128]{2,1,0:T(8,128)}, s32[]{:T(128)}) while((s32[]{:T(128)}, f32[1024,1024]{1,0:T(8,128)}, s32[8,2]{0,1:T(2,128)S(1)}, f32[8,128,128]{2,1,0:T(8,128)}, s32[]{:T(128)}) %tuple.58), condition=%wide.while_cond.1, body=%wide.while_body.1.sunk | while | flops 2 | bytes 132205 | solution.py:79
  596.8 2.8 bitcast_dynamic-update-slice_fusion.2
  600.2 2.8 bitcast_dynamic-update-slice_fusion.2
  603.7 2.8 bitcast_dynamic-update-slice_fusion.2
  607.1 2.8 bitcast_dynamic-update-slice_fusion.2
  610.5 2.8 bitcast_dynamic-update-slice_fusion.2
  614.0 2.8 bitcast_dynamic-update-slice_fusion.2
  617.4 2.8 bitcast_dynamic-update-slice_fusion.2
  620.8 2.8 bitcast_dynamic-update-slice_fusion.2
  623.6 80.4 %custom-call.69 = f32[8,128,128]{1,2,0:T(8,128)} custom-call(f32[8,128,128]{2,1,0:T(8,128)} %get-tuple-element.24), custom_call_target="InvertDiagBlocksLowerTriangular" | custom-call | tf_op jit(solution)/shard_map/triangular_solve | solution.py:79
  704.0 2.4 constant_dynamic-update-slice_fusion.17
  708.9 2.5 constant_dynamic-update-slice_fusion.16
  713.4 2.4 convolution_subtract_fusion.6
  715.8 2.6 constant_dynamic-update-slice_fusion.15
  720.3 3.3 convolution_subtract_fusion.3
  723.6 2.4 constant_dynamic-update-slice_fusion.14
  726.8 4.3 fusion.30
  733.1 2.7 constant_dynamic-update-slice_fusion.13
  735.8 5.0 convolution_subtract_fusion.2
  740.8 2.4 constant_dynamic-update-slice_fusion.12
  743.3 5.5 convolution_subtract_fusion.5
  751.1 7.2 convolution_subtract_fusion.1
  765.1 2.8 fusion.27
  (121 shorter events, 68.6 us)
Async XLA Ops:
  20.1 2.5 copy-start.13
  31.4 5.3 copy-start.5
  50.8 6.4 copy-start.14
  50.8 77.4 %all-to-all-start = ((f32[8,256,768]{2,1,0:T(8,128)}), f32[8,256,768]{2,1,0:T(8,128)}, u32[]{:S(2)}, u32[]{:S(2)}) async-start(f32[8,256,768]{2,1,0:T(8,128)} %pad_maximum_fusion), calls=%async_computation | async-start | bytes 12582912 | tf_op jit(solution)/shard_map/all_to_all | solution.py:48
  56.9 203.7 %reduce-scatter.2.cloned.1.call-start = ((), (), s32[]{:S(2)}) async-start(), calls=%async_computation.2 | async-start | bytes 11141120 | tf_op jit(solution)/shard_map/reduce_scatter | solution.py:56
  139.4 3.8 copy-start
  170.4 174.0 %all-gather.3.cloned.1.call-start = ((), (), s32[]{:S(2)}) async-start(), calls=%async_computation.3 | async-start | bytes 16908288 | tf_op jit(solution)/shard_map/all_gather | solution.py:65
  374.6 1.9 copy-start.1
  404.5 0.8 copy-start.6
  720.3 6.5 copy-start.2
  720.3 6.5 copy-start.3
  726.1 0.8 copy-start.4
  751.1 10.8 %copy-start.7 = (f32[768,128]{1,0:T(8,128)S(1)}, f32[768,128]{1,0:T(8,128)}, u32[]{:S(2)}) copy-start(f32[768,128]{1,0:T(8,128)} %copy.59) | copy-start | bytes 1179652
  758.2 3.7 copy-start.8
  758.2 3.8 copy-start.9
  758.2 3.8 copy-start.10
  760.6 1.6 copy-start.11
  762.1 2.9 copy-start.12
Sparse Core Ops, SparseCore 0:
  170.5 90.0 reduce-scatter.1
  263.8 80.5 all-gather.2

commit v2 on v1

--- a/solution.py
+++ b/solution.py
@@ -53,36 +53,72 @@
     summed = jnp.einsum("ft,tbc->fbc", picked, child_part, precision=highest)
     own_parent = jnp.concatenate([parent_front, parent_slab], axis=1)
     summed = summed.at[leaf_id].add(own_parent)
-    reduced = lax.psum_scatter(
-        summed.reshape(leaf_count * height, col_width + slab),
-        "leaf",
-        scatter_dimension=0,
-        tiled=True,
-    )
+    summed = summed.reshape(leaf_count * height, col_width + slab)
+    top_share = pivot_span // leaf_count
+    slab_rows = summed[:, col_width:]
+    slab_rows = jnp.concatenate(
+        [
+            slab_rows[:pivot_span].reshape(leaf_count, top_share, slab),
+            slab_rows[pivot_span:].reshape(leaf_count, height - top_share, slab),
+        ],
+        axis=1,
+    ).reshape(leaf_count * height, slab)
+    summed = jnp.concatenate([summed[:, :col_width], slab_rows], axis=1)
+    reduced = lax.psum_scatter(summed, "leaf", scatter_dimension=0, tiled=True)
     front_block = reduced[:, :col_width]
     my_slab = reduced[:, col_width:]
 
-    gathered = lax.all_gather(my_slab, ("leaf", "panel"), axis=0, tiled=False)
-    gathered = gathered.reshape(leaf_count, panel_count, height, slab)
+    def assemble(piece):
+        rows = piece.shape[0]
+        got = lax.all_gather(piece, ("leaf", "panel"), axis=0, tiled=False)
+        got = got.reshape(leaf_count, panel_count, rows, slab).transpose(0, 2, 1, 3)
+        return got.reshape(leaf_count * rows, panel_count * slab)
 
-    def rows_of(tiles):
-        count = tiles.shape[0]
-        return tiles.transpose(0, 2, 1, 3).reshape(count * height, panel_count * slab)
+    pivot_block = assemble(my_slab[:top_share])
+    lower_block = assemble(my_slab[top_share:])
+
+    blocks = pivot_span // TILE
+    eye = jnp.eye(TILE, dtype=jnp.float32)
+    work = pivot_block
+    factor_cols = []
+    inverses = []
+    for k in range(blocks):
+        lo, hi = k * TILE, (k + 1) * TILE
+        diag = lax.linalg.cholesky(work[lo:hi, lo:hi], symmetrize_input=True)
+        diag = jnp.tril(diag)
+        inverse = lax.linalg.triangular_solve(diag, eye, left_side=True, lower=True)
+        inverses.append(inverse)
+        if k + 1 < blocks:
+            below = jnp.dot(work[hi:, lo:hi], inverse.T, precision=highest)
+            work = work.at[hi:, hi:].add(-jnp.dot(below, below.T, precision=highest))
+            column = jnp.concatenate([jnp.zeros((lo, TILE), jnp.float32), diag, below], axis=0)
+        else:
+            column = jnp.concatenate([jnp.zeros((lo, TILE), jnp.float32), diag], axis=0)
+        factor_cols.append(column)
+    factor = jnp.concatenate(factor_cols, axis=1)
 
     top_tiles = pivot_span // height
-    pivot_block = rows_of(gathered[:top_tiles])
-    own_rows = rows_of(lax.dynamic_slice_in_dim(gathered, leaf_id, 1, 0))
-    col_tiles = col_width // height
-    col_rows = rows_of(lax.dynamic_slice_in_dim(gathered, panel_id * col_tiles, col_tiles, 0))
+    own_rows = lax.dynamic_slice_in_dim(
+        lower_block, jnp.maximum(leaf_id - top_tiles, 0) * height, height, 0
+    )
+    col_rows = lax.dynamic_slice_in_dim(
+        lower_block,
+        jnp.maximum(panel_id - pivot_span // col_width, 0) * col_width,
+        col_width,
+        0,
+    )
+    extra = jnp.concatenate([own_rows, col_rows], axis=0)
+    solved = []
+    for k in range(blocks):
+        lo, hi = k * TILE, (k + 1) * TILE
+        part = extra[:, lo:hi]
+        if k:
+            part = part - jnp.dot(
+                jnp.concatenate(solved, axis=1), factor[lo:hi, :lo].T, precision=highest
+            )
+        solved.append(jnp.dot(part, inverses[k].T, precision=highest))
+    solved = jnp.concatenate(solved, axis=1)
 
-    factor = jnp.linalg.cholesky(pivot_block)
-    solved = lax.linalg.triangular_solve(
-        factor,
-        jnp.concatenate([own_rows, col_rows], axis=0),
-        left_side=False,
-        lower=True,
-        transpose_a=True,
-    )
     factor_rows = lax.dynamic_slice_in_dim(
         factor, jnp.minimum(leaf_id, top_tiles - 1) * height, height, 0
     )

time: 786 us -> 694 us (0.88)
  matrix products: 100 us -> 61.1 us
  other arithmetic: 280 us -> 242 us
  waiting for transfers between devices: 243 us -> 228 us
    another operation x29 -> x20, matrix products: 73.8 us -> 6.23 us  [the longest x12 4.15 us: shards(): inverse = lax.linalg.triangular_solve(diag, eye, left_side=True, lower=True)]
    another operation x35 -> x38, other arithmetic: 268 us -> 223 us  [the longest x27 139 us: shards(): diag = lax.linalg.cholesky(work[lo:hi, lo:hi], symmetrize_input=True)]
    dot_general x0 -> x13, matrix products: none -> 30.1 us  [the longest x3 12.5 us: shards(): jnp.dot(jnp.concatenate(solved, axis=1), factor[lo:hi, :lo].T, precision=...]
    another operation x40 -> x43, local copies, waits for them, and re-layouts: 40.8 us -> 16.1 us  [the longest x29 15.5 us: shards(): inverse = lax.linalg.triangular_solve(diag, eye, left_side=True, lower=True)]
    reshape x2, local copies, waits for them, and re-layouts: 5.83 us -> 24.3 us  [assemble(): got = got.reshape(leaf_count, panel_count, rows, slab).transpose(0, 2, 1, 3)]
    all_gather x1 -> x2, waiting for transfers between devices: 82.1 us -> 67.2 us  [assemble(): got = lax.all_gather(piece, ('leaf', 'panel'), axis=0, tiled=False)]
    concatenate x0 -> x2, other arithmetic: none -> 8.44 us  [the longest x1 8.26 us: shards(): summed = jnp.concatenate([summed[:, :col_width], slab_rows], axis=1)]
    unnamed x42 -> x73, local copies, waits for them, and re-layouts: 17.3 us -> 24 us
  transfers between devices with their start and end apart: 3 -> 4, of which waited for: 3 -> 3; matrix products, arithmetic and copies ran while one was open for 0% -> 39% of each run, Pallas kernels for 0% -> 0%
where the time goes in v2:
time: 694 us; the launch traced here: 684 us
  other arithmetic  242 us (35%)
  waiting for transfers between devices  228 us (33%)
  local copies, waits for them, and re-layouts  126 us (18%)
  matrix products  61.1 us (9%)
  between operations  20.6 us (3%)
    another operation x27, other arithmetic, shards(): diag = lax.linalg.cholesky(work[lo:hi, lo:hi], symmetrize_input=True)  139 us
    reduce_scatter x1, waiting for transfers between devices, shards(): reduced = lax.psum_scatter(summed, 'leaf', scatter_dimension=0, tiled=True)  90.2 us
    another operation x9, other arithmetic, shards(): inverse = lax.linalg.triangular_solve(diag, eye, left_side=True, lower=True)  82.1 us
    all_to_all x1, waiting for transfers between devices, shards(): lax.all_to_all(send, 'panel', split_axis=0, concat_axis=0, tiled=True)  70.3 us
    all_gather x2, waiting for transfers between devices, assemble(): got = lax.all_gather(piece, ('leaf', 'panel'), axis=0, tiled=False)  67.2 us
    reshape x2, local copies, waits for them, and re-layouts, assemble(): got = got.reshape(leaf_count, panel_count, rows, slab).transpose(0, 2, 1, 3)  24.3 us
    unnamed x73, local copies, waits for them, and re-layouts  24 us
    scatter-add x2, local copies, waits for them, and re-layouts, shards(): summed = summed.at[leaf_id].add(own_parent)  21.6 us
  transfers between devices with their start and end apart: 4, of which 3 were waited for; matrix products, arithmetic and copies ran while one was open for 39% of the time, Pallas kernels for 0%

profile of v2, /device:TPU:1, one launch (start us, length us, event | category | flops | bytes accessed | tf_op | source)
XLA Modules:
  0.0 684.4 jit_solution(8020882153570738754)
XLA Ops:
  6.5 11.5 %fusion.4 = f32[256,2048]{1,0:T(8,128)S(1)} fusion(bf16[1,2048,4096]{2,1,0:T(8,128)(2,1)} %param.17, f32[1,256,2048]{2,1,0:T(8,128)} %param.16, s32[]{:T(128)S(6)} %select_n.84), kind=kOutput, calls=%fused_computation.32 | convolution fusion | flops 4295491584 | bytes 23068676 | tf_op jit(solution)/shard_map/dot_general | solution.py:29
  19.6 3.6 convolution_bitcast_fusion
  23.2 5.2 reshape_reshape.3
  28.4 5.3 copy.108
  33.7 6.6 copy.122
  40.2 1.4 slice.310
  42.3 5.5 pad_maximum_fusion.1
  47.8 6.1 all-to-all-start
  54.9 70.3 %all-to-all-done = f32[8,256,768]{2,1,0:T(8,128)} async-done(((f32[8,256,768]{2,1,0:T(8,128)}), f32[8,256,768]{2,1,0:T(8,128)}, u32[]{:S(2)}, u32[]{:S(2)}) %all-to-all-start) | async-done | bytes 6291488 | tf_op jit(solution)/shard_map/all_to_all | solution.py:48
  125.2 2.9 slice.311
  128.1 7.0 %fusion.2 = f32[16,256,640]{2,0,1:T(8,128)S(1)} fusion(f32[8,256,640]{2,1,0:T(8,128)S(1)} %slice.311, s32[8]{0:T(128)S(1)} %bitcast.213, pred[8]{0:T(512)(128)(4,1)S(1)} %iota_compare_fusion.6), kind=kOutput, calls=%fused_computation.13 | convolution fusion | flops 251658496 | bytes 15728680 | tf_op jit(solution)/shard_map/ft,tbc->fbc/dot_general | solution.py:53
  135.1 2.1 slice_reduce_fusion
  137.3 1.8 copy-done
  140.4 14.3 %scatter-add.4 = f32[16,256,640]{2,0,1:T(8,128)} dynamic-update-slice(f32[16,256,640]{2,0,1:T(8,128)} %copy-done, f32[1,256,640]{2,0,1:T(1,128)S(1)} %broadcast_select_fusion, s32[]{:T(128)} %select_n.87, s32[]{:T(128)} %copy.165, s32[]{:T(128)} %copy.165) | dynamic-update-slice | bytes 1310724 | tf_op jit(solution)/shard_map/scatter-add | solution.py:55
  154.7 7.3 %copy.81 = f32[16,256,640]{2,1,0:T(8,128)S(1)} copy(f32[16,256,640]{2,0,1:T(8,128)} %scatter-add.4) | data formatting | bytes 20971520 | tf_op jit(solution)/shard_map/scatter-add | solution.py:55
  162.2 4.5 slice.313
  166.9 8.3 %pad_maximum_fusion = f32[4096,640]{1,0:T(8,128)} fusion(f32[4096,128]{1,0:T(8,128)S(1)} %bitcast.203, f32[4096,512]{1,0:T(8,128)} %slice.313), kind=kLoop, calls=%fused_computation.11 | loop fusion | flops 2621440 | bytes 20971520 | tf_op jit(solution)/shard_map/concatenate | solution.py:66
  175.3 90.2 %reduce-scatter.2.cloned.1.call-done = f32[256,640]{1,0:T(8,128)} async-done(((f32[4096,640]{1,0:T(8,128)}), f32[256,640]{1,0:T(8,128)}) %reduce-scatter.2.cloned.1.call-update) | async-done | bytes 655376 | tf_op jit(solution)/shard_map/reduce_scatter | solution.py:67
  265.5 1.4 slice.316
  266.9 1.5 slice.349
  268.5 67.2 %all-gather.5.cloned.1.call-done = f32[8192,128]{1,0:T(8,128)} async-done(((f32[64,128]{1,0:T(8,128)}), f32[8192,128]{1,0:T(8,128)}) %all-gather.5.cloned.1.call-update) | async-done | bytes 4194320 | tf_op jit(solution)/shard_map/all_gather | solution.py:73
  335.7 5.5 copy.82
  342.4 1.7 copy-done.3
  344.1 2.1 copy.111
  347.4 11.7 %custom-call.25 = f32[128,128]{1,0:T(8,128)S(1)} custom-call(f32[128,128]{1,0:T(8,128)S(1)} %slice.318), custom_call_target="Cholesky" | custom-call | tf_op jit(solution)/shard_map/cholesky/custom-call.2 | solution.py:87
  359.2 9.8 %custom-call.26 = f32[1,128,128]{1,2,0:T(8,128)S(1)} custom-call(f32[1,128,128]{2,1,0:T(8,128)S(1)} %get-tuple-element.148), custom_call_target="InvertDiagBlocksLowerTriangular" | custom-call | tf_op jit(solution)/shard_map/cholesky/custom-call.4 | solution.py:87
  369.5 11.7 %custom-call.27 = f32[128,128]{1,0:T(8,128)S(1)} custom-call(f32[128,128]{1,0:T(8,128)S(1)} %convolution_subtract_fusion.8), custom_call_target="Cholesky" | custom-call | tf_op jit(solution)/shard_map/cholesky/custom-call.3 | solution.py:87
  384.0 4.1 while.12
  384.6 1.4 bitcast_dynamic-update-slice_fusion.12
  386.7 1.4 bitcast_dynamic-update-slice_fusion.12
  388.1 20.1 %custom-call.28 = f32[2,128,128]{1,2,0:T(8,128)S(1)} custom-call(f32[2,128,128]{2,1,0:T(8,128)S(1)} %get-tuple-element.81), custom_call_target="InvertDiagBlocksLowerTriangular" | custom-call | tf_op jit(solution)/shard_map/triangular_solve/custom-call.0 | solution.py:89
  409.1 2.0 fusion.54
  411.1 4.0 negate_add_fusion
  415.1 1.4 copy-done.4
  417.7 11.7 %custom-call.29 = f32[128,128]{1,0:T(8,128)S(1)} custom-call(f32[128,128]{1,0:T(8,128)S(1)} %copy.89), custom_call_target="Cholesky" | custom-call | tf_op jit(solution)/shard_map/cholesky/custom-call.2 | solution.py:87
  429.5 9.8 %custom-call.30 = f32[1,128,128]{1,2,0:T(8,128)S(1)} custom-call(f32[1,128,128]{2,1,0:T(8,128)S(1)} %get-tuple-element.144), custom_call_target="InvertDiagBlocksLowerTriangular" | custom-call | tf_op jit(solution)/shard_map/cholesky/custom-call.4 | solution.py:87
  440.0 11.9 %custom-call.31 = f32[128,128]{1,0:T(8,128)S(1)} custom-call(f32[128,128]{1,0:T(8,128)S(1)} %copy.91), custom_call_target="Cholesky" | custom-call | tf_op jit(solution)/shard_map/cholesky/custom-call.3 | solution.py:87
  455.3 4.1 while.13
  455.9 1.3 bitcast_dynamic-update-slice_fusion.13
  459.3 19.7 %custom-call.32 = f32[2,128,128]{1,2,0:T(8,128)S(1)} custom-call(f32[2,128,128]{2,1,0:T(8,128)S(1)} %get-tuple-element.82), custom_call_target="InvertDiagBlocksLowerTriangular" | custom-call | tf_op jit(solution)/shard_map/triangular_solve/custom-call.0 | solution.py:89
  480.6 2.0 fusion.60
  482.7 2.3 fusion.21
  485.2 11.7 %custom-call.33 = f32[128,128]{1,0:T(8,128)S(1)} custom-call(f32[128,128]{1,0:T(8,128)S(1)} %slice.338), custom_call_target="Cholesky" | custom-call | tf_op jit(solution)/shard_map/cholesky/custom-call.2 | solution.py:87
  497.0 9.8 %custom-call.34 = f32[1,128,128]{1,2,0:T(8,128)S(1)} custom-call(f32[1,128,128]{2,1,0:T(8,128)S(1)} %get-tuple-element.140), custom_call_target="InvertDiagBlocksLowerTriangular" | custom-call | tf_op jit(solution)/shard_map/cholesky/custom-call.4 | solution.py:87
  507.3 12.1 %custom-call.35 = f32[128,128]{1,0:T(8,128)S(1)} custom-call(f32[128,128]{1,0:T(8,128)S(1)} %convolution_subtract_fusion.6), custom_call_target="Cholesky" | custom-call | tf_op jit(solution)/shard_map/cholesky/custom-call.3 | solution.py:87
  522.9 3.9 while.14
  526.8 19.7 %custom-call.36 = f32[2,128,128]{1,2,0:T(8,128)S(1)} custom-call(f32[2,128,128]{2,1,0:T(8,128)S(1)} %get-tuple-element.83), custom_call_target="InvertDiagBlocksLowerTriangular" | custom-call | tf_op jit(solution)/shard_map/triangular_solve/custom-call.0 | solution.py:89
  549.5 11.7 %custom-call.37 = f32[128,128]{1,0:T(8,128)S(1)} custom-call(f32[128,128]{1,0:T(8,128)S(1)} %slice.346), custom_call_target="Cholesky" | custom-call | tf_op jit(solution)/shard_map/cholesky/custom-call.2 | solution.py:87
  561.2 9.8 %custom-call.38 = f32[1,128,128]{1,2,0:T(8,128)S(1)} custom-call(f32[1,128,128]{2,1,0:T(8,128)S(1)} %get-tuple-element.136), custom_call_target="InvertDiagBlocksLowerTriangular" | custom-call | tf_op jit(solution)/shard_map/cholesky/custom-call.4 | solution.py:87
  571.7 11.7 %custom-call.39 = f32[128,128]{1,0:T(8,128)S(1)} custom-call(f32[128,128]{1,0:T(8,128)S(1)} %convolution_subtract_fusion.5), custom_call_target="Cholesky" | custom-call | tf_op jit(solution)/shard_map/cholesky/custom-call.3 | solution.py:87
  587.1 3.6 while.15
  590.7 19.7 %custom-call.40 = f32[2,128,128]{1,2,0:T(8,128)S(1)} custom-call(f32[2,128,128]{2,1,0:T(8,128)S(1)} %get-tuple-element.84), custom_call_target="InvertDiagBlocksLowerTriangular" | custom-call | tf_op jit(solution)/shard_map/triangular_solve/custom-call.0 | solution.py:89
  611.9 18.8 %copy.98 = f32[16,8,192,128]{3,1,2,0:T(8,128)} copy(f32[16,8,192,128]{3,2,1,0:T(8,128)} %bitcast.202) | data formatting | bytes 25165824 | tf_op jit(solution)/shard_map/reshape | solution.py:74
  630.8 12.5 %copy.120 = f32[384,8,8,128]{3,1,2,0:T(8,128)} copy(f32[384,8,8,128]{3,2,1,0:T(8,128)} %bitcast.190) | data formatting | bytes 25165824
  643.2 1.8 constant_dynamic-slice_fusion.4
  648.2 2.3 convolution_subtract_fusion
  650.5 2.3 copy.99
  652.9 2.9 fusion.78
  655.7 2.3 copy.100
  658.1 4.2 fusion.25
  662.3 1.8 fusion.77
  664.1 2.3 copy.101
  666.5 6.0 fusion.22
  674.7 2.7 fusion.30
  (187 shorter events, 42.2 us)
Async XLA Ops:
  18.0 1.6 copy-start.32
  40.2 1.7 copy-start.21
  47.8 6.4 copy-start.33
  47.8 77.4 %all-to-all-start = ((f32[8,256,768]{2,1,0:T(8,128)}), f32[8,256,768]{2,1,0:T(8,128)}, u32[]{:S(2)}, u32[]{:S(2)}) async-start(f32[8,256,768]{2,1,0:T(8,128)} %pad_maximum_fusion.1), calls=%async_computation | async-start | bytes 12582912 | tf_op jit(solution)/shard_map/all_to_all | solution.py:48
  53.9 211.6 %reduce-scatter.2.cloned.1.call-start = ((), (), s32[]{:S(2)}) async-start(), calls=%async_computation.2 | async-start | bytes 11141120 | tf_op jit(solution)/shard_map/reduce_scatter | solution.py:67
  135.1 4.0 copy-start
  175.2 160.5 %all-gather.5.cloned.1.call-start = ((), (), s32[]{:S(2)}) async-start(), calls=%async_computation.3 | async-start | bytes 4227072 | tf_op jit(solution)/shard_map/all_gather | solution.py:73
  266.9 345.1 %all-gather.7.cloned.1.call-start = ((), (), s32[]{:S(2)}) async-start(), calls=%async_computation.4 | async-start | bytes 12681216 | tf_op jit(solution)/shard_map/all_gather | solution.py:73
  268.5 210.8 %copy-start.8 = (f32[256,256]{1,0:T(8,128)}, f32[256,256]{1,0:T(8,128)S(1)}, u32[]{:S(2)}) copy-start(f32[256,256]{1,0:T(8,128)S(1)} %fusion.76) | copy-start | bytes 786436
  342.2 1.9 copy-start.3
  409.1 6.0 copy-start.22
  415.1 1.4 copy-start.4
  479.3 0.7 copy-start.17
  480.0 0.7 copy-start.24
  485.0 61.5 %copy-start.9 = (f32[256,256]{1,0:T(8,128)S(1)}, f32[256,256]{1,0:T(8,128)}, u32[]{:S(2)}) copy-start(f32[256,256]{1,0:T(8,128)} %copy-done.8) | copy-start | bytes 786436
  546.8 0.7 copy-start.19
  547.4 0.7 copy-start.27
  548.7 38.4 %copy-start.10 = (f32[256,256]{1,0:T(8,128)}, f32[256,256]{1,0:T(8,128)S(1)}, u32[]{:S(2)}) copy-start(f32[256,256]{1,0:T(8,128)S(1)} %fusion.63) | copy-start | bytes 786436
  610.7 20.1 %copy-start.25 = (f32[128,256]{1,0:T(8,128)}, f32[128,256]{1,0:T(8,128)S(1)}, u32[]{:S(2)}) copy-start(f32[128,256]{1,0:T(8,128)S(1)} %fusion.79) | copy-start | bytes 393220
  643.2 3.1 copy-start.23
  646.4 1.0 copy-start.1
  647.3 0.9 copy-start.2
  648.2 4.6 copy-start.18
  658.1 4.2 copy-start.12
  658.1 4.2 copy-start.20
  658.1 4.2 copy-start.28
  666.4 6.1 copy-start.26
  666.4 6.1 copy-start.31
  666.5 6.9 %copy-start.5 = (f32[768,256]{1,0:T(8,128)S(1)}, f32[768,256]{1,0:T(8,128)}, u32[]{:S(2)}) copy-start(f32[768,256]{1,0:T(8,128)} %copy.99) | copy-start | bytes 2359300
  666.5 6.9 %copy-start.6 = (f32[768,256]{1,0:T(8,128)S(1)}, f32[768,256]{1,0:T(8,128)}, u32[]{:S(2)}) copy-start(f32[768,256]{1,0:T(8,128)} %copy.100) | copy-start | bytes 2359300
  666.5 6.9 %copy-start.7 = (f32[768,256]{1,0:T(8,128)S(1)}, f32[768,256]{1,0:T(8,128)}, u32[]{:S(2)}) copy-start(f32[768,256]{1,0:T(8,128)} %copy.101) | copy-start | bytes 2359300
  666.5 6.9 %copy-start.11 = (f32[256,256]{1,0:T(8,128)S(1)}, f32[256,256]{1,0:T(8,128)}, u32[]{:S(2)}) copy-start(f32[256,256]{1,0:T(8,128)} %copy-done.10) | copy-start | bytes 786436
  666.5 6.9 %copy-start.13 = (f32[256,256]{1,0:T(8,128)S(1)}, f32[256,256]{1,0:T(8,128)}, u32[]{:S(2)}) copy-start(f32[256,256]{1,0:T(8,128)} %copy-done.12) | copy-start | bytes 786436
  666.5 6.9 %copy-start.14 = (f32[256,256]{1,0:T(8,128)S(1)}, f32[256,256]{1,0:T(8,128)}, u32[]{:S(2)}) copy-start(f32[256,256]{1,0:T(8,128)} %get-tuple-element.124) | copy-start | bytes 786436
  666.5 6.9 %copy-start.15 = (f32[256,256]{1,0:T(8,128)S(1)}, f32[256,256]{1,0:T(8,128)}, u32[]{:S(2)}) copy-start(f32[256,256]{1,0:T(8,128)} %get-tuple-element.122) | copy-start | bytes 786436
  666.5 6.9 %copy-start.16 = (f32[256,256]{1,0:T(8,128)S(1)}, f32[256,256]{1,0:T(8,128)}, u32[]{:S(2)}) copy-start(f32[256,256]{1,0:T(8,128)} %get-tuple-element.120) | copy-start | bytes 786436
  666.5 6.9 %copy-start.29 = (f32[256,256]{1,0:T(8,128)S(1)}, f32[256,256]{1,0:T(8,128)}, u32[]{:S(2)}) copy-start(f32[256,256]{1,0:T(8,128)} %get-tuple-element.118) | copy-start | bytes 786436
  673.5 1.2 copy-start.30
Sparse Core Ops, SparseCore 0:
  175.3 90.0 reduce-scatter.1
  268.6 67.0 all-gather.4
  338.8 71.5 all-gather.6

commit v3 on v2

--- a/solution.py
+++ b/solution.py
@@ -7,6 +7,7 @@
 NF = 4096
 CB = 2048
 STEPS = 4
+FACTOR_TILE = 128
 
 
 def shards(child_front, child_panel, parent_front, tile_map, tile_count):
@@ -50,9 +51,10 @@
     parent_slab = jnp.sum(moved[:, :, col_width + slab :], axis=0)
     targets = jnp.arange(leaf_count * height // TILE, dtype=jnp.int32)
     picked = ((mapped[None, :] == targets[:, None]) & live_tiles[None, :]).astype(jnp.float32)
-    summed = jnp.einsum("ft,tbc->fbc", picked, child_part, precision=highest)
     own_parent = jnp.concatenate([parent_front, parent_slab], axis=1)
-    summed = summed.at[leaf_id].add(own_parent)
+    picked = jnp.concatenate([picked, (targets == leaf_id).astype(jnp.float32)[:, None]], axis=1)
+    sources = jnp.concatenate([child_part, own_parent[None]], axis=0)
+    summed = jnp.einsum("ft,tbc->fbc", picked, sources, precision=highest)
     summed = summed.reshape(leaf_count * height, col_width + slab)
     top_share = pivot_span // leaf_count
     slab_rows = summed[:, col_width:]
@@ -75,15 +77,24 @@
         return got.reshape(leaf_count * rows, panel_count * slab)
 
     pivot_block = assemble(my_slab[:top_share])
-    lower_block = assemble(my_slab[top_share:])
+    lower_share = height - top_share
+    lower_pieces = lax.all_gather(my_slab[top_share:], ("leaf", "panel"), axis=0, tiled=False)
+    lower_pieces = lower_pieces.reshape(leaf_count, panel_count, lower_share, slab)
 
-    blocks = pivot_span // TILE
-    eye = jnp.eye(TILE, dtype=jnp.float32)
+    def lower_rows(first, count):
+        span = -(-(count + lower_share - 1) // lower_share)
+        start = jnp.minimum(first // lower_share, leaf_count - span)
+        pieces = lax.dynamic_slice_in_dim(lower_pieces, start, span, 0)
+        pieces = pieces.transpose(0, 2, 1, 3).reshape(span * lower_share, panel_count * slab)
+        return lax.dynamic_slice_in_dim(pieces, first - start * lower_share, count, 0)
+
+    blocks = pivot_span // FACTOR_TILE
+    eye = jnp.eye(FACTOR_TILE, dtype=jnp.float32)
     work = pivot_block
     factor_cols = []
     inverses = []
     for k in range(blocks):
-        lo, hi = k * TILE, (k + 1) * TILE
+        lo, hi = k * FACTOR_TILE, (k + 1) * FACTOR_TILE
         diag = lax.linalg.cholesky(work[lo:hi, lo:hi], symmetrize_input=True)
         diag = jnp.tril(diag)
         inverse = lax.linalg.triangular_solve(diag, eye, left_side=True, lower=True)
@@ -91,26 +102,19 @@
         if k + 1 < blocks:
             below = jnp.dot(work[hi:, lo:hi], inverse.T, precision=highest)
             work = work.at[hi:, hi:].add(-jnp.dot(below, below.T, precision=highest))
-            column = jnp.concatenate([jnp.zeros((lo, TILE), jnp.float32), diag, below], axis=0)
+            column = jnp.concatenate([jnp.zeros((lo, FACTOR_TILE), jnp.float32), diag, below], axis=0)
         else:
-            column = jnp.concatenate([jnp.zeros((lo, TILE), jnp.float32), diag], axis=0)
+            column = jnp.concatenate([jnp.zeros((lo, FACTOR_TILE), jnp.float32), diag], axis=0)
         factor_cols.append(column)
     factor = jnp.concatenate(factor_cols, axis=1)
 
     top_tiles = pivot_span // height
-    own_rows = lax.dynamic_slice_in_dim(
-        lower_block, jnp.maximum(leaf_id - top_tiles, 0) * height, height, 0
-    )
-    col_rows = lax.dynamic_slice_in_dim(
-        lower_block,
-        jnp.maximum(panel_id - pivot_span // col_width, 0) * col_width,
-        col_width,
-        0,
-    )
+    own_rows = lower_rows(jnp.maximum(leaf_id - top_tiles, 0) * height, height)
+    col_rows = lower_rows(jnp.maximum(panel_id - pivot_span // col_width, 0) * col_width, col_width)
     extra = jnp.concatenate([own_rows, col_rows], axis=0)
     solved = []
     for k in range(blocks):
-        lo, hi = k * TILE, (k + 1) * TILE
+        lo, hi = k * FACTOR_TILE, (k + 1) * FACTOR_TILE
         part = extra[:, lo:hi]
         if k:
             part = part - jnp.dot(

time: 694 us -> 656 us (0.945)
  other arithmetic: 242 us -> 209 us
  local copies, waits for them, and re-layouts: 126 us -> 102 us
  matrix products: 61.1 us -> 84.7 us
    another operation x27 -> x24, other arithmetic: 139 us -> 100 us  [shards(): diag = lax.linalg.cholesky(work[lo:hi, lo:hi], symmetrize_input=True)]
    scatter-add x2 -> x0, local copies, waits for them, and re-layouts: 21.6 us -> none  [shards(): summed = summed.at[leaf_id].add(own_parent)]
    reshape x2 -> x1, local copies, waits for them, and re-layouts: 24.3 us -> 5.46 us  [assemble(): got = got.reshape(leaf_count, panel_count, rows, slab).transpose(0, 2, 1, 3)]
    dot_general x0 -> x1, local copies, waits for them, and re-layouts: none -> 18.1 us  [shards(): summed = jnp.einsum('ft,tbc->fbc', picked, sources, precision=highest)]
    another operation x31 -> x1, local copies, waits for them, and re-layouts: 15.7 us -> 0.28 us  [the longest x29 15.5 us: shards(): inverse = lax.linalg.triangular_solve(diag, eye, left_side=True, lower=True)]
    dot_general x3 -> x7, matrix products: 12.5 us -> 25.3 us  [shards(): jnp.dot(jnp.concatenate(solved, axis=1), factor[lo:hi, :lo].T, precision=...]
    dot_general x3 -> x7, matrix products: 6.68 us -> 14 us  [shards(): work = work.at[hi:, hi:].add(-jnp.dot(below, below.T, precision=highest))]
    unnamed x0 -> x7, other arithmetic: none -> 7.34 us
  transfers between devices with their start and end apart: 4 -> 4, of which waited for: 3 -> 3; matrix products, arithmetic and copies ran while one was open for 39% -> 36% of each run, Pallas kernels for 0% -> 0%
where the time goes in v3:
time: 656 us; the launch traced here: 646 us
  waiting for transfers between devices  228 us (35%)
  other arithmetic  209 us (32%)
  local copies, waits for them, and re-layouts  102 us (16%)
  matrix products  84.7 us (13%)
  between operations  15.4 us (2%)
    another operation x24, other arithmetic, shards(): diag = lax.linalg.cholesky(work[lo:hi, lo:hi], symmetrize_input=True)  100 us
    reduce_scatter x1, waiting for transfers between devices, shards(): reduced = lax.psum_scatter(summed, 'leaf', scatter_dimension=0, tiled=True)  89.9 us
    another operation x16, other arithmetic, shards(): inverse = lax.linalg.triangular_solve(diag, eye, left_side=True, lower=True)  85.7 us
    all_to_all x1, waiting for transfers between devices, shards(): lax.all_to_all(send, 'panel', split_axis=0, concat_axis=0, tiled=True)  70.9 us
    all_gather x1, waiting for transfers between devices, assemble(): got = lax.all_gather(piece, ('leaf', 'panel'), axis=0, tiled=False)  67.1 us
    unnamed x126, local copies, waits for them, and re-layouts  26.2 us
    dot_general x7, matrix products, shards(): jnp.dot(jnp.concatenate(solved, axis=1), factor[lo:hi, :lo].T, precision=...  25.3 us
    dot_general x1, local copies, waits for them, and re-layouts, shards(): summed = jnp.einsum('ft,tbc->fbc', picked, sources, precision=highest)  18.1 us
  transfers between devices with their start and end apart: 4, of which 3 were waited for; matrix products, arithmetic and copies ran while one was open for 36% of the time, Pallas kernels for 0%

profile of v3, /device:TPU:1, one launch (start us, length us, event | category | flops | bytes accessed | tf_op | source)
XLA Modules:
  0.0 645.7 jit_solution(17881528234524848925)
XLA Ops:
  6.5 11.5 %fusion.6 = f32[256,2048]{1,0:T(8,128)S(1)} fusion(bf16[1,2048,4096]{2,1,0:T(8,128)(2,1)} %param.23, f32[1,256,2048]{2,1,0:T(8,128)} %param.22, s32[]{:T(128)S(6)} %select_n.117), kind=kOutput, calls=%fused_computation.26 | convolution fusion | flops 4295491584 | bytes 23068676 | tf_op jit(solution)/shard_map/dot_general | solution.py:30
  19.6 3.8 convolution_bitcast_fusion
  23.4 5.3 reshape_reshape.3
  28.7 5.3 copy.186
  33.9 6.6 %copy.201 = f32[256,8,512]{2,0,1:T(8,128)} copy(f32[256,8,512]{2,1,0:T(8,128)} %reshape_reshape.3) | data formatting | bytes 8388608 | tf_op jit(solution)/shard_map/reshape;reshape | solution.py:40
  42.6 5.4 pad_maximum_fusion.1
  48.1 6.0 all-to-all-start
  54.5 70.9 %all-to-all-done = f32[8,256,768]{2,1,0:T(8,128)} async-done(((f32[8,256,768]{2,1,0:T(8,128)}), f32[8,256,768]{2,1,0:T(8,128)}, u32[]{:S(2)}, u32[]{:S(2)}) %all-to-all-start) | async-done | bytes 6291488 | tf_op jit(solution)/shard_map/all_to_all | solution.py:49
  125.3 2.9 slice.364
  128.2 3.0 copy.187
  133.1 5.5 fusion.2
  138.6 18.1 %copy.136 = f32[16,256,640]{2,1,0:T(8,128)} copy(f32[16,256,640]{2,0,1:T(8,128)S(1)} %fusion.2) | data formatting | bytes 20971520 | tf_op jit(solution)/shard_map/ft,tbc->fbc/dot_general | solution.py:57
  159.2 4.4 slice.366
  163.8 4.9 pad_maximum_fusion
  168.8 89.9 %reduce-scatter.2.cloned.1.call-done = f32[256,640]{1,0:T(8,128)} async-done(((f32[4096,640]{1,0:T(8,128)}), f32[256,640]{1,0:T(8,128)}) %reduce-scatter.2.cloned.1.call-update) | async-done | bytes 655376 | tf_op jit(solution)/shard_map/reduce_scatter | solution.py:69
  260.1 1.5 slice.391
  261.9 67.1 %all-gather.5.cloned.1.call-done = f32[8192,128]{1,0:T(8,128)} async-done(((f32[64,128]{1,0:T(8,128)}), f32[8192,128]{1,0:T(8,128)}) %all-gather.5.cloned.1.call-update) | async-done | bytes 4194320 | tf_op jit(solution)/shard_map/all_gather | solution.py:75
  328.9 5.5 copy.137
  335.4 1.9 copy-done.2
  338.6 11.7 %custom-call.20 = f32[128,128]{1,0:T(8,128)S(1)} custom-call(f32[128,128]{1,0:T(8,128)S(1)} %fusion.148), custom_call_target="Cholesky" | custom-call | tf_op jit(solution)/shard_map/cholesky/custom-call.1 | solution.py:98
  352.2 9.8 %custom-call.21 = f32[1,128,128]{1,2,0:T(8,128)S(1)} custom-call(f32[1,128,128]{2,1,0:T(8,128)S(1)} %get-tuple-element.105), custom_call_target="InvertDiagBlocksLowerTriangular" | custom-call | tf_op jit(solution)/shard_map/triangular_solve/custom-call.0 | solution.py:100
  362.1 3.3 copy.189
  366.3 1.5 fusion.55
  367.9 5.1 negate_add_fusion
  373.0 1.6 copy-done.6
  375.7 11.7 %custom-call.22 = f32[128,128]{1,0:T(8,128)S(1)} custom-call(f32[128,128]{1,0:T(8,128)S(1)} %copy.144), custom_call_target="Cholesky" | custom-call | tf_op jit(solution)/shard_map/cholesky/custom-call.1 | solution.py:98
  389.4 9.8 %custom-call.23 = f32[1,128,128]{1,2,0:T(8,128)S(1)} custom-call(f32[1,128,128]{2,1,0:T(8,128)S(1)} %get-tuple-element.103), custom_call_target="InvertDiagBlocksLowerTriangular" | custom-call | tf_op jit(solution)/shard_map/triangular_solve/custom-call.0 | solution.py:100
  400.1 1.8 fusion.67
  401.9 3.9 slice_add_fusion
  406.0 11.7 %custom-call.24 = f32[128,128]{1,0:T(8,128)S(1)} custom-call(f32[128,128]{1,0:T(8,128)S(1)} %copy.148), custom_call_target="Cholesky" | custom-call | tf_op jit(solution)/shard_map/cholesky/custom-call.1 | solution.py:98
  419.7 9.8 %custom-call.25 = f32[1,128,128]{1,2,0:T(8,128)S(1)} custom-call(f32[1,128,128]{2,1,0:T(8,128)S(1)} %get-tuple-element.101), custom_call_target="InvertDiagBlocksLowerTriangular" | custom-call | tf_op jit(solution)/shard_map/triangular_solve/custom-call.0 | solution.py:100
  434.8 11.9 %custom-call.26 = f32[128,128]{1,0:T(8,128)S(1)} custom-call(f32[128,128]{1,0:T(8,128)S(1)} %copy.152), custom_call_target="Cholesky" | custom-call | tf_op jit(solution)/shard_map/cholesky/custom-call.1 | solution.py:98
  448.1 9.8 %custom-call.27 = f32[1,128,128]{1,2,0:T(8,128)S(1)} custom-call(f32[1,128,128]{2,1,0:T(8,128)S(1)} %get-tuple-element.99), custom_call_target="InvertDiagBlocksLowerTriangular" | custom-call | tf_op jit(solution)/shard_map/triangular_solve/custom-call.0 | solution.py:100
  460.4 2.3 fusion.21
  462.9 11.7 %custom-call.28 = f32[128,128]{1,0:T(8,128)S(1)} custom-call(f32[128,128]{1,0:T(8,128)S(1)} %copy.156), custom_call_target="Cholesky" | custom-call | tf_op jit(solution)/shard_map/cholesky/custom-call.1 | solution.py:98
  476.1 9.8 %custom-call.29 = f32[1,128,128]{1,2,0:T(8,128)S(1)} custom-call(f32[1,128,128]{2,1,0:T(8,128)S(1)} %get-tuple-element.97), custom_call_target="InvertDiagBlocksLowerTriangular" | custom-call | tf_op jit(solution)/shard_map/triangular_solve/custom-call.0 | solution.py:100
  488.2 12.1 %custom-call.30 = f32[128,128]{1,0:T(8,128)S(1)} custom-call(f32[128,128]{1,0:T(8,128)S(1)} %copy.160), custom_call_target="Cholesky" | custom-call | tf_op jit(solution)/shard_map/cholesky/custom-call.1 | solution.py:98
  501.7 9.8 %custom-call.31 = f32[1,128,128]{1,2,0:T(8,128)S(1)} custom-call(f32[1,128,128]{2,1,0:T(8,128)S(1)} %get-tuple-element.95), custom_call_target="InvertDiagBlocksLowerTriangular" | custom-call | tf_op jit(solution)/shard_map/triangular_solve/custom-call.0 | solution.py:100
  513.3 11.7 %custom-call.32 = f32[128,128]{1,0:T(8,128)S(1)} custom-call(f32[128,128]{1,0:T(8,128)S(1)} %fusion.136), custom_call_target="Cholesky" | custom-call | tf_op jit(solution)/shard_map/cholesky/custom-call.1 | solution.py:98
  526.4 10.0 %custom-call.33 = f32[1,128,128]{1,2,0:T(8,128)S(1)} custom-call(f32[1,128,128]{2,1,0:T(8,128)S(1)} %get-tuple-element.93), custom_call_target="InvertDiagBlocksLowerTriangular" | custom-call | tf_op jit(solution)/shard_map/triangular_solve/custom-call.0 | solution.py:100
  537.8 11.7 %custom-call.34 = f32[128,128]{1,0:T(8,128)S(1)} custom-call(f32[128,128]{1,0:T(8,128)S(1)} %broadcast_multiply_fusion), custom_call_target="Cholesky" | custom-call | tf_op jit(solution)/shard_map/cholesky/custom-call.1 | solution.py:98
  550.9 9.8 %custom-call.35 = f32[1,128,128]{1,2,0:T(8,128)S(1)} custom-call(f32[1,128,128]{2,1,0:T(8,128)S(1)} %get-tuple-element.91), custom_call_target="InvertDiagBlocksLowerTriangular" | custom-call | tf_op jit(solution)/shard_map/triangular_solve/custom-call.0 | solution.py:100
  571.8 2.1 constant_dynamic-slice_fusion.1
  573.9 1.8 copy.191
  576.5 1.8 constant_dynamic-slice_fusion.3
  578.3 1.6 copy.190
  581.3 1.6 constant_dynamic-update-slice_fusion.17
  583.7 1.6 constant_dynamic-update-slice_fusion.16
  586.8 1.6 constant_dynamic-update-slice_fusion.15
  588.4 2.1 convolution_subtract_fusion.2
  590.6 1.6 constant_dynamic-update-slice_fusion.14
  592.9 3.5 fusion.32
  596.4 2.0 copy.171
  598.4 2.0 copy.170
  600.4 1.9 copy.169
  602.3 1.9 copy.168
  604.2 2.5 constant_dynamic-update-slice_fusion.13
  606.7 5.3 convolution_subtract_fusion.1
  613.5 5.6 convolution_subtract_fusion.4
  620.5 1.9 copy.174
  622.5 1.9 copy.173
  624.4 1.9 copy.172
  626.4 6.7 %convolution_subtract_fusion = f32[768,128]{1,0:T(8,128)S(1)} fusion(f32[768,896]{0,1:T(8,128)} %get-tuple-element.155, f32[1024,896]{1,0:T(8,128)} %copy-done.52, f32[512,1024]{1,0:T(8,128)S(1)} %constant_dynamic-slice_fusion, f32[256,1024]{1,0:T(8,128)S(1)} %constant_dynamic-slice_fusion.2), kind=kOutput, calls=%fused_computation.53 | convolution fusion | flops 1057161216 | bytes 6750208 | tf_op jit(solution)/shard_map/dot_general | solution.py:120
  636.2 2.8 fusion.29
  (239 shorter events, 62.8 us)
Async XLA Ops:
  18.0 1.6 copy-start.54
  40.5 1.7 copy-start.15
  48.1 77.3 %all-to-all-start = ((f32[8,256,768]{2,1,0:T(8,128)}), f32[8,256,768]{2,1,0:T(8,128)}, u32[]{:S(2)}, u32[]{:S(2)}) async-start(f32[8,256,768]{2,1,0:T(8,128)} %pad_maximum_fusion.1), calls=%async_computation | async-start | bytes 12582912 | tf_op jit(solution)/shard_map/all_to_all | solution.py:49
  54.1 204.6 %reduce-scatter.2.cloned.1.call-start = ((), (), s32[]{:S(2)}) async-start(), calls=%async_computation.2 | async-start | bytes 11141120 | tf_op jit(solution)/shard_map/reduce_scatter | solution.py:69
  168.7 160.2 %all-gather.5.cloned.1.call-start = ((), (), s32[]{:S(2)}) async-start(), calls=%async_computation.3 | async-start | bytes 4227072 | tf_op jit(solution)/shard_map/all_gather | solution.py:75
  260.1 311.7 %all-gather.7.cloned.1.call-start = ((), (), s32[]{:S(2)}) async-start(), calls=%async_computation.4 | async-start | bytes 12681216 | tf_op jit(solution)/shard_map/all_gather | solution.py:81
  335.4 1.9 copy-start.2
  365.7 0.6 copy-start.37
  367.9 192.8 %copy-start = (f32[896,128]{1,0:T(8,128)}, f32[896,128]{1,0:T(8,128)S(1)}, u32[]{:S(2)}) copy-start(f32[896,128]{1,0:T(8,128)S(1)} %fusion.55) | copy-start | bytes 1376260
  373.0 1.7 copy-start.6
  399.5 0.6 copy-start.46
  429.8 0.6 copy-start.48
  431.1 131.6 %copy-start.4 = (f32[640,128]{1,0:T(8,128)}, f32[640,128]{1,0:T(8,128)S(1)}, u32[]{:S(2)}) copy-start(f32[640,128]{1,0:T(8,128)S(1)} %fusion.74) | copy-start | bytes 983044
  432.6 1.2 copy-start.11
  448.1 115.6 %copy-start.35 = (f32[128,128]{1,0:T(8,128)}, f32[128,128]{1,0:T(8,128)S(1)}, u32[]{:S(2)}) copy-start(f32[128,128]{1,0:T(8,128)S(1)} %get-tuple-element.100) | copy-start | bytes 196612
  458.2 0.6 copy-start.40
  460.4 103.3 %copy-start.8 = (f32[512,128]{1,0:T(8,128)}, f32[512,128]{1,0:T(8,128)S(1)}, u32[]{:S(2)}) copy-start(f32[512,128]{1,0:T(8,128)S(1)} %fusion.86) | copy-start | bytes 786436
  486.2 0.6 copy-start.39
  486.8 73.9 %copy-start.18 = (f32[128,128]{1,0:T(8,128)S(1)}, f32[128,128]{1,0:T(8,128)}, u32[]{:S(2)}) copy-start(f32[128,128]{1,0:T(8,128)} %get-tuple-element.106) | copy-start | bytes 196612
  501.0 60.7 %copy-start.20 = (f32[128,128]{1,0:T(8,128)S(1)}, f32[128,128]{1,0:T(8,128)}, u32[]{:S(2)}) copy-start(f32[128,128]{1,0:T(8,128)} %get-tuple-element.104) | copy-start | bytes 196612
  511.8 0.6 copy-start.42
  536.7 0.6 copy-start.44
  537.6 25.1 %copy-start.32 = (f32[128,128]{1,0:T(8,128)S(1)}, f32[128,128]{1,0:T(8,128)}, u32[]{:S(2)}) copy-start(f32[128,128]{1,0:T(8,128)} %get-tuple-element.102) | copy-start | bytes 196612
  561.7 1.0 copy-start.22
  562.7 3.0 copy-start.13
  563.7 3.2 copy-start.16
  565.8 2.4 copy-start.50
  566.9 1.9 copy-start.51
  568.2 1.8 copy-start.52
  580.4 0.8 copy-start.38
  580.6 2.3 copy-start.1
  582.8 9.3 %copy-start.3 = (f32[768,128]{0,1:T(8,128)}, f32[768,128]{0,1:T(8,128)S(1)}, u32[]{:S(2)}) copy-start(f32[768,128]{0,1:T(8,128)S(1)} %get-tuple-element.149) | copy-start | bytes 1179652
  582.8 0.9 copy-start.47
  582.8 2.5 copy-start.19
  582.8 2.5 copy-start.21
  582.8 2.5 copy-start.23
  585.3 6.8 %copy-start.7 = (f32[768,128]{0,1:T(8,128)}, f32[768,128]{0,1:T(8,128)S(1)}, u32[]{:S(2)}) copy-start(f32[768,128]{0,1:T(8,128)S(1)} %get-tuple-element.150) | copy-start | bytes 1179652
  585.3 1.5 copy-start.49
  585.3 3.0 copy-start.5
  585.3 3.0 copy-start.14
  585.3 3.0 copy-start.33
  588.3 3.8 copy-start.10
  588.4 2.2 copy-start.41
  588.4 4.6 copy-start.9
  588.4 4.6 copy-start.17
  588.4 4.5 copy-start.36
  592.1 0.8 copy-start.12
  596.4 7.8 %copy-start.24 = (f32[768,128]{1,0:T(8,128)S(1)}, f32[768,128]{1,0:T(8,128)}, u32[]{:S(2)}) copy-start(f32[768,128]{1,0:T(8,128)} %fusion.32) | copy-start | bytes 1179652
  606.7 5.3 copy-start.43
  613.5 5.6 copy-start.45
  619.1 7.2 %copy-start.28 = (f32[768,128]{1,0:T(8,128)S(1)}, f32[768,128]{1,0:T(8,128)}, u32[]{:S(2)}) copy-start(f32[768,128]{1,0:T(8,128)} %copy.168) | copy-start | bytes 1179652
  626.4 6.7 %copy-start.27 = (f32[768,128]{1,0:T(8,128)S(1)}, f32[768,128]{1,0:T(8,128)}, u32[]{:S(2)}) copy-start(f32[768,128]{1,0:T(8,128)} %copy.169) | copy-start | bytes 1179652
  626.4 6.8 %copy-start.26 = (f32[768,128]{1,0:T(8,128)S(1)}, f32[768,128]{1,0:T(8,128)}, u32[]{:S(2)}) copy-start(f32[768,128]{1,0:T(8,128)} %copy.170) | copy-start | bytes 1179652
  626.4 6.9 %copy-start.25 = (f32[768,128]{1,0:T(8,128)S(1)}, f32[768,128]{1,0:T(8,128)}, u32[]{:S(2)}) copy-start(f32[768,128]{1,0:T(8,128)} %copy.171) | copy-start | bytes 1179652
  626.4 6.9 %copy-start.31 = (f32[768,128]{1,0:T(8,128)S(1)}, f32[768,128]{1,0:T(8,128)}, u32[]{:S(2)}) copy-start(f32[768,128]{1,0:T(8,128)} %copy.172) | copy-start | bytes 1179652
  633.1 1.0 copy-start.30
  633.1 1.1 copy-start.29
  633.1 1.1 copy-start.53
  633.3 2.9 copy-start.34
Sparse Core Ops, SparseCore 0:
  168.9 89.7 reduce-scatter.1
  261.8 67.0 all-gather.4
  332.0 70.9 all-gather.6

commit v4 on v3

--- a/solution.py
+++ b/solution.py
@@ -45,19 +45,17 @@
     parent_slabs = jnp.where(
         (dest // slabs_per_block == panel_id)[:, None, None], parent_slabs, 0.0
     )
-    send = jnp.concatenate([regular, pivot_slabs, parent_slabs], axis=2)
-    moved = lax.all_to_all(send, "panel", split_axis=0, concat_axis=0, tiled=True)
-    child_part = moved[:, :, : col_width + slab]
-    parent_slab = jnp.sum(moved[:, :, col_width + slab :], axis=0)
+    send_slabs = jnp.concatenate([pivot_slabs, parent_slabs], axis=2)
+    moved_slabs = lax.all_to_all(send_slabs, "panel", split_axis=0, concat_axis=0, tiled=True)
+    moved = lax.all_to_all(regular, "panel", split_axis=0, concat_axis=0, tiled=True)
+    parent_slab = jnp.sum(moved_slabs[:, :, slab:], axis=0)
     targets = jnp.arange(leaf_count * height // TILE, dtype=jnp.int32)
     picked = ((mapped[None, :] == targets[:, None]) & live_tiles[None, :]).astype(jnp.float32)
-    own_parent = jnp.concatenate([parent_front, parent_slab], axis=1)
     picked = jnp.concatenate([picked, (targets == leaf_id).astype(jnp.float32)[:, None]], axis=1)
-    sources = jnp.concatenate([child_part, own_parent[None]], axis=0)
-    summed = jnp.einsum("ft,tbc->fbc", picked, sources, precision=highest)
-    summed = summed.reshape(leaf_count * height, col_width + slab)
+    slab_sources = jnp.concatenate([moved_slabs[:, :, :slab], parent_slab[None]], axis=0)
+    slab_rows = jnp.einsum("ft,tbc->fbc", picked, slab_sources, precision=highest)
+    slab_rows = slab_rows.reshape(leaf_count * height, slab)
     top_share = pivot_span // leaf_count
-    slab_rows = summed[:, col_width:]
     slab_rows = jnp.concatenate(
         [
             slab_rows[:pivot_span].reshape(leaf_count, top_share, slab),
@@ -65,10 +63,12 @@
         ],
         axis=1,
     ).reshape(leaf_count * height, slab)
-    summed = jnp.concatenate([summed[:, :col_width], slab_rows], axis=1)
-    reduced = lax.psum_scatter(summed, "leaf", scatter_dimension=0, tiled=True)
-    front_block = reduced[:, :col_width]
-    my_slab = reduced[:, col_width:]
+    my_slab = lax.psum_scatter(slab_rows, "leaf", scatter_dimension=0, tiled=True)
+    sources = jnp.concatenate([moved, parent_front[None]], axis=0)
+    summed = jnp.einsum("ft,tbc->fbc", picked, sources, precision=highest)
+    front_block = lax.psum_scatter(
+        summed.reshape(leaf_count * height, col_width), "leaf", scatter_dimension=0, tiled=True
+    )
 
     def assemble(piece):
         rows = piece.shape[0]

time: 656 us -> 585 us (0.89)
  waiting for transfers between devices: 228 us -> 156 us
  other arithmetic: 209 us -> 198 us
  starting transfers between devices: 6.46 us -> 13.2 us
    all_gather x1, waiting for transfers between devices: 67.1 us -> 0.02 us  [assemble(): got = lax.all_gather(piece, ('leaf', 'panel'), axis=0, tiled=False)]
    reduce_scatter x1 -> x2, waiting for transfers between devices: 89.9 us -> 74.5 us  [the longest x1 74.4 us: shards(): lax.psum_scatter(slab_rows, 'leaf', scatter_dimension=0, tiled=True)]
    all_to_all x1 -> x2, waiting for transfers between devices: 70.9 us -> 81.4 us  [the longest x1 55.2 us: shards(): lax.all_to_all(regular, 'panel', split_axis=0, concat_axis=0, tiled=True)]
    concatenate x3 -> x1, other arithmetic: 10.4 us -> 0.18 us  [shards(): send_slabs = jnp.concatenate([pivot_slabs, parent_slabs], axis=2)]
    slice x2 -> x0, local copies, waits for them, and re-layouts: 7.22 us -> none  [the longest x1 4.36 us: shards(): summed = jnp.concatenate([summed[:, :col_width], slab_rows], axis=1)]
    all_to_all x1 -> x2, starting transfers between devices: 6 us -> 12.8 us  [the longest x1 6.88 us: shards(): lax.all_to_all(regular, 'panel', split_axis=0, concat_axis=0, tiled=True)]
    unnamed x126 -> x94, local copies, waits for them, and re-layouts: 26.2 us -> 28 us
  transfers between devices with their start and end apart: 4 -> 6, of which waited for: 3 -> 3; matrix products, arithmetic and copies ran while one was open for 36% -> 60% of each run, Pallas kernels for 0% -> 0%
where the time goes in v4:
time: 585 us; the launch traced here: 574 us
  other arithmetic  198 us (34%)
  waiting for transfers between devices  156 us (27%)
  local copies, waits for them, and re-layouts  101 us (17%)
  matrix products  90.4 us (15%)
  between operations  15.2 us (3%)
  starting transfers between devices  13.2 us (2%)
    another operation x24, other arithmetic, shards(): diag = lax.linalg.cholesky(work[lo:hi, lo:hi], symmetrize_input=True)  99.6 us
    another operation x16, other arithmetic, shards(): inverse = lax.linalg.triangular_solve(diag, eye, left_side=True, lower=True)  85.1 us
    reduce_scatter x1, waiting for transfers between devices, shards(): lax.psum_scatter(slab_rows, 'leaf', scatter_dimension=0, tiled=True)  74.4 us
    all_to_all x1, waiting for transfers between devices, shards(): lax.all_to_all(regular, 'panel', split_axis=0, concat_axis=0, tiled=True)  55.2 us
    dot_general x7, matrix products, shards(): jnp.dot(jnp.concatenate(solved, axis=1), factor[lo:hi, :lo].T, precision=...  28.8 us
    unnamed x94, local copies, waits for them, and re-layouts  28 us
    all_to_all x1, waiting for transfers between devices, shards(): lax.all_to_all(send_slabs, 'panel', split_axis=0, concat_axis=0, tiled=True)  26.2 us
    dot_general x1, local copies, waits for them, and re-layouts, shards(): summed = jnp.einsum('ft,tbc->fbc', picked, sources, precision=highest)  16.8 us
  transfers between devices with their start and end apart: 6, of which 3 were waited for; matrix products, arithmetic and copies ran while one was open for 60% of the time, Pallas kernels for 0%

profile of v4, /device:TPU:1, one launch (start us, length us, event | category | flops | bytes accessed | tf_op | source)
XLA Modules:
  0.0 574.1 jit_solution(13147944634463905368)
XLA Ops:
  6.5 11.5 %fusion.6 = f32[256,2048]{1,0:T(8,128)S(1)} fusion(bf16[1,2048,4096]{2,1,0:T(8,128)(2,1)} %param.23, f32[1,256,2048]{2,1,0:T(8,128)} %param.22, s32[]{:T(128)S(6)} %select_n.117), kind=kOutput, calls=%fused_computation.24 | convolution fusion | flops 4295491584 | bytes 23068676 | tf_op jit(solution)/shard_map/dot_general | solution.py:30
  19.6 3.7 convolution_bitcast_fusion
  23.3 5.3 copy.193
  30.7 1.8 copy.137
  32.5 6.0 %all-to-all-start = ((f32[8,256,256]{2,1,0:T(8,128)}), f32[8,256,256]{2,1,0:T(8,128)S(1)}, u32[]{:S(2)}, u32[]{:S(2)}) async-start(f32[8,256,256]{2,1,0:T(8,128)} %copy.137), calls=%async_computation | async-start | bytes 4194304 | tf_op jit(solution)/shard_map/all_to_all | solution.py:49
  38.5 26.2 %all-to-all-done = f32[8,256,256]{2,1,0:T(8,128)S(1)} async-done(((f32[8,256,256]{2,1,0:T(8,128)}), f32[8,256,256]{2,1,0:T(8,128)S(1)}, u32[]{:S(2)}, u32[]{:S(2)}) %all-to-all-start) | async-done | bytes 2097184 | tf_op jit(solution)/shard_map/all_to_all | solution.py:49
  69.0 74.4 %reduce-scatter.3.cloned.1.call-done = f32[256,128]{1,0:T(8,128)} async-done(((f32[4096,128]{1,0:T(8,128)}), f32[256,128]{1,0:T(8,128)}) %reduce-scatter.3.cloned.1.call-update) | async-done | bytes 131088 | tf_op jit(solution)/shard_map/reduce_scatter | solution.py:66
  146.7 5.2 reshape_reshape.3
  151.9 6.6 %copy.208 = f32[256,8,512]{2,0,1:T(8,128)} copy(f32[256,8,512]{2,1,0:T(8,128)} %reshape_reshape.3) | data formatting | bytes 8388608 | tf_op jit(solution)/shard_map/reshape;reshape | solution.py:40
  158.5 6.9 %all-to-all-start.1 = ((f32[8,256,512]{2,1,0:T(8,128)}), f32[8,256,512]{2,1,0:T(8,128)}, u32[]{:S(2)}, u32[]{:S(2)}) async-start(f32[8,256,512]{2,1,0:T(8,128)} %bitcast.173), calls=%async_computation.2 | async-start | bytes 8388608 | tf_op jit(solution)/shard_map/all_to_all | solution.py:50
  165.9 55.2 %all-to-all-done.1 = f32[8,256,512]{2,1,0:T(8,128)} async-done(((f32[8,256,512]{2,1,0:T(8,128)}), f32[8,256,512]{2,1,0:T(8,128)}, u32[]{:S(2)}, u32[]{:S(2)}) %all-to-all-start.1) | async-done | bytes 4194336 | tf_op jit(solution)/shard_map/all_to_all | solution.py:50
  221.0 4.6 copy.181
  225.6 5.0 fusion.2
  230.6 16.8 %copy.182 = f32[16,256,512]{2,1,0:T(8,128)} copy(f32[16,256,512]{2,0,1:T(8,128)S(1)} %fusion.2) | data formatting | bytes 16777216 | tf_op jit(solution)/shard_map/ft,tbc->fbc/dot_general | solution.py:68
  247.5 5.5 copy.141
  254.0 2.0 copy-done.1
  256.0 2.0 slice.359
  258.9 11.7 %custom-call.20 = f32[128,128]{1,0:T(8,128)S(1)} custom-call(f32[128,128]{1,0:T(8,128)S(1)} %fusion.152), custom_call_target="Cholesky" | custom-call | tf_op jit(solution)/shard_map/cholesky/custom-call.1 | solution.py:98
  272.6 9.8 %custom-call.21 = f32[1,128,128]{1,2,0:T(8,128)S(1)} custom-call(f32[1,128,128]{2,1,0:T(8,128)S(1)} %get-tuple-element.105), custom_call_target="InvertDiagBlocksLowerTriangular" | custom-call | tf_op jit(solution)/shard_map/triangular_solve/custom-call.0 | solution.py:100
  283.3 2.0 fusion.59
  285.3 4.6 copy.196
  289.9 4.9 negate_add_fusion
  294.8 1.7 copy-done.3
  297.6 11.7 %custom-call.22 = f32[128,128]{1,0:T(8,128)S(1)} custom-call(f32[128,128]{1,0:T(8,128)S(1)} %copy.148), custom_call_target="Cholesky" | custom-call | tf_op jit(solution)/shard_map/cholesky/custom-call.1 | solution.py:98
  311.1 9.8 %custom-call.23 = f32[1,128,128]{1,2,0:T(8,128)S(1)} custom-call(f32[1,128,128]{2,1,0:T(8,128)S(1)} %get-tuple-element.103), custom_call_target="InvertDiagBlocksLowerTriangular" | custom-call | tf_op jit(solution)/shard_map/triangular_solve/custom-call.0 | solution.py:100
  321.8 1.8 fusion.71
  323.7 3.7 slice_add_fusion
  327.6 11.9 %custom-call.24 = f32[128,128]{1,0:T(8,128)S(1)} custom-call(f32[128,128]{1,0:T(8,128)S(1)} %copy.152), custom_call_target="Cholesky" | custom-call | tf_op jit(solution)/shard_map/cholesky/custom-call.1 | solution.py:98
  341.3 9.8 %custom-call.25 = f32[1,128,128]{1,2,0:T(8,128)S(1)} custom-call(f32[1,128,128]{2,1,0:T(8,128)S(1)} %get-tuple-element.101), custom_call_target="InvertDiagBlocksLowerTriangular" | custom-call | tf_op jit(solution)/shard_map/triangular_solve/custom-call.0 | solution.py:100
  356.5 11.7 %custom-call.26 = f32[128,128]{1,0:T(8,128)S(1)} custom-call(f32[128,128]{1,0:T(8,128)S(1)} %copy.156), custom_call_target="Cholesky" | custom-call | tf_op jit(solution)/shard_map/cholesky/custom-call.1 | solution.py:98
  369.4 10.0 %custom-call.27 = f32[1,128,128]{1,2,0:T(8,128)S(1)} custom-call(f32[1,128,128]{2,1,0:T(8,128)S(1)} %get-tuple-element.99), custom_call_target="InvertDiagBlocksLowerTriangular" | custom-call | tf_op jit(solution)/shard_map/triangular_solve/custom-call.0 | solution.py:100
  381.9 2.4 fusion.25
  384.5 11.7 %custom-call.28 = f32[128,128]{1,0:T(8,128)S(1)} custom-call(f32[128,128]{1,0:T(8,128)S(1)} %copy.160), custom_call_target="Cholesky" | custom-call | tf_op jit(solution)/shard_map/cholesky/custom-call.1 | solution.py:98
  397.4 9.8 %custom-call.29 = f32[1,128,128]{1,2,0:T(8,128)S(1)} custom-call(f32[1,128,128]{2,1,0:T(8,128)S(1)} %get-tuple-element.97), custom_call_target="InvertDiagBlocksLowerTriangular" | custom-call | tf_op jit(solution)/shard_map/triangular_solve/custom-call.0 | solution.py:100
  409.5 12.1 %custom-call.30 = f32[128,128]{1,0:T(8,128)S(1)} custom-call(f32[128,128]{1,0:T(8,128)S(1)} %copy.164), custom_call_target="Cholesky" | custom-call | tf_op jit(solution)/shard_map/cholesky/custom-call.1 | solution.py:98
  422.9 9.8 %custom-call.31 = f32[1,128,128]{1,2,0:T(8,128)S(1)} custom-call(f32[1,128,128]{2,1,0:T(8,128)S(1)} %get-tuple-element.95), custom_call_target="InvertDiagBlocksLowerTriangular" | custom-call | tf_op jit(solution)/shard_map/triangular_solve/custom-call.0 | solution.py:100
  434.5 11.7 %custom-call.32 = f32[128,128]{1,0:T(8,128)S(1)} custom-call(f32[128,128]{1,0:T(8,128)S(1)} %fusion.140), custom_call_target="Cholesky" | custom-call | tf_op jit(solution)/shard_map/cholesky/custom-call.1 | solution.py:98
  447.4 9.8 %custom-call.33 = f32[1,128,128]{1,2,0:T(8,128)S(1)} custom-call(f32[1,128,128]{2,1,0:T(8,128)S(1)} %get-tuple-element.93), custom_call_target="InvertDiagBlocksLowerTriangular" | custom-call | tf_op jit(solution)/shard_map/triangular_solve/custom-call.0 | solution.py:100
  458.5 11.7 %custom-call.34 = f32[128,128]{1,0:T(8,128)S(1)} custom-call(f32[128,128]{1,0:T(8,128)S(1)} %broadcast_multiply_fusion), custom_call_target="Cholesky" | custom-call | tf_op jit(solution)/shard_map/cholesky/custom-call.1 | solution.py:98
  471.6 9.8 %custom-call.35 = f32[1,128,128]{1,2,0:T(8,128)S(1)} custom-call(f32[1,128,128]{2,1,0:T(8,128)S(1)} %get-tuple-element.91), custom_call_target="InvertDiagBlocksLowerTriangular" | custom-call | tf_op jit(solution)/shard_map/triangular_solve/custom-call.0 | solution.py:100
  492.5 2.1 constant_dynamic-slice_fusion.1
  494.6 1.8 copy.198
  497.2 1.8 constant_dynamic-slice_fusion.3
  499.1 1.8 copy.197
  502.2 1.7 constant_dynamic-update-slice_fusion.17
  503.9 1.9 copy.172
  505.8 1.8 convolution_subtract_fusion.3
  507.7 1.7 constant_dynamic-update-slice_fusion.16
  509.4 1.9 copy.173
  511.3 2.6 convolution_subtract_fusion.5
  513.8 1.7 constant_dynamic-update-slice_fusion.15
  515.5 2.0 copy.174
  517.5 3.3 convolution_subtract_fusion.2
  522.5 1.9 copy.175
  524.4 4.0 fusion.36
  528.4 1.7 constant_dynamic-update-slice_fusion.13
  530.1 5.0 convolution_subtract_fusion.1
  536.7 5.6 convolution_subtract_fusion.4
  543.7 1.9 copy.178
  545.6 1.9 copy.177
  547.6 1.9 copy.176
  553.0 6.4 %convolution_subtract_fusion = f32[768,128]{1,0:T(8,128)S(1)} fusion(f32[768,896]{0,1:T(8,128)} %get-tuple-element.157, f32[1024,896]{1,0:T(8,128)} %copy-done.36, f32[512,1024]{1,0:T(8,128)S(1)} %constant_dynamic-slice_fusion, f32[256,1024]{1,0:T(8,128)S(1)} %constant_dynamic-slice_fusion.2), kind=kOutput, calls=%fused_computation.56 | convolution fusion | flops 1057161216 | bytes 6750208 | tf_op jit(solution)/shard_map/dot_general | solution.py:120
  559.9 1.6 copy-done.6
  563.0 4.4 fusion.33
  (212 shorter events, 63.8 us)
Async XLA Ops:
  18.0 1.6 copy-start.38
  23.3 6.6 %copy-start.8 = (f32[256,512]{1,0:T(8,128)S(1)}, f32[256,512]{1,0:T(8,128)}, u32[]{:S(2)}) copy-start(f32[256,512]{1,0:T(8,128)} %param.24) | copy-start | bytes 1572868
  32.5 32.2 %all-to-all-start = ((f32[8,256,256]{2,1,0:T(8,128)}), f32[8,256,256]{2,1,0:T(8,128)S(1)}, u32[]{:S(2)}, u32[]{:S(2)}) async-start(f32[8,256,256]{2,1,0:T(8,128)} %copy.137), calls=%async_computation | async-start | bytes 4194304 | tf_op jit(solution)/shard_map/all_to_all | solution.py:49
  38.5 105.0 %reduce-scatter.3.cloned.1.call-start = ((), (), s32[]{:S(2)}) async-start(), calls=%async_computation.4 | async-start | bytes 2228224 | tf_op jit(solution)/shard_map/reduce_scatter | solution.py:66
  69.0 178.5 %all-gather.5.cloned.1.call-start = ((), (), s32[]{:S(2)}) async-start(), calls=%async_computation.6 | async-start | bytes 4227072 | tf_op jit(solution)/shard_map/all_gather | solution.py:75
  144.8 347.7 %all-gather.7.cloned.1.call-start = ((), (), s32[]{:S(2)}) async-start(), calls=%async_computation.7 | async-start | bytes 12681216 | tf_op jit(solution)/shard_map/all_gather | solution.py:81
  158.5 6.9 %copy-start.9 = (f32[256,512]{1,0:T(8,128)S(1)}, f32[256,512]{1,0:T(8,128)}, u32[]{:S(2)}) copy-start(f32[256,512]{1,0:T(8,128)} %param.24) | copy-start | bytes 1572868
  158.5 62.6 %all-to-all-start.1 = ((f32[8,256,512]{2,1,0:T(8,128)}), f32[8,256,512]{2,1,0:T(8,128)}, u32[]{:S(2)}, u32[]{:S(2)}) async-start(f32[8,256,512]{2,1,0:T(8,128)} %bitcast.173), calls=%async_computation.2 | async-start | bytes 8388608 | tf_op jit(solution)/shard_map/all_to_all | solution.py:50
  165.4 397.6 %reduce-scatter.5.cloned.1.call-start = ((), (), s32[]{:S(2)}) async-start(), calls=%async_computation.5 | async-start | bytes 8912896 | tf_op jit(solution)/shard_map/reduce_scatter | solution.py:69
  254.0 2.0 copy-start.1
  282.7 0.6 copy-start.20
  285.3 196.2 %copy-start = (f32[896,128]{1,0:T(8,128)}, f32[896,128]{1,0:T(8,128)S(1)}, u32[]{:S(2)}) copy-start(f32[896,128]{1,0:T(8,128)S(1)} %fusion.59) | copy-start | bytes 1376260
  294.8 1.7 copy-start.3
  321.2 0.6 copy-start.30
  351.4 0.6 copy-start.32
  352.8 130.7 %copy-start.2 = (f32[640,128]{1,0:T(8,128)}, f32[640,128]{1,0:T(8,128)S(1)}, u32[]{:S(2)}) copy-start(f32[640,128]{1,0:T(8,128)S(1)} %fusion.78) | copy-start | bytes 983044
  354.2 1.2 copy-start.5
  369.4 115.0 %copy-start.19 = (f32[128,128]{1,0:T(8,128)}, f32[128,128]{1,0:T(8,128)S(1)}, u32[]{:S(2)}) copy-start(f32[128,128]{1,0:T(8,128)S(1)} %get-tuple-element.100) | copy-start | bytes 196612
  379.7 0.6 copy-start.24
  381.9 102.6 %copy-start.4 = (f32[512,128]{1,0:T(8,128)}, f32[512,128]{1,0:T(8,128)S(1)}, u32[]{:S(2)}) copy-start(f32[512,128]{1,0:T(8,128)S(1)} %fusion.90) | copy-start | bytes 786436
  407.5 0.6 copy-start.22
  408.6 72.8 %copy-start.11 = (f32[128,128]{1,0:T(8,128)S(1)}, f32[128,128]{1,0:T(8,128)}, u32[]{:S(2)}) copy-start(f32[128,128]{1,0:T(8,128)} %get-tuple-element.106) | copy-start | bytes 196612
  433.0 0.6 copy-start.26
  434.0 48.5 %copy-start.12 = (f32[128,128]{1,0:T(8,128)S(1)}, f32[128,128]{1,0:T(8,128)}, u32[]{:S(2)}) copy-start(f32[128,128]{1,0:T(8,128)} %get-tuple-element.104) | copy-start | bytes 196612
  457.7 13.3 %copy-start.28 = (f32[128,128]{1,0:T(8,128)}, f32[128,128]{1,0:T(8,128)S(1)}, u32[]{:S(2)}) copy-start(f32[128,128]{1,0:T(8,128)S(1)} %fusion.102) | copy-start | bytes 196612
  471.6 11.8 %copy-start.18 = (f32[128,128]{1,0:T(8,128)S(1)}, f32[128,128]{1,0:T(8,128)}, u32[]{:S(2)}) copy-start(f32[128,128]{1,0:T(8,128)} %get-tuple-element.102) | copy-start | bytes 196612
  482.5 1.0 copy-start.13
  483.5 3.1 copy-start.7
  484.5 3.2 copy-start.10
  486.5 2.4 copy-start.34
  487.7 1.8 copy-start.35
  489.0 1.8 copy-start.36
  501.4 0.8 copy-start.21
  505.8 1.8 copy-start.31
  511.3 2.6 copy-start.33
  517.5 3.3 copy-start.25
  524.4 4.0 copy-start.23
  530.1 5.0 copy-start.27
  536.7 5.6 copy-start.29
  542.3 7.2 %copy-start.14 = (f32[768,128]{1,0:T(8,128)S(1)}, f32[768,128]{1,0:T(8,128)}, u32[]{:S(2)}) copy-start(f32[768,128]{1,0:T(8,128)} %copy.172) | copy-start | bytes 1179652
  549.5 3.3 copy-start.17
  549.5 3.4 copy-start.16
  549.5 3.4 copy-start.15
  552.9 6.5 %copy-start.37 = (f32[128,128]{1,0:T(8,128)S(1)}, f32[128,128]{1,0:T(8,128)}, u32[]{:S(2)}) copy-start(f32[128,128]{1,0:T(8,128)} %fusion.100) | copy-start | bytes 196612
  559.9 1.7 copy-start.6
Sparse Core Ops, SparseCore 0:
  69.1 74.3 reduce-scatter.2
  146.6 69.8 all-gather.4
  219.6 77.3 all-gather.6
  300.3 84.1 reduce-scatter.4

commit v5 on v1

--- a/solution.py
+++ b/solution.py
@@ -7,6 +7,7 @@
 NF = 4096
 CB = 2048
 STEPS = 4
+FACTOR_TILE = 128
 
 
 def shards(child_front, child_panel, parent_front, tile_map, tile_count):
@@ -44,23 +45,22 @@
     parent_slabs = jnp.where(
         (dest // slabs_per_block == panel_id)[:, None, None], parent_slabs, 0.0
     )
-    send = jnp.concatenate([regular, pivot_slabs, parent_slabs], axis=2)
-    moved = lax.all_to_all(send, "panel", split_axis=0, concat_axis=0, tiled=True)
-    child_part = moved[:, :, : col_width + slab]
-    parent_slab = jnp.sum(moved[:, :, col_width + slab :], axis=0)
+    send_slabs = jnp.concatenate([pivot_slabs, parent_slabs], axis=2)
+    moved_slabs = lax.all_to_all(send_slabs, "panel", split_axis=0, concat_axis=0, tiled=True)
+    moved = lax.all_to_all(regular, "panel", split_axis=0, concat_axis=0, tiled=True)
+    parent_slab = jnp.sum(moved_slabs[:, :, slab:], axis=0)
     targets = jnp.arange(leaf_count * height // TILE, dtype=jnp.int32)
     picked = ((mapped[None, :] == targets[:, None]) & live_tiles[None, :]).astype(jnp.float32)
-    summed = jnp.einsum("ft,tbc->fbc", picked, child_part, precision=highest)
-    own_parent = jnp.concatenate([parent_front, parent_slab], axis=1)
-    summed = summed.at[leaf_id].add(own_parent)
-    reduced = lax.psum_scatter(
-        summed.reshape(leaf_count * height, col_width + slab),
-        "leaf",
-        scatter_dimension=0,
-        tiled=True,
+    picked = jnp.concatenate([picked, (targets == leaf_id).astype(jnp.float32)[:, None]], axis=1)
+    slab_sources = jnp.concatenate([moved_slabs[:, :, :slab], parent_slab[None]], axis=0)
+    slab_rows = jnp.einsum("ft,tbc->fbc", picked, slab_sources, precision=highest)
+    slab_rows = slab_rows.reshape(leaf_count * height, slab)
+    my_slab = lax.psum_scatter(slab_rows, "leaf", scatter_dimension=0, tiled=True)
+    sources = jnp.concatenate([moved, parent_front[None]], axis=0)
+    summed = jnp.einsum("ft,tbc->fbc", picked, sources, precision=highest)
+    front_block = lax.psum_scatter(
+        summed.reshape(leaf_count * height, col_width), "leaf", scatter_dimension=0, tiled=True
     )
-    front_block = reduced[:, :col_width]
-    my_slab = reduced[:, col_width:]
 
     gathered = lax.all_gather(my_slab, ("leaf", "panel"), axis=0, tiled=False)
     gathered = gathered.reshape(leaf_count, panel_count, height, slab)
@@ -70,19 +70,34 @@
         return tiles.transpose(0, 2, 1, 3).reshape(count * height, panel_count * slab)
 
     top_tiles = pivot_span // height
-    pivot_block = rows_of(gathered[:top_tiles])
+    col_tiles = col_width // height
     own_rows = rows_of(lax.dynamic_slice_in_dim(gathered, leaf_id, 1, 0))
-    col_tiles = col_width // height
     col_rows = rows_of(lax.dynamic_slice_in_dim(gathered, panel_id * col_tiles, col_tiles, 0))
+    work = jnp.concatenate([rows_of(gathered[:top_tiles]), own_rows, col_rows], axis=0)
 
-    factor = jnp.linalg.cholesky(pivot_block)
-    solved = lax.linalg.triangular_solve(
-        factor,
-        jnp.concatenate([own_rows, col_rows], axis=0),
-        left_side=False,
-        lower=True,
-        transpose_a=True,
-    )
+    blocks = pivot_span // FACTOR_TILE
+    eye = jnp.eye(FACTOR_TILE, dtype=jnp.float32)
+    factor_cols = []
+    solved = []
+    for k in range(blocks):
+        lo, hi = k * FACTOR_TILE, (k + 1) * FACTOR_TILE
+        diag = lax.linalg.cholesky(work[lo:hi, lo:hi], symmetrize_input=True)
+        diag = jnp.tril(diag)
+        inverse = lax.linalg.triangular_solve(diag, eye, left_side=True, lower=True)
+        below = jnp.dot(work[hi:, lo:hi], inverse.T, precision=highest)
+        if hi < pivot_span:
+            work = work.at[hi:, hi:].add(
+                -jnp.dot(below, below[: pivot_span - hi].T, precision=highest)
+            )
+        factor_cols.append(
+            jnp.concatenate(
+                [jnp.zeros((lo, FACTOR_TILE), jnp.float32), diag, below[: pivot_span - hi]], axis=0
+            )
+        )
+        solved.append(below[pivot_span - hi :])
+    factor = jnp.concatenate(factor_cols, axis=1)
+    solved = jnp.concatenate(solved, axis=1)
+
     factor_rows = lax.dynamic_slice_in_dim(
         factor, jnp.minimum(leaf_id, top_tiles - 1) * height, height, 0
     )

time: 786 us -> 564 us (0.72)
  other arithmetic: 280 us -> 202 us
  waiting for transfers between devices: 243 us -> 166 us
  local copies, waits for them, and re-layouts: 126 us -> 90 us
  matrix products: 100 us -> 72.5 us
    all_gather x1, waiting for transfers between devices: 82.1 us -> 0.02 us  [shards(): gathered = lax.all_gather(my_slab, ('leaf', 'panel'), axis=0, tiled=False)]
    another operation x35 -> x40, other arithmetic: 268 us -> 190 us  [the longest x24 101 us: shards(): diag = lax.linalg.cholesky(work[lo:hi, lo:hi], symmetrize_input=True)]
    another operation x29 -> x8, matrix products: 73.8 us -> 2.28 us  [shards(): inverse = lax.linalg.triangular_solve(diag, eye, left_side=True, lower=True)]
    dot_general x1 -> x17, matrix products: 7.01 us -> 49.3 us  [the longest x7 27.1 us: shards(): jnp.dot(below, below[:pivot_span - hi].T, precision=highest)]
    another operation x40 -> x1, local copies, waits for them, and re-layouts: 40.8 us -> 0.01 us  [shards(): diag = lax.linalg.cholesky(work[lo:hi, lo:hi], symmetrize_input=True)]
    scatter-add x2 -> x0, local copies, waits for them, and re-layouts: 25.6 us -> none  [shards(): summed = summed.at[leaf_id].add(own_parent)]
    all_to_all x1 -> x2, waiting for transfers between devices: 70.3 us -> 91.4 us  [the longest x1 65.2 us: shards(): lax.all_to_all(regular, 'panel', split_axis=0, concat_axis=0, tiled=True)]
    dot_general x0 -> x2, local copies, waits for them, and re-layouts: none -> 20.3 us  [the longest x1 18.3 us: shards(): summed = jnp.einsum('ft,tbc->fbc', picked, sources, precision=highest)]
  transfers between devices with their start and end apart: 3 -> 5, of which waited for: 3 -> 3; matrix products, arithmetic and copies ran while one was open for 0% -> 56% of each run, Pallas kernels for 0% -> 0%
where the time goes in v5:
time: 564 us; the launch traced here: 558 us
  other arithmetic  202 us (36%)
  waiting for transfers between devices  166 us (29%)
  local copies, waits for them, and re-layouts  90 us (16%)
  matrix products  72.5 us (13%)
  between operations  15.1 us (3%)
  starting transfers between devices  13 us (2%)
    another operation x24, other arithmetic, shards(): diag = lax.linalg.cholesky(work[lo:hi, lo:hi], symmetrize_input=True)  101 us
    another operation x16, other arithmetic, shards(): inverse = lax.linalg.triangular_solve(diag, eye, left_side=True, lower=True)  89.3 us
    reduce_scatter x1, waiting for transfers between devices, shards(): lax.psum_scatter(slab_rows, 'leaf', scatter_dimension=0, tiled=True)  74.2 us
    all_to_all x1, waiting for transfers between devices, shards(): lax.all_to_all(regular, 'panel', split_axis=0, concat_axis=0, tiled=True)  65.2 us
    dot_general x7, matrix products, shards(): jnp.dot(below, below[:pivot_span - hi].T, precision=highest)  27.1 us
    all_to_all x1, waiting for transfers between devices, shards(): lax.all_to_all(send_slabs, 'panel', split_axis=0, concat_axis=0, tiled=True)  26.2 us
    unnamed x70, local copies, waits for them, and re-layouts  21.9 us
    dot_general x1, local copies, waits for them, and re-layouts, shards(): summed = jnp.einsum('ft,tbc->fbc', picked, sources, precision=highest)  18.3 us
  transfers between devices with their start and end apart: 5, of which 3 were waited for; matrix products, arithmetic and copies ran while one was open for 56% of the time, Pallas kernels for 0%

profile of v5, /device:TPU:1, one launch (start us, length us, event | category | flops | bytes accessed | tf_op | source)
XLA Modules:
  0.0 557.8 jit_solution(9423121733334572174)
XLA Ops:
  6.5 12.8 %fusion.9 = f32[256,2048]{1,0:T(8,128)} fusion(bf16[1,2048,4096]{2,1,0:T(8,128)(2,1)} %param.23, f32[1,256,2048]{2,1,0:T(8,128)} %param.22, s32[]{:T(128)S(6)} %select_n.103), kind=kOutput, calls=%fused_computation.16 | convolution fusion | flops 4295491584 | bytes 23068676 | tf_op jit(solution)/shard_map/dot_general | solution.py:30
  19.4 2.5 copy.164
  24.8 3.7 convolution_bitcast_fusion
  28.5 5.2 copy.162
  33.8 1.3 slice.348
  35.5 1.9 copy.114
  37.3 6.0 %all-to-all-start = ((f32[8,256,256]{2,1,0:T(8,128)}), f32[8,256,256]{2,1,0:T(8,128)S(1)}, u32[]{:S(2)}, u32[]{:S(2)}) async-start(f32[8,256,256]{2,1,0:T(8,128)} %copy.114), calls=%async_computation | async-start | bytes 4194304 | tf_op jit(solution)/shard_map/all_to_all | solution.py:49
  43.3 26.2 %all-to-all-done = f32[8,256,256]{2,1,0:T(8,128)S(1)} async-done(((f32[8,256,256]{2,1,0:T(8,128)}), f32[8,256,256]{2,1,0:T(8,128)S(1)}, u32[]{:S(2)}, u32[]{:S(2)}) %all-to-all-start) | async-done | bytes 2097184 | tf_op jit(solution)/shard_map/all_to_all | solution.py:49
  71.4 2.0 copy.116
  73.8 74.2 %reduce-scatter.3.cloned.1.call-done = f32[256,128]{1,0:T(8,128)} async-done(((f32[4096,128]{1,0:T(8,128)}), f32[256,128]{1,0:T(8,128)}) %reduce-scatter.3.cloned.1.call-update) | async-done | bytes 131088 | tf_op jit(solution)/shard_map/reduce_scatter | solution.py:58
  147.9 5.2 reshape_reshape.3
  153.2 6.6 %copy.168 = f32[256,8,512]{2,0,1:T(8,128)} copy(f32[256,8,512]{2,1,0:T(8,128)} %reshape_reshape.3) | data formatting | bytes 8388608 | tf_op jit(solution)/shard_map/reshape;reshape | solution.py:40
  159.7 6.7 %all-to-all-start.1 = ((f32[8,256,512]{2,1,0:T(8,128)}), f32[8,256,512]{2,1,0:T(8,128)}, u32[]{:S(2)}, u32[]{:S(2)}) async-start(f32[8,256,512]{2,1,0:T(8,128)} %bitcast.150), calls=%async_computation.2 | async-start | bytes 8388608 | tf_op jit(solution)/shard_map/all_to_all | solution.py:50
  166.8 65.2 %all-to-all-done.1 = f32[8,256,512]{2,1,0:T(8,128)} async-done(((f32[8,256,512]{2,1,0:T(8,128)}), f32[8,256,512]{2,1,0:T(8,128)}, u32[]{:S(2)}, u32[]{:S(2)}) %all-to-all-start.1) | async-done | bytes 4194336 | tf_op jit(solution)/shard_map/all_to_all | solution.py:50
  232.0 4.6 copy.150
  236.6 5.0 fusion.2
  241.6 18.3 %copy.151 = f32[16,256,512]{2,1,0:T(8,128)} copy(f32[16,256,512]{2,0,1:T(8,128)S(1)} %fusion.2) | data formatting | bytes 16777216 | tf_op jit(solution)/shard_map/ft,tbc->fbc/dot_general | solution.py:60
  260.7 1.7 dynamic-slice_bitcast_fusion
  262.4 2.4 copy.122
  264.8 1.8 copy.166
  266.5 1.6 dynamic-slice_bitcast_fusion.1
  268.1 1.4 copy.121
  269.5 4.4 slice.351
  273.9 5.3 copy.117
  279.2 3.5 copy.165
  282.8 1.9 copy-done
  285.8 11.7 %custom-call.20 = f32[128,128]{1,0:T(8,128)S(1)} custom-call(f32[128,128]{1,0:T(8,128)S(1)} %copy.120), custom_call_target="Cholesky" | custom-call | tf_op jit(solution)/shard_map/cholesky/custom-call.1 | solution.py:84
  298.2 1.3 select_bitcast_fusion.7
  299.5 9.8 %custom-call.21 = f32[1,128,128]{1,2,0:T(8,128)S(1)} custom-call(f32[1,128,128]{2,1,0:T(8,128)S(1)} %get-tuple-element.105), custom_call_target="InvertDiagBlocksLowerTriangular" | custom-call | tf_op jit(solution)/shard_map/triangular_solve/custom-call.0 | solution.py:86
  309.6 2.7 fusion.31
  312.4 5.8 %fusion.6 = f32[1664,896]{0,1:T(8,128)S(1)} fusion(f32[512,1024]{0,1:T(8,128)S(1)} %bitcast.149, f32[256,1024]{0,1:T(8,128)S(1)} %bitcast.154, f32[1024,1024]{0,1:T(8,128)S(1)} %bitcast.146, f32[1664,128]{1,0:T(8,128)S(1)} %fusion.31), kind=kOutput, calls=%fused_computation.7 | convolution fusion | flops 2296053760 | bytes 14614528 | tf_op jit(solution)/shard_map/dot_general | solution.py:90
  318.2 2.5 copy-done.2
  321.8 11.7 %custom-call.22 = f32[128,128]{1,0:T(8,128)S(1)} custom-call(f32[128,128]{1,0:T(8,128)S(1)} %copy.126), custom_call_target="Cholesky" | custom-call | tf_op jit(solution)/shard_map/cholesky/custom-call.1 | solution.py:84
  334.2 1.3 select_bitcast_fusion.6
  335.5 9.8 %custom-call.23 = f32[1,128,128]{1,2,0:T(8,128)S(1)} custom-call(f32[1,128,128]{2,1,0:T(8,128)S(1)} %get-tuple-element.103), custom_call_target="InvertDiagBlocksLowerTriangular" | custom-call | tf_op jit(solution)/shard_map/triangular_solve/custom-call.0 | solution.py:86
  345.6 2.5 fusion.37
  348.1 6.1 %slice_add_fusion = f32[1536,768]{0,1:T(8,128)S(1)} fusion(f32[1664,896]{0,1:T(8,128)} %copy-done.2, f32[1536,128]{1,0:T(8,128)S(1)} %fusion.37), kind=kOutput, calls=%fused_computation.9 | convolution fusion | flops 1814298624 | bytes 10616832 | tf_op jit(solution)/shard_map/dot_general | solution.py:90
  354.2 2.1 copy-done.3
  357.4 11.7 %custom-call.24 = f32[128,128]{1,0:T(8,128)S(1)} custom-call(f32[128,128]{1,0:T(8,128)S(1)} %copy.130), custom_call_target="Cholesky" | custom-call | tf_op jit(solution)/shard_map/cholesky/custom-call.1 | solution.py:84
  371.1 9.8 %custom-call.25 = f32[1,128,128]{1,2,0:T(8,128)S(1)} custom-call(f32[1,128,128]{2,1,0:T(8,128)S(1)} %get-tuple-element.101), custom_call_target="InvertDiagBlocksLowerTriangular" | custom-call | tf_op jit(solution)/shard_map/triangular_solve/custom-call.0 | solution.py:86
  381.2 2.4 fusion.39
  383.6 5.5 slice_add_fusion.1
  389.1 1.8 copy-done.4
  391.9 11.9 %custom-call.26 = f32[128,128]{1,0:T(8,128)S(1)} custom-call(f32[128,128]{1,0:T(8,128)S(1)} %copy.134), custom_call_target="Cholesky" | custom-call | tf_op jit(solution)/shard_map/cholesky/custom-call.1 | solution.py:84
  404.5 1.3 select_bitcast_fusion.4
  405.8 9.8 %custom-call.27 = f32[1,128,128]{1,2,0:T(8,128)S(1)} custom-call(f32[1,128,128]{2,1,0:T(8,128)S(1)} %get-tuple-element.99), custom_call_target="InvertDiagBlocksLowerTriangular" | custom-call | tf_op jit(solution)/shard_map/triangular_solve/custom-call.0 | solution.py:86
  415.9 2.3 fusion.41
  419.2 4.0 fusion.7
  424.0 12.9 %custom-call.28 = f32[128,128]{1,0:T(8,128)S(1)} custom-call(f32[128,128]{1,0:T(8,128)} %copy.138), custom_call_target="Cholesky" | custom-call | tf_op jit(solution)/shard_map/cholesky/custom-call.1 | solution.py:84
  438.9 9.8 %custom-call.29 = f32[1,128,128]{1,2,0:T(8,128)S(1)} custom-call(f32[1,128,128]{2,1,0:T(8,128)S(1)} %get-tuple-element.97), custom_call_target="InvertDiagBlocksLowerTriangular" | custom-call | tf_op jit(solution)/shard_map/triangular_solve/custom-call.0 | solution.py:86
  450.1 1.6 fusion.8
  454.0 11.7 %custom-call.30 = f32[128,128]{1,0:T(8,128)S(1)} custom-call(f32[128,128]{1,0:T(8,128)S(1)} %copy.142), custom_call_target="Cholesky" | custom-call | tf_op jit(solution)/shard_map/cholesky/custom-call.1 | solution.py:84
  466.4 1.3 select_bitcast_fusion.2
  467.7 9.8 %custom-call.31 = f32[1,128,128]{1,2,0:T(8,128)S(1)} custom-call(f32[1,128,128]{2,1,0:T(8,128)S(1)} %get-tuple-element.95), custom_call_target="InvertDiagBlocksLowerTriangular" | custom-call | tf_op jit(solution)/shard_map/triangular_solve/custom-call.0 | solution.py:86
  477.8 2.2 fusion.45
  480.1 2.4 fusion.20
  484.5 11.7 %custom-call.32 = f32[128,128]{1,0:T(8,128)S(1)} custom-call(f32[128,128]{1,0:T(8,128)S(1)} %fusion.68), custom_call_target="Cholesky" | custom-call | tf_op jit(solution)/shard_map/cholesky/custom-call.1 | solution.py:84
  498.1 9.8 %custom-call.33 = f32[1,128,128]{1,2,0:T(8,128)S(1)} custom-call(f32[1,128,128]{2,1,0:T(8,128)S(1)} %get-tuple-element.93), custom_call_target="InvertDiagBlocksLowerTriangular" | custom-call | tf_op jit(solution)/shard_map/triangular_solve/custom-call.0 | solution.py:86
  508.2 1.9 fusion.47
  510.2 1.8 fusion.30
  513.8 11.9 %custom-call.34 = f32[128,128]{1,0:T(8,128)S(1)} custom-call(f32[128,128]{1,0:T(8,128)S(1)} %broadcast_multiply_fusion), custom_call_target="Cholesky" | custom-call | tf_op jit(solution)/shard_map/cholesky/custom-call.1 | solution.py:84
  527.7 10.4 %custom-call.35 = f32[1,128,128]{1,2,0:T(8,128)} custom-call(f32[1,128,128]{2,1,0:T(8,128)S(1)} %get-tuple-element.91), custom_call_target="InvertDiagBlocksLowerTriangular" | custom-call | tf_op jit(solution)/shard_map/triangular_solve/custom-call.0 | solution.py:86
  544.8 1.6 copy-done.20
  546.6 4.4 fusion.27
  (175 shorter events, 38.0 us)
Async XLA Ops:
  19.4 3.2 copy-start.23
  19.4 5.4 copy-start.29
  37.3 32.2 %all-to-all-start = ((f32[8,256,256]{2,1,0:T(8,128)}), f32[8,256,256]{2,1,0:T(8,128)S(1)}, u32[]{:S(2)}, u32[]{:S(2)}) async-start(f32[8,256,256]{2,1,0:T(8,128)} %copy.114), calls=%async_computation | async-start | bytes 4194304 | tf_op jit(solution)/shard_map/all_to_all | solution.py:49
  43.3 104.6 %reduce-scatter.3.cloned.1.call-start = ((), (), s32[]{:S(2)}) async-start(), calls=%async_computation.4 | async-start | bytes 2228224 | tf_op jit(solution)/shard_map/reduce_scatter | solution.py:58
  73.5 187.2 %all-gather.3.cloned.1.call-start = ((), (), s32[]{:S(2)}) async-start(), calls=%async_computation.6 | async-start | bytes 16908288 | tf_op jit(solution)/shard_map/all_gather | solution.py:65
  159.7 72.3 %all-to-all-start.1 = ((f32[8,256,512]{2,1,0:T(8,128)}), f32[8,256,512]{2,1,0:T(8,128)}, u32[]{:S(2)}, u32[]{:S(2)}) async-start(f32[8,256,512]{2,1,0:T(8,128)} %bitcast.150), calls=%async_computation.2 | async-start | bytes 8388608 | tf_op jit(solution)/shard_map/all_to_all | solution.py:50
  166.5 380.2 %reduce-scatter.5.cloned.1.call-start = ((), (), s32[]{:S(2)}) async-start(), calls=%async_computation.5 | async-start | bytes 8912896 | tf_op jit(solution)/shard_map/reduce_scatter | solution.py:61
  282.8 1.9 copy-start
  309.6 2.8 copy-start.1
  309.6 2.8 copy-start.7
  312.4 5.8 %copy-start.5 = (f32[1664,128]{1,0:T(8,128)}, f32[1664,128]{1,0:T(8,128)S(1)}, u32[]{:S(2)}) copy-start(f32[1664,128]{1,0:T(8,128)S(1)} %fusion.31) | copy-start | bytes 2555908
  318.2 2.6 copy-start.2
  354.2 2.1 copy-start.3
  383.6 5.5 copy-start.8
  389.1 1.8 copy-start.4
  418.2 1.0 copy-start.10
  450.1 1.6 copy-start.13
  451.7 1.2 copy-start.12
  480.0 28.2 %copy-start.15 = (f32[1024,128]{1,0:T(8,128)}, f32[1024,128]{1,0:T(8,128)S(1)}, u32[]{:S(2)}) copy-start(f32[1024,128]{1,0:T(8,128)S(1)} %fusion.45) | copy-start | bytes 1572868
  480.0 58.1 %slice-start = ((f32[1664,128]{1,0:T(8,128)}), f32[896,128]{1,0:T(8,128)S(1)}, s32[]{:S(2)}) async-start(f32[1664,128]{1,0:T(8,128)} %copy-done.5), calls=%async_computation.7 | async-start | bytes 917504 | tf_op jit(solution)/shard_map/slice | solution.py:94
  480.0 58.1 %copy-start.24 = (f32[128,128]{1,0:T(8,128)S(1)}, f32[128,128]{1,0:T(8,128)}, u32[]{:S(2)}) copy-start(f32[128,128]{1,0:T(8,128)} %get-tuple-element.106) | copy-start | bytes 196612
  480.1 58.1 %copy-start.6 = (f32[1664,128]{1,0:T(8,128)S(1)}, f32[1664,128]{1,0:T(8,128)}, u32[]{:S(2)}) copy-start(f32[1664,128]{1,0:T(8,128)} %copy-done.5) | copy-start | bytes 2555908
  482.5 1.0 copy-start.19
  498.1 40.3 %copy-start.25 = (f32[128,128]{1,0:T(8,128)S(1)}, f32[128,128]{1,0:T(8,128)}, u32[]{:S(2)}) copy-start(f32[128,128]{1,0:T(8,128)} %get-tuple-element.104) | copy-start | bytes 196612
  510.2 28.0 %copy-start.17 = (f32[896,128]{1,0:T(8,128)}, f32[896,128]{1,0:T(8,128)S(1)}, u32[]{:S(2)}) copy-start(f32[896,128]{1,0:T(8,128)S(1)} %fusion.47) | copy-start | bytes 1376260
  510.2 28.3 %slice-start.1 = ((f32[1408,128]{1,0:T(8,128)}), f32[640,128]{1,0:T(8,128)S(1)}, s32[]{:S(2)}) async-start(f32[1408,128]{1,0:T(8,128)} %copy-done.8), calls=%async_computation.8 | async-start | bytes 655360 | tf_op jit(solution)/shard_map/slice | solution.py:94
  512.0 0.8 copy-start.21
  512.8 28.1 %slice-start.2 = ((f32[1152,128]{1,0:T(8,128)}), f32[384,128]{1,0:T(8,128)S(1)}, s32[]{:S(2)}) async-start(f32[1152,128]{1,0:T(8,128)} %copy-done.13), calls=%async_computation.9 | async-start | bytes 393216 | tf_op jit(solution)/shard_map/slice | solution.py:94
  526.4 15.6 %slice-start.3 = ((f32[1024,128]{1,0:T(8,128)}), f32[256,128]{1,0:T(8,128)S(1)}, s32[]{:S(2)}) async-start(f32[1024,128]{1,0:T(8,128)} %copy-done.15), calls=%async_computation.10 | async-start | bytes 262144 | tf_op jit(solution)/shard_map/slice | solution.py:94
  538.2 4.9 copy-start.26
  538.2 5.1 copy-start.27
  538.3 4.8 slice-start.4
  538.3 5.1 copy-start.28
  538.3 5.4 copy-start.9
  538.4 5.4 copy-start.11
  538.4 5.4 copy-start.14
  538.5 5.4 copy-start.16
  539.7 4.2 copy-start.18
  540.9 3.1 copy-start.22
  544.8 1.7 copy-start.20
Sparse Core Ops, SparseCore 0:
  73.6 74.2 reduce-scatter.2
  151.1 95.1 all-gather.2
  260.1 82.5 reduce-scatter.4

commit v6 on v5

--- a/solution.py
+++ b/solution.py
@@ -12,6 +12,7 @@
 
 def shards(child_front, child_panel, parent_front, tile_map, tile_count):
     highest = lax.Precision.HIGHEST
+    high = lax.Precision.HIGH
     panel_count = lax.axis_size("panel")
     leaf_count = lax.axis_size("leaf")
     leaf_id = lax.axis_index("leaf")
@@ -84,10 +85,10 @@
         diag = lax.linalg.cholesky(work[lo:hi, lo:hi], symmetrize_input=True)
         diag = jnp.tril(diag)
         inverse = lax.linalg.triangular_solve(diag, eye, left_side=True, lower=True)
-        below = jnp.dot(work[hi:, lo:hi], inverse.T, precision=highest)
+        below = jnp.dot(work[hi:, lo:hi], inverse.T, precision=high)
         if hi < pivot_span:
             work = work.at[hi:, hi:].add(
-                -jnp.dot(below, below[: pivot_span - hi].T, precision=highest)
+                -jnp.dot(below, below[: pivot_span - hi].T, precision=high)
             )
         factor_cols.append(
             jnp.concatenate(
@@ -107,7 +108,7 @@
         row_part,
         col_part,
         (((1,), (1,)), ((), ())),
-        precision=highest,
+        precision=high,
         preferred_element_type=jnp.float32,
     )
     pivot_blocks = pivot_span // col_width

time: 564 us -> 547 us (0.970)
  matrix products: 72.5 us -> 59.9 us
  local copies, waits for them, and re-layouts: 90 us -> 80.6 us
    dot_general x15, matrix products: 43.1 us -> 31.4 us  [the longest x7 19.4 us: shards(): jnp.dot(below, below[:pivot_span - hi].T, precision=high)]
    dot_general x1, local copies, waits for them, and re-layouts: 18.3 us -> 8.25 us  [shards(): summed = jnp.einsum('ft,tbc->fbc', picked, sources, precision=highest)]
  transfers between devices with their start and end apart: 5 -> 5, of which waited for: 3 -> 3; matrix products, arithmetic and copies ran while one was open for 56% -> 54% of each run, Pallas kernels for 0% -> 0%
where the time goes in v6:
time: 547 us; the launch traced here: 536 us
  other arithmetic  202 us (37%)
  waiting for transfers between devices  165 us (30%)
  local copies, waits for them, and re-layouts  80.6 us (15%)
  matrix products  59.9 us (11%)
  between operations  15.1 us (3%)
  starting transfers between devices  13.2 us (2%)
    another operation x24, other arithmetic, shards(): diag = lax.linalg.cholesky(work[lo:hi, lo:hi], symmetrize_input=True)  101 us
    another operation x16, other arithmetic, shards(): inverse = lax.linalg.triangular_solve(diag, eye, left_side=True, lower=True)  89.3 us
    reduce_scatter x1, waiting for transfers between devices, shards(): lax.psum_scatter(slab_rows, 'leaf', scatter_dimension=0, tiled=True)  74 us
    all_to_all x1, waiting for transfers between devices, shards(): lax.all_to_all(regular, 'panel', split_axis=0, concat_axis=0, tiled=True)  65.2 us
    all_to_all x1, waiting for transfers between devices, shards(): lax.all_to_all(send_slabs, 'panel', split_axis=0, concat_axis=0, tiled=True)  26.2 us
    unnamed x70, local copies, waits for them, and re-layouts  22.6 us
    dot_general x7, matrix products, shards(): jnp.dot(below, below[:pivot_span - hi].T, precision=high)  19.4 us
    dot_general x1, matrix products, shards(): lax.dot_general(own_panel, panel_all, (((1,), (1,)), ((), ())), preferred...  12.8 us
  transfers between devices with their start and end apart: 5, of which 3 were waited for; matrix products, arithmetic and copies ran while one was open for 54% of the time, Pallas kernels for 0%

profile of v6, /device:TPU:1, one launch (start us, length us, event | category | flops | bytes accessed | tf_op | source)
XLA Modules:
  0.0 536.1 jit_solution(5696650660345154615)
XLA Ops:
  6.5 12.8 %fusion.9 = f32[256,2048]{1,0:T(8,128)} fusion(bf16[1,2048,4096]{2,1,0:T(8,128)(2,1)} %param.23, f32[1,256,2048]{2,1,0:T(8,128)} %param.22, s32[]{:T(128)S(6)} %select_n.103), kind=kOutput, calls=%fused_computation.16 | convolution fusion | flops 4295491584 | bytes 23068676 | tf_op jit(solution)/shard_map/dot_general | solution.py:31
  19.4 2.5 copy.164
  24.8 3.7 convolution_bitcast_fusion
  28.5 5.2 copy.162
  33.8 1.3 slice.348
  35.5 1.9 copy.114
  37.3 6.0 %all-to-all-start = ((f32[8,256,256]{2,1,0:T(8,128)}), f32[8,256,256]{2,1,0:T(8,128)S(1)}, u32[]{:S(2)}, u32[]{:S(2)}) async-start(f32[8,256,256]{2,1,0:T(8,128)} %copy.114), calls=%async_computation | async-start | bytes 4194304 | tf_op jit(solution)/shard_map/all_to_all | solution.py:50
  43.3 26.2 %all-to-all-done = f32[8,256,256]{2,1,0:T(8,128)S(1)} async-done(((f32[8,256,256]{2,1,0:T(8,128)}), f32[8,256,256]{2,1,0:T(8,128)S(1)}, u32[]{:S(2)}, u32[]{:S(2)}) %all-to-all-start) | async-done | bytes 2097184 | tf_op jit(solution)/shard_map/all_to_all | solution.py:50
  71.4 2.0 copy.116
  74.0 74.0 %reduce-scatter.3.cloned.1.call-done = f32[256,128]{1,0:T(8,128)} async-done(((f32[4096,128]{1,0:T(8,128)}), f32[256,128]{1,0:T(8,128)}) %reduce-scatter.3.cloned.1.call-update) | async-done | bytes 131088 | tf_op jit(solution)/shard_map/reduce_scatter | solution.py:59
  148.0 5.2 reshape_reshape.3
  153.2 6.6 %copy.168 = f32[256,8,512]{2,0,1:T(8,128)} copy(f32[256,8,512]{2,1,0:T(8,128)} %reshape_reshape.3) | data formatting | bytes 8388608 | tf_op jit(solution)/shard_map/reshape;reshape | solution.py:41
  159.8 6.7 %all-to-all-start.1 = ((f32[8,256,512]{2,1,0:T(8,128)}), f32[8,256,512]{2,1,0:T(8,128)}, u32[]{:S(2)}, u32[]{:S(2)}) async-start(f32[8,256,512]{2,1,0:T(8,128)} %bitcast.150), calls=%async_computation.2 | async-start | bytes 8388608 | tf_op jit(solution)/shard_map/all_to_all | solution.py:51
  166.9 65.2 %all-to-all-done.1 = f32[8,256,512]{2,1,0:T(8,128)} async-done(((f32[8,256,512]{2,1,0:T(8,128)}), f32[8,256,512]{2,1,0:T(8,128)}, u32[]{:S(2)}, u32[]{:S(2)}) %all-to-all-start.1) | async-done | bytes 4194336 | tf_op jit(solution)/shard_map/all_to_all | solution.py:51
  232.1 4.6 copy.150
  236.7 5.0 fusion.2
  241.7 8.3 %copy.151 = f32[16,256,512]{2,1,0:T(8,128)} copy(f32[16,256,512]{2,0,1:T(8,128)S(1)} %fusion.2) | data formatting | bytes 16777216 | tf_op jit(solution)/shard_map/ft,tbc->fbc/dot_general | solution.py:61
  250.7 1.7 dynamic-slice_bitcast_fusion
  252.5 2.4 copy.122
  254.8 1.8 copy.166
  256.6 1.6 dynamic-slice_bitcast_fusion.1
  258.2 1.4 copy.121
  259.6 4.4 slice.351
  264.0 5.3 copy.117
  269.3 3.6 copy.165
  272.8 1.9 copy-done
  275.8 11.7 %custom-call.20 = f32[128,128]{1,0:T(8,128)S(1)} custom-call(f32[128,128]{1,0:T(8,128)S(1)} %copy.120), custom_call_target="Cholesky" | custom-call | tf_op jit(solution)/shard_map/cholesky/custom-call.1 | solution.py:85
  288.2 1.3 select_bitcast_fusion.7
  289.5 9.8 %custom-call.21 = f32[1,128,128]{1,2,0:T(8,128)S(1)} custom-call(f32[1,128,128]{2,1,0:T(8,128)S(1)} %get-tuple-element.105), custom_call_target="InvertDiagBlocksLowerTriangular" | custom-call | tf_op jit(solution)/shard_map/triangular_solve/custom-call.0 | solution.py:87
  299.7 2.1 fusion.31
  302.4 3.0 fusion.6
  305.5 2.5 copy-done.2
  309.1 12.1 %custom-call.22 = f32[128,128]{1,0:T(8,128)S(1)} custom-call(f32[128,128]{1,0:T(8,128)S(1)} %copy.126), custom_call_target="Cholesky" | custom-call | tf_op jit(solution)/shard_map/cholesky/custom-call.1 | solution.py:85
  321.8 1.3 select_bitcast_fusion.6
  323.1 9.8 %custom-call.23 = f32[1,128,128]{1,2,0:T(8,128)S(1)} custom-call(f32[1,128,128]{2,1,0:T(8,128)S(1)} %get-tuple-element.103), custom_call_target="InvertDiagBlocksLowerTriangular" | custom-call | tf_op jit(solution)/shard_map/triangular_solve/custom-call.0 | solution.py:87
  333.2 1.9 fusion.37
  335.2 4.6 slice_add_fusion
  339.8 2.1 copy-done.3
  343.0 11.7 %custom-call.24 = f32[128,128]{1,0:T(8,128)S(1)} custom-call(f32[128,128]{1,0:T(8,128)S(1)} %copy.130), custom_call_target="Cholesky" | custom-call | tf_op jit(solution)/shard_map/cholesky/custom-call.1 | solution.py:85
  356.8 9.8 %custom-call.25 = f32[1,128,128]{1,2,0:T(8,128)S(1)} custom-call(f32[1,128,128]{2,1,0:T(8,128)S(1)} %get-tuple-element.101), custom_call_target="InvertDiagBlocksLowerTriangular" | custom-call | tf_op jit(solution)/shard_map/triangular_solve/custom-call.0 | solution.py:87
  366.9 1.9 fusion.39
  368.8 4.1 slice_add_fusion.1
  372.9 1.8 copy-done.4
  375.7 11.7 %custom-call.26 = f32[128,128]{1,0:T(8,128)S(1)} custom-call(f32[128,128]{1,0:T(8,128)S(1)} %copy.134), custom_call_target="Cholesky" | custom-call | tf_op jit(solution)/shard_map/cholesky/custom-call.1 | solution.py:85
  388.1 1.3 select_bitcast_fusion.4
  389.4 9.8 %custom-call.27 = f32[1,128,128]{1,2,0:T(8,128)S(1)} custom-call(f32[1,128,128]{2,1,0:T(8,128)S(1)} %get-tuple-element.99), custom_call_target="InvertDiagBlocksLowerTriangular" | custom-call | tf_op jit(solution)/shard_map/triangular_solve/custom-call.0 | solution.py:87
  399.5 1.8 fusion.41
  402.3 3.2 fusion.7
  406.3 12.5 %custom-call.28 = f32[128,128]{1,0:T(8,128)S(1)} custom-call(f32[128,128]{1,0:T(8,128)} %copy.138), custom_call_target="Cholesky" | custom-call | tf_op jit(solution)/shard_map/cholesky/custom-call.1 | solution.py:85
  419.5 1.3 select_bitcast_fusion.3
  420.8 9.8 %custom-call.29 = f32[1,128,128]{1,2,0:T(8,128)S(1)} custom-call(f32[1,128,128]{2,1,0:T(8,128)S(1)} %get-tuple-element.97), custom_call_target="InvertDiagBlocksLowerTriangular" | custom-call | tf_op jit(solution)/shard_map/triangular_solve/custom-call.0 | solution.py:87
  434.8 12.1 %custom-call.30 = f32[128,128]{1,0:T(8,128)S(1)} custom-call(f32[128,128]{1,0:T(8,128)S(1)} %copy.142), custom_call_target="Cholesky" | custom-call | tf_op jit(solution)/shard_map/cholesky/custom-call.1 | solution.py:85
  447.6 1.3 select_bitcast_fusion.2
  448.9 9.8 %custom-call.31 = f32[1,128,128]{1,2,0:T(8,128)S(1)} custom-call(f32[1,128,128]{2,1,0:T(8,128)S(1)} %get-tuple-element.95), custom_call_target="InvertDiagBlocksLowerTriangular" | custom-call | tf_op jit(solution)/shard_map/triangular_solve/custom-call.0 | solution.py:87
  459.0 1.6 fusion.45
  460.7 2.0 fusion.20
  464.6 11.7 %custom-call.32 = f32[128,128]{1,0:T(8,128)S(1)} custom-call(f32[128,128]{1,0:T(8,128)S(1)} %fusion.68), custom_call_target="Cholesky" | custom-call | tf_op jit(solution)/shard_map/cholesky/custom-call.1 | solution.py:85
  478.3 9.8 %custom-call.33 = f32[1,128,128]{1,2,0:T(8,128)S(1)} custom-call(f32[1,128,128]{2,1,0:T(8,128)S(1)} %get-tuple-element.93), custom_call_target="InvertDiagBlocksLowerTriangular" | custom-call | tf_op jit(solution)/shard_map/triangular_solve/custom-call.0 | solution.py:87
  488.4 1.6 fusion.47
  490.0 1.6 fusion.30
  493.4 11.9 %custom-call.34 = f32[128,128]{1,0:T(8,128)S(1)} custom-call(f32[128,128]{1,0:T(8,128)S(1)} %broadcast_multiply_fusion), custom_call_target="Cholesky" | custom-call | tf_op jit(solution)/shard_map/cholesky/custom-call.1 | solution.py:85
  507.2 10.4 %custom-call.35 = f32[1,128,128]{1,2,0:T(8,128)} custom-call(f32[1,128,128]{2,1,0:T(8,128)S(1)} %get-tuple-element.91), custom_call_target="InvertDiagBlocksLowerTriangular" | custom-call | tf_op jit(solution)/shard_map/triangular_solve/custom-call.0 | solution.py:87
  524.1 1.6 copy-done.20
  525.9 3.5 fusion.27
  (175 shorter events, 37.9 us)
Async XLA Ops:
  19.4 3.2 copy-start.23
  19.4 5.4 %copy-start.29 = (s32[1,8]{1,0:T(1,128)S(1)}, s32[1,8]{1,0:T(1,128)}, u32[]{:S(2)}) copy-start(s32[1,8]{1,0:T(1,128)} %param.25) | copy-start | bytes 100
  37.3 32.2 %all-to-all-start = ((f32[8,256,256]{2,1,0:T(8,128)}), f32[8,256,256]{2,1,0:T(8,128)S(1)}, u32[]{:S(2)}, u32[]{:S(2)}) async-start(f32[8,256,256]{2,1,0:T(8,128)} %copy.114), calls=%async_computation | async-start | bytes 4194304 | tf_op jit(solution)/shard_map/all_to_all | solution.py:50
  43.3 104.7 %reduce-scatter.3.cloned.1.call-start = ((), (), s32[]{:S(2)}) async-start(), calls=%async_computation.4 | async-start | bytes 2228224 | tf_op jit(solution)/shard_map/reduce_scatter | solution.py:59
  73.5 177.2 %all-gather.3.cloned.1.call-start = ((), (), s32[]{:S(2)}) async-start(), calls=%async_computation.6 | async-start | bytes 16908288 | tf_op jit(solution)/shard_map/all_gather | solution.py:66
  159.8 72.3 %all-to-all-start.1 = ((f32[8,256,512]{2,1,0:T(8,128)}), f32[8,256,512]{2,1,0:T(8,128)}, u32[]{:S(2)}, u32[]{:S(2)}) async-start(f32[8,256,512]{2,1,0:T(8,128)} %bitcast.150), calls=%async_computation.2 | async-start | bytes 8388608 | tf_op jit(solution)/shard_map/all_to_all | solution.py:51
  166.5 359.3 %reduce-scatter.5.cloned.1.call-start = ((), (), s32[]{:S(2)}) async-start(), calls=%async_computation.5 | async-start | bytes 8912896 | tf_op jit(solution)/shard_map/reduce_scatter | solution.py:62
  272.8 1.9 copy-start
  299.6 2.4 copy-start.1
  299.7 2.8 copy-start.7
  301.8 3.7 copy-start.5
  305.4 2.6 copy-start.2
  339.8 2.1 copy-start.3
  368.8 4.1 copy-start.8
  372.9 1.8 copy-start.4
  401.3 1.0 copy-start.10
  431.6 0.9 copy-start.13
  432.5 1.2 copy-start.12
  460.6 27.8 %copy-start.15 = (f32[1024,128]{1,0:T(8,128)}, f32[1024,128]{1,0:T(8,128)S(1)}, u32[]{:S(2)}) copy-start(f32[1024,128]{1,0:T(8,128)S(1)} %fusion.45) | copy-start | bytes 1572868
  460.6 57.0 %slice-start = ((f32[1664,128]{1,0:T(8,128)}), f32[896,128]{1,0:T(8,128)S(1)}, s32[]{:S(2)}) async-start(f32[1664,128]{1,0:T(8,128)} %copy-done.5), calls=%async_computation.7 | async-start | bytes 917504 | tf_op jit(solution)/shard_map/slice | solution.py:95
  460.6 57.0 %copy-start.24 = (f32[128,128]{1,0:T(8,128)S(1)}, f32[128,128]{1,0:T(8,128)}, u32[]{:S(2)}) copy-start(f32[128,128]{1,0:T(8,128)} %get-tuple-element.106) | copy-start | bytes 196612
  460.7 57.1 %copy-start.6 = (f32[1664,128]{1,0:T(8,128)S(1)}, f32[1664,128]{1,0:T(8,128)}, u32[]{:S(2)}) copy-start(f32[1664,128]{1,0:T(8,128)} %copy-done.5) | copy-start | bytes 2555908
  462.7 1.0 copy-start.19
  478.3 39.7 %copy-start.25 = (f32[128,128]{1,0:T(8,128)S(1)}, f32[128,128]{1,0:T(8,128)}, u32[]{:S(2)}) copy-start(f32[128,128]{1,0:T(8,128)} %get-tuple-element.104) | copy-start | bytes 196612
  490.0 27.8 %copy-start.17 = (f32[896,128]{1,0:T(8,128)}, f32[896,128]{1,0:T(8,128)S(1)}, u32[]{:S(2)}) copy-start(f32[896,128]{1,0:T(8,128)S(1)} %fusion.47) | copy-start | bytes 1376260
  490.0 28.1 %slice-start.1 = ((f32[1408,128]{1,0:T(8,128)}), f32[640,128]{1,0:T(8,128)S(1)}, s32[]{:S(2)}) async-start(f32[1408,128]{1,0:T(8,128)} %copy-done.8), calls=%async_computation.8 | async-start | bytes 655360 | tf_op jit(solution)/shard_map/slice | solution.py:95
  491.6 0.8 copy-start.21
  492.4 28.1 %slice-start.2 = ((f32[1152,128]{1,0:T(8,128)}), f32[384,128]{1,0:T(8,128)S(1)}, s32[]{:S(2)}) async-start(f32[1152,128]{1,0:T(8,128)} %copy-done.13), calls=%async_computation.9 | async-start | bytes 393216 | tf_op jit(solution)/shard_map/slice | solution.py:95
  506.0 15.6 %slice-start.3 = ((f32[1024,128]{1,0:T(8,128)}), f32[256,128]{1,0:T(8,128)S(1)}, s32[]{:S(2)}) async-start(f32[1024,128]{1,0:T(8,128)} %copy-done.15), calls=%async_computation.10 | async-start | bytes 262144 | tf_op jit(solution)/shard_map/slice | solution.py:95
  517.8 4.9 copy-start.26
  517.8 5.1 copy-start.27
  517.8 4.8 slice-start.4
  517.8 5.1 copy-start.28
  517.9 5.4 %copy-start.9 = (f32[1408,128]{1,0:T(8,128)S(1)}, f32[1408,128]{1,0:T(8,128)}, u32[]{:S(2)}) copy-start(f32[1408,128]{1,0:T(8,128)} %copy-done.8) | copy-start | bytes 2162692
  517.9 5.4 %copy-start.11 = (f32[1280,128]{1,0:T(8,128)S(1)}, f32[1280,128]{1,0:T(8,128)}, u32[]{:S(2)}) copy-start(f32[1280,128]{1,0:T(8,128)} %copy-done.10) | copy-start | bytes 1966084
  518.0 5.4 %copy-start.14 = (f32[1152,128]{1,0:T(8,128)S(1)}, f32[1152,128]{1,0:T(8,128)}, u32[]{:S(2)}) copy-start(f32[1152,128]{1,0:T(8,128)} %copy-done.13) | copy-start | bytes 1769476
  518.0 5.4 %copy-start.16 = (f32[1024,128]{1,0:T(8,128)S(1)}, f32[1024,128]{1,0:T(8,128)}, u32[]{:S(2)}) copy-start(f32[1024,128]{1,0:T(8,128)} %copy-done.15) | copy-start | bytes 1572868
  519.3 4.2 copy-start.18
  520.5 3.1 copy-start.22
  524.1 1.7 copy-start.20
Sparse Core Ops, SparseCore 0:
  73.6 74.3 reduce-scatter.2
  151.1 95.1 all-gather.2
  250.1 82.6 reduce-scatter.4

commit v7 on v6

--- a/solution.py
+++ b/solution.py
@@ -10,7 +10,7 @@
 FACTOR_TILE = 128
 
 
-def shards(child_front, child_panel, parent_front, tile_map, tile_count):
+def shards_body(child_front, child_panel, parent_front, tile_map, tile_count):
     highest = lax.Precision.HIGHEST
     high = lax.Precision.HIGH
     panel_count = lax.axis_size("panel")
@@ -28,18 +28,35 @@
 
     panel_all = child_panel[0]
     own_panel = lax.dynamic_slice_in_dim(panel_all, panel_id * child_rows, child_rows, 0)
-    update = child_front[0] - lax.dot_general(
-        own_panel, panel_all, (((1,), (1,)), ((), ())), preferred_element_type=jnp.float32
-    )
     mapped = tile_map[0]
     live_tiles = jnp.arange(tiles_child, dtype=jnp.int32) < tile_count[0]
     everywhere = jnp.arange(tiles_front, dtype=jnp.int32)
     chosen = ((mapped[None, :] == everywhere[:, None]) & live_tiles[None, :]).astype(jnp.float32)
+    lead = min(pivot_span, CB)
+    lead_tiles = lead // TILE
+    pivot_tiles = pivot_span // TILE
+
+    def child_update(first, count):
+        return child_front[0][:, first : first + count] - lax.dot_general(
+            own_panel,
+            panel_all[first : first + count],
+            (((1,), (1,)), ((), ())),
+            preferred_element_type=jnp.float32,
+        )
+
+    update_lead = child_update(0, lead)
+    placed_pivot = jnp.einsum(
+        "rtb,ft->rfb",
+        update_lead.reshape(child_rows, lead_tiles, TILE),
+        chosen[:pivot_tiles, :lead_tiles],
+        precision=highest,
+    ).reshape(child_rows, pivot_span)
+    update = jnp.concatenate([update_lead, child_update(lead, CB - lead)], axis=1)
     placed = jnp.einsum(
         "rtb,ft->rfb", update.reshape(child_rows, tiles_child, TILE), chosen, precision=highest
     ).reshape(child_rows, NF)
     regular = placed.reshape(child_rows, panel_count, col_width).transpose(1, 0, 2)
-    pivot_slabs = placed[:, :pivot_span].reshape(child_rows, panel_count, slab).transpose(1, 0, 2)
+    pivot_slabs = placed_pivot.reshape(child_rows, panel_count, slab).transpose(1, 0, 2)
     parent_slabs = parent_front.reshape(height, slabs_per_block, slab).transpose(1, 0, 2)
     parent_slabs = jnp.tile(parent_slabs, (panel_count // slabs_per_block, 1, 1))
     dest = jnp.arange(panel_count, dtype=jnp.int32)
@@ -82,7 +99,7 @@
     solved = []
     for k in range(blocks):
         lo, hi = k * FACTOR_TILE, (k + 1) * FACTOR_TILE
-        diag = lax.linalg.cholesky(work[lo:hi, lo:hi], symmetrize_input=True)
+        diag = lax.linalg.cholesky(work[lo:hi, lo:hi], symmetrize_input=False)
         diag = jnp.tril(diag)
         inverse = lax.linalg.triangular_solve(diag, eye, left_side=True, lower=True)
         below = jnp.dot(work[hi:, lo:hi], inverse.T, precision=high)
@@ -128,5 +145,5 @@
         P("leaf"),
     )
     return jax.shard_map(
-        shards, mesh=mesh, in_specs=placed, out_specs=P("leaf", "panel"), check_vma=False
+        shards_body, mesh=mesh, in_specs=placed, out_specs=P("leaf", "panel"), check_vma=False
     )

time: 547 us -> 529 us (0.967)
  local copies, waits for them, and re-layouts: 80.6 us -> 61.9 us
  waiting for transfers between devices: 165 us -> 174 us
    all_to_all x2, waiting for transfers between devices: 91.4 us -> 100 us  [the longest x1 74.1 us: shards_body(): lax.all_to_all(regular, 'panel', split_axis=0, concat_axis=0, tiled=True)]
    unnamed x70 -> x65, local copies, waits for them, and re-layouts: 22.6 us -> 19.3 us
    dot_general x20 -> x22, matrix products: 57.7 us -> 55.2 us  [the longest x7 18.9 us: shards_body(): jnp.dot(below, below[:pivot_span - hi].T, precision=high)]
    another operation x3 -> x5, local copies, waits for them, and re-layouts: 11.8 us -> 12.4 us  [the longest x2 11.8 us: shards_body(): placed.reshape(child_rows, panel_count, col_width).transpose(1, 0, 2)]
  transfers between devices with their start and end apart: 5 -> 5, of which waited for: 3 -> 3; matrix products, arithmetic and copies ran while one was open for 54% -> 55% of each run, Pallas kernels for 0% -> 0%
where the time goes in v7:
time: 529 us; the launch traced here: 521 us
  other arithmetic  199 us (38%)
  waiting for transfers between devices  174 us (33%)
  local copies, waits for them, and re-layouts  61.9 us (12%)
  matrix products  57.7 us (11%)
  between operations  15 us (3%)
  starting transfers between devices  13.5 us (3%)
    another operation x24, other arithmetic, shards_body(): diag = lax.linalg.cholesky(work[lo:hi, lo:hi], symmetrize_input=False)  99.4 us
    another operation x16, other arithmetic, shards_body(): inverse = lax.linalg.triangular_solve(diag, eye, left_side=True, lower=True)  89.9 us
    all_to_all x1, waiting for transfers between devices, shards_body(): lax.all_to_all(regular, 'panel', split_axis=0, concat_axis=0, tiled=True)  74.1 us
    reduce_scatter x1, waiting for transfers between devices, shards_body(): lax.psum_scatter(slab_rows, 'leaf', scatter_dimension=0, tiled=True)  73.9 us
    all_to_all x1, waiting for transfers between devices, shards_body(): lax.all_to_all(send_slabs, 'panel', split_axis=0, concat_axis=0, tiled=True)  26.2 us
    unnamed x65, local copies, waits for them, and re-layouts  19.3 us
    dot_general x7, matrix products, shards_body(): jnp.dot(below, below[:pivot_span - hi].T, precision=high)  18.9 us
    dot_general x2, matrix products, child_update(): lax.dot_general(own_panel, panel_all[first:first + count], (((1,), (1,)),...  13 us
  transfers between devices with their start and end apart: 5, of which 3 were waited for; matrix products, arithmetic and copies ran while one was open for 55% of the time, Pallas kernels for 0%

profile of v7, /device:TPU:1, one launch (start us, length us, event | category | flops | bytes accessed | tf_op | source)
XLA Modules:
  0.0 521.1 jit_solution(2134042817393083230)
XLA Ops:
  7.2 1.2 reshape.273
  9.3 6.6 %fusion.23 = f32[256,1024]{1,0:T(8,128)S(1)} fusion(bf16[1,2048,4096]{2,1,0:T(8,128)(2,1)} %param.23, s32[]{:T(128)S(6)} %select_n.103, f32[256,2048]{1,0:T(8,128)} %bitcast.150), kind=kOutput, calls=%fused_computation.37 | convolution fusion | flops 2147745792 | bytes 12582916 | tf_op jit(solution)/shard_map/dot_general | solution.py:40
  19.3 1.5 pad_maximum_fusion
  20.8 6.0 %all-to-all-start = ((f32[8,256,256]{2,1,0:T(8,128)}), f32[8,256,256]{2,1,0:T(8,128)S(1)}, u32[]{:S(2)}, u32[]{:S(2)}) async-start(f32[8,256,256]{2,1,0:T(8,128)} %pad_maximum_fusion), calls=%async_computation | async-start | bytes 4194304 | tf_op jit(solution)/shard_map/all_to_all | solution.py:67
  26.7 26.2 %all-to-all-done = f32[8,256,256]{2,1,0:T(8,128)S(1)} async-done(((f32[8,256,256]{2,1,0:T(8,128)}), f32[8,256,256]{2,1,0:T(8,128)S(1)}, u32[]{:S(2)}, u32[]{:S(2)}) %all-to-all-start) | async-done | bytes 2097184 | tf_op jit(solution)/shard_map/all_to_all | solution.py:67
  53.7 1.2 fusion.14
  54.9 2.0 copy.19
  57.4 73.9 %reduce-scatter.3.cloned.1.call-done = f32[256,128]{1,0:T(8,128)} async-done(((f32[4096,128]{1,0:T(8,128)}), f32[256,128]{1,0:T(8,128)}) %reduce-scatter.3.cloned.1.call-update) | async-done | bytes 131088 | tf_op jit(solution)/shard_map/reduce_scatter | solution.py:76
  131.3 6.4 %fusion.28 = f32[256,1024]{1,0:T(8,128)S(1)} fusion(bf16[1,2048,4096]{2,1,0:T(8,128)(2,1)} %param.23, s32[]{:T(128)S(6)} %select_n.103, f32[256,2048]{1,0:T(8,128)S(1)} %bitcast.151), kind=kOutput, calls=%fused_computation.38 | convolution fusion | flops 2147745792 | bytes 12582916 | tf_op jit(solution)/shard_map/dot_general | solution.py:40
  138.8 3.7 convolution_bitcast_fusion
  142.5 5.2 %reshape_reshape.7 = f32[256,8,512]{2,1,0:T(8,128)} reshape(f32[256,16,256]{2,1,0:T(8,128)} %convolution_bitcast_fusion) | data formatting | bytes 8388608 | tf_op jit(solution)/shard_map/reshape;reshape | solution.py:58
  147.7 6.6 %copy.44 = f32[256,8,512]{2,0,1:T(8,128)} copy(f32[256,8,512]{2,1,0:T(8,128)} %reshape_reshape.7) | data formatting | bytes 8388608 | tf_op jit(solution)/shard_map/reshape;reshape | solution.py:58
  154.3 6.9 %all-to-all-start.1 = ((f32[8,256,512]{2,1,0:T(8,128)}), f32[8,256,512]{2,1,0:T(8,128)}, u32[]{:S(2)}, u32[]{:S(2)}) async-start(f32[8,256,512]{2,1,0:T(8,128)} %bitcast.135), calls=%async_computation.2 | async-start | bytes 8388608 | tf_op jit(solution)/shard_map/all_to_all | solution.py:68
  161.7 74.1 %all-to-all-done.1 = f32[8,256,512]{2,1,0:T(8,128)} async-done(((f32[8,256,512]{2,1,0:T(8,128)}), f32[8,256,512]{2,1,0:T(8,128)}, u32[]{:S(2)}, u32[]{:S(2)}) %all-to-all-start.1) | async-done | bytes 4194336 | tf_op jit(solution)/shard_map/all_to_all | solution.py:68
  235.8 4.8 copy.26
  240.6 5.0 fusion
  245.6 8.3 %copy.27 = f32[16,256,512]{2,1,0:T(8,128)} copy(f32[16,256,512]{2,0,1:T(8,128)S(1)} %fusion) | data formatting | bytes 16777216 | tf_op jit(solution)/shard_map/ft,tbc->fbc/dot_general | solution.py:78
  254.6 1.3 dynamic-slice_bitcast_fusion.1
  256.5 1.7 dynamic-slice_bitcast_fusion
  258.3 1.2 copy.22
  259.5 2.8 slice.376
  262.3 2.4 copy.20
  266.8 11.7 %custom-call.20 = f32[128,128]{1,0:T(8,128)S(1)} custom-call(f32[128,128]{1,0:T(8,128)S(1)} %slice.377), custom_call_target="Cholesky" | custom-call | tf_op jit(solution)/shard_map/cholesky/custom-call.1 | solution.py:102
  279.2 1.3 select_bitcast_fusion.7
  280.5 10.2 %custom-call.21 = f32[1,128,128]{1,2,0:T(8,128)S(1)} custom-call(f32[1,128,128]{2,1,0:T(8,128)S(1)} %get-tuple-element.105), custom_call_target="InvertDiagBlocksLowerTriangular" | custom-call | tf_op jit(solution)/shard_map/triangular_solve/custom-call.0 | solution.py:104
  291.0 3.3 constant_dynamic-update-slice_fusion
  295.5 3.0 slice_add_fusion
  298.5 2.5 copy-done.1
  301.0 11.7 %custom-call.22 = f32[128,128]{1,0:T(8,128)S(1)} custom-call(f32[128,128]{1,0:T(8,128)S(1)} %slice.381), custom_call_target="Cholesky" | custom-call | tf_op jit(solution)/shard_map/cholesky/custom-call.1 | solution.py:102
  313.4 1.3 select_bitcast_fusion.6
  314.7 9.8 %custom-call.23 = f32[1,128,128]{1,2,0:T(8,128)S(1)} custom-call(f32[1,128,128]{2,1,0:T(8,128)S(1)} %get-tuple-element.103), custom_call_target="InvertDiagBlocksLowerTriangular" | custom-call | tf_op jit(solution)/shard_map/triangular_solve/custom-call.0 | solution.py:104
  325.0 1.6 fusion.45
  326.6 4.6 slice_add_fusion.1
  331.2 2.1 copy-done.2
  333.4 11.7 %custom-call.24 = f32[128,128]{1,0:T(8,128)S(1)} custom-call(f32[128,128]{1,0:T(8,128)S(1)} %slice.385), custom_call_target="Cholesky" | custom-call | tf_op jit(solution)/shard_map/cholesky/custom-call.1 | solution.py:102
  345.7 1.3 select_bitcast_fusion.5
  347.0 9.8 %custom-call.25 = f32[1,128,128]{1,2,0:T(8,128)S(1)} custom-call(f32[1,128,128]{2,1,0:T(8,128)S(1)} %get-tuple-element.101), custom_call_target="InvertDiagBlocksLowerTriangular" | custom-call | tf_op jit(solution)/shard_map/triangular_solve/custom-call.0 | solution.py:104
  357.1 1.6 fusion.47
  358.7 4.1 slice_add_fusion.2
  362.8 1.8 copy-done.3
  364.6 11.9 %custom-call.26 = f32[128,128]{1,0:T(8,128)S(1)} custom-call(f32[128,128]{1,0:T(8,128)S(1)} %slice.389), custom_call_target="Cholesky" | custom-call | tf_op jit(solution)/shard_map/cholesky/custom-call.1 | solution.py:102
  377.2 1.3 select_bitcast_fusion.4
  378.5 9.8 %custom-call.27 = f32[1,128,128]{1,2,0:T(8,128)S(1)} custom-call(f32[1,128,128]{2,1,0:T(8,128)S(1)} %get-tuple-element.99), custom_call_target="InvertDiagBlocksLowerTriangular" | custom-call | tf_op jit(solution)/shard_map/triangular_solve/custom-call.0 | solution.py:104
  388.6 1.5 fusion.49
  391.1 3.0 fusion.10
  394.1 11.7 %custom-call.28 = f32[128,128]{1,0:T(8,128)S(1)} custom-call(f32[128,128]{1,0:T(8,128)S(1)} %slice.393), custom_call_target="Cholesky" | custom-call | tf_op jit(solution)/shard_map/cholesky/custom-call.1 | solution.py:102
  406.5 1.3 select_bitcast_fusion.3
  407.8 10.2 %custom-call.29 = f32[1,128,128]{1,2,0:T(8,128)S(1)} custom-call(f32[1,128,128]{2,1,0:T(8,128)S(1)} %get-tuple-element.97), custom_call_target="InvertDiagBlocksLowerTriangular" | custom-call | tf_op jit(solution)/shard_map/triangular_solve/custom-call.0 | solution.py:104
  419.6 1.2 copy-done.10
  420.8 11.7 %custom-call.30 = f32[128,128]{1,0:T(8,128)S(1)} custom-call(f32[128,128]{1,0:T(8,128)S(1)} %slice.397), custom_call_target="Cholesky" | custom-call | tf_op jit(solution)/shard_map/cholesky/custom-call.1 | solution.py:102
  433.2 1.3 select_bitcast_fusion.2
  434.5 9.8 %custom-call.31 = f32[1,128,128]{1,2,0:T(8,128)S(1)} custom-call(f32[1,128,128]{2,1,0:T(8,128)S(1)} %get-tuple-element.95), custom_call_target="InvertDiagBlocksLowerTriangular" | custom-call | tf_op jit(solution)/shard_map/triangular_solve/custom-call.0 | solution.py:104
  444.6 1.5 fusion.53
  446.9 1.8 fusion.22
  449.7 11.8 %custom-call.32 = f32[128,128]{1,0:T(8,128)S(1)} custom-call(f32[128,128]{1,0:T(8,128)S(1)} %slice.401), custom_call_target="Cholesky" | custom-call | tf_op jit(solution)/shard_map/cholesky/custom-call.1 | solution.py:102
  462.2 1.2 select_bitcast_fusion.1
  463.4 9.8 %custom-call.33 = f32[1,128,128]{1,2,0:T(8,128)S(1)} custom-call(f32[1,128,128]{2,1,0:T(8,128)S(1)} %get-tuple-element.93), custom_call_target="InvertDiagBlocksLowerTriangular" | custom-call | tf_op jit(solution)/shard_map/triangular_solve/custom-call.0 | solution.py:104
  473.5 1.4 fusion.55
  474.9 1.6 fusion.42
  477.3 11.7 %custom-call.34 = f32[128,128]{1,0:T(8,128)S(1)} custom-call(f32[128,128]{1,0:T(8,128)S(1)} %slice.405), custom_call_target="Cholesky" | custom-call | tf_op jit(solution)/shard_map/cholesky/custom-call.1 | solution.py:102
  489.6 1.2 select_bitcast_fusion
  490.8 10.4 %custom-call.35 = f32[1,128,128]{1,2,0:T(8,128)} custom-call(f32[1,128,128]{2,1,0:T(8,128)S(1)} %get-tuple-element.91), custom_call_target="InvertDiagBlocksLowerTriangular" | custom-call | tf_op jit(solution)/shard_map/triangular_solve/custom-call.0 | solution.py:104
  509.1 1.6 copy-done.17
  510.9 3.5 fusion.39
  (149 shorter events, 31.6 us)
Async XLA Ops:
  9.2 7.1 %copy-start.25 = (s32[1,8]{1,0:T(1,128)S(1)}, s32[1,8]{1,0:T(1,128)}, u32[]{:S(2)}) copy-start(s32[1,8]{1,0:T(1,128)} %param.25) | copy-start | bytes 100
  20.8 32.2 %all-to-all-start = ((f32[8,256,256]{2,1,0:T(8,128)}), f32[8,256,256]{2,1,0:T(8,128)S(1)}, u32[]{:S(2)}, u32[]{:S(2)}) async-start(f32[8,256,256]{2,1,0:T(8,128)} %pad_maximum_fusion), calls=%async_computation | async-start | bytes 4194304 | tf_op jit(solution)/shard_map/all_to_all | solution.py:67
  26.7 104.6 %reduce-scatter.3.cloned.1.call-start = ((), (), s32[]{:S(2)}) async-start(), calls=%async_computation.4 | async-start | bytes 2228224 | tf_op jit(solution)/shard_map/reduce_scatter | solution.py:76
  53.7 77.7 %copy-start.26 = (f32[1,256,2048]{2,1,0:T(8,128)S(1)}, f32[1,256,2048]{2,1,0:T(8,128)}, u32[]{:S(2)}) copy-start(f32[1,256,2048]{2,1,0:T(8,128)} %param.22) | copy-start | bytes 6291460
  56.9 197.7 %all-gather.3.cloned.1.call-start = ((), (), s32[]{:S(2)}) async-start(), calls=%async_computation.6 | async-start | bytes 16908288 | tf_op jit(solution)/shard_map/all_gather | solution.py:83
  154.3 7.0 %copy-start.19 = (f32[256,512]{1,0:T(8,128)S(1)}, f32[256,512]{1,0:T(8,128)}, u32[]{:S(2)}) copy-start(f32[256,512]{1,0:T(8,128)} %param.24) | copy-start | bytes 1572868
  154.3 81.5 %all-to-all-start.1 = ((f32[8,256,512]{2,1,0:T(8,128)}), f32[8,256,512]{2,1,0:T(8,128)}, u32[]{:S(2)}, u32[]{:S(2)}) async-start(f32[8,256,512]{2,1,0:T(8,128)} %bitcast.135), calls=%async_computation.2 | async-start | bytes 8388608 | tf_op jit(solution)/shard_map/all_to_all | solution.py:68
  161.2 349.7 %reduce-scatter.5.cloned.1.call-start = ((), (), s32[]{:S(2)}) async-start(), calls=%async_computation.5 | async-start | bytes 8912896 | tf_op jit(solution)/shard_map/reduce_scatter | solution.py:79
  264.7 2.1 copy-start
  295.5 3.0 copy-start.4
  298.5 2.5 copy-start.1
  331.2 2.1 copy-start.2
  358.7 4.1 copy-start.6
  362.8 1.8 copy-start.3
  390.1 1.0 copy-start.8
  418.7 0.9 copy-start.11
  419.6 1.2 copy-start.10
  420.8 80.4 %slice-start = ((f32[1664,128]{1,0:T(8,128)}), f32[896,128]{1,0:T(8,128)S(1)}, s32[]{:S(2)}) async-start(f32[1664,128]{1,0:T(8,128)} %copy-done.4), calls=%async_computation.7 | async-start | bytes 917504 | tf_op jit(solution)/shard_map/slice | solution.py:112
  420.8 80.4 %copy-start.22 = (f32[128,128]{1,0:T(8,128)S(1)}, f32[128,128]{1,0:T(8,128)}, u32[]{:S(2)}) copy-start(f32[128,128]{1,0:T(8,128)} %get-tuple-element.106) | copy-start | bytes 196612
  444.6 56.7 %copy-start.5 = (f32[1664,128]{1,0:T(8,128)S(1)}, f32[1664,128]{1,0:T(8,128)}, u32[]{:S(2)}) copy-start(f32[1664,128]{1,0:T(8,128)} %copy-done.4) | copy-start | bytes 2555908
  446.1 0.8 copy-start.13
  448.7 1.0 copy-start.18
  449.7 52.9 %slice-start.1 = ((f32[1408,128]{1,0:T(8,128)}), f32[640,128]{1,0:T(8,128)S(1)}, s32[]{:S(2)}) async-start(f32[1408,128]{1,0:T(8,128)} %copy-done.6), calls=%async_computation.8 | async-start | bytes 655360 | tf_op jit(solution)/shard_map/slice | solution.py:112
  474.9 26.4 %copy-start.15 = (f32[896,128]{1,0:T(8,128)}, f32[896,128]{1,0:T(8,128)S(1)}, u32[]{:S(2)}) copy-start(f32[896,128]{1,0:T(8,128)S(1)} %fusion.55) | copy-start | bytes 1376260
  474.9 30.0 %slice-start.2 = ((f32[1152,128]{1,0:T(8,128)}), f32[384,128]{1,0:T(8,128)S(1)}, s32[]{:S(2)}) async-start(f32[1152,128]{1,0:T(8,128)} %copy-done.11), calls=%async_computation.9 | async-start | bytes 393216 | tf_op jit(solution)/shard_map/slice | solution.py:112
  476.5 0.8 copy-start.20
  501.3 6.8 %copy-start.23 = (f32[128,128]{1,0:T(8,128)S(1)}, f32[128,128]{1,0:T(8,128)}, u32[]{:S(2)}) copy-start(f32[128,128]{1,0:T(8,128)} %get-tuple-element.92) | copy-start | bytes 196612
  501.4 5.6 %slice-start.3 = ((f32[896,128]{1,0:T(8,128)}), f32[128,128]{1,0:T(8,128)S(1)}, s32[]{:S(2)}) async-start(f32[896,128]{1,0:T(8,128)} %copy-done.15), calls=%async_computation.10 | async-start | bytes 131072 | tf_op jit(solution)/shard_map/slice | solution.py:112
  501.4 6.8 %copy-start.24 = (f32[1,128,128]{1,2,0:T(8,128)S(1)}, f32[1,128,128]{1,2,0:T(8,128)}, u32[]{:S(2)}) copy-start(f32[1,128,128]{1,2,0:T(8,128)} %custom-call.35) | copy-start | bytes 196612
  501.4 7.1 %copy-start.7 = (f32[1408,128]{1,0:T(8,128)S(1)}, f32[1408,128]{1,0:T(8,128)}, u32[]{:S(2)}) copy-start(f32[1408,128]{1,0:T(8,128)} %copy-done.6) | copy-start | bytes 2162692
  501.4 7.1 %copy-start.9 = (f32[1280,128]{1,0:T(8,128)S(1)}, f32[1280,128]{1,0:T(8,128)}, u32[]{:S(2)}) copy-start(f32[1280,128]{1,0:T(8,128)} %copy-done.8) | copy-start | bytes 1966084
  501.4 7.1 %copy-start.12 = (f32[1152,128]{1,0:T(8,128)S(1)}, f32[1152,128]{1,0:T(8,128)}, u32[]{:S(2)}) copy-start(f32[1152,128]{1,0:T(8,128)} %copy-done.11) | copy-start | bytes 1769476
  501.5 7.1 %copy-start.14 = (f32[1024,128]{1,0:T(8,128)S(1)}, f32[1024,128]{1,0:T(8,128)}, u32[]{:S(2)}) copy-start(f32[1024,128]{1,0:T(8,128)} %copy-done.13) | copy-start | bytes 1572868
  501.6 7.1 %copy-start.16 = (f32[896,128]{1,0:T(8,128)S(1)}, f32[896,128]{1,0:T(8,128)}, u32[]{:S(2)}) copy-start(f32[896,128]{1,0:T(8,128)} %copy-done.15) | copy-start | bytes 1376260
  502.6 6.1 %copy-start.21 = (f32[896,128]{1,0:T(8,128)S(1)}, f32[896,128]{1,0:T(8,128)}, u32[]{:S(2)}) copy-start(f32[896,128]{1,0:T(8,128)} %copy-done.20) | copy-start | bytes 1376260
  509.1 1.7 copy-start.17
Sparse Core Ops, SparseCore 0:
  57.0 74.2 reduce-scatter.2
  134.4 105.3 all-gather.2
  254.0 82.3 reduce-scatter.4

commit v8 on v7

--- a/solution.py
+++ b/solution.py
@@ -64,8 +64,11 @@
         (dest // slabs_per_block == panel_id)[:, None, None], parent_slabs, 0.0
     )
     send_slabs = jnp.concatenate([pivot_slabs, parent_slabs], axis=2)
-    moved_slabs = lax.all_to_all(send_slabs, "panel", split_axis=0, concat_axis=0, tiled=True)
-    moved = lax.all_to_all(regular, "panel", split_axis=0, concat_axis=0, tiled=True)
+    both = lax.all_to_all(
+        jnp.concatenate([send_slabs, regular], axis=2), "panel", split_axis=0, concat_axis=0, tiled=True
+    )
+    moved_slabs = both[:, :, : 2 * slab]
+    moved = both[:, :, 2 * slab :]
     parent_slab = jnp.sum(moved_slabs[:, :, slab:], axis=0)
     targets = jnp.arange(leaf_count * height // TILE, dtype=jnp.int32)
     picked = ((mapped[None, :] == targets[:, None]) & live_tiles[None, :]).astype(jnp.float32)
@@ -73,7 +76,10 @@
     slab_sources = jnp.concatenate([moved_slabs[:, :, :slab], parent_slab[None]], axis=0)
     slab_rows = jnp.einsum("ft,tbc->fbc", picked, slab_sources, precision=highest)
     slab_rows = slab_rows.reshape(leaf_count * height, slab)
-    my_slab = lax.psum_scatter(slab_rows, "leaf", scatter_dimension=0, tiled=True)
+    pieces = lax.all_to_all(
+        slab_rows.reshape(leaf_count, height, slab), "leaf", split_axis=0, concat_axis=0, tiled=True
+    )
+    my_slab = jnp.sum(pieces, axis=0)
     sources = jnp.concatenate([moved, parent_front[None]], axis=0)
     summed = jnp.einsum("ft,tbc->fbc", picked, sources, precision=highest)
     front_block = lax.psum_scatter(

time: 529 us -> 529 us (level)
  waiting for transfers between devices: 174 us -> 137 us
  blocking collectives: 0 us -> 34.9 us
  starting transfers between devices: 13.5 us -> 6.22 us
    reduce_scatter x1 -> x0, waiting for transfers between devices: 73.9 us -> none  [shards_body(): lax.psum_scatter(slab_rows, 'leaf', scatter_dimension=0, tiled=True)]
    all_gather x1, waiting for transfers between devices: 0.02 us -> 66.1 us  [shards_body(): gathered = lax.all_gather(my_slab, ('leaf', 'panel'), axis=0, tiled=False)]
    all_to_all x0 -> x1, blocking collectives: none -> 34.9 us  [shards_body(): lax.all_to_all(slab_rows.reshape(leaf_count, height, slab), 'leaf', split...]
    all_to_all x2 -> x1, waiting for transfers between devices: 100 us -> 71.3 us  [shards_body(): lax.all_to_all(jnp.concatenate([send_slabs, regular], axis=2), 'panel', s...]
    all_to_all x2 -> x1, starting transfers between devices: 12.8 us -> 6 us  [shards_body(): lax.all_to_all(jnp.concatenate([send_slabs, regular], axis=2), 'panel', s...]
    unnamed x65 -> x72, local copies, waits for them, and re-layouts: 19.3 us -> 24 us
  transfers between devices with their start and end apart: 5 -> 3, of which waited for: 3 -> 2; matrix products, arithmetic and copies ran while one was open for 55% -> 50% of each run, Pallas kernels for 0% -> 0%
where the time goes in v8:
time: 529 us; the launch traced here: 520 us
  other arithmetic  204 us (39%)
  waiting for transfers between devices  137 us (26%)
  local copies, waits for them, and re-layouts  64.1 us (12%)
  matrix products  57.1 us (11%)
  blocking collectives  34.9 us (7%)
  between operations  16.7 us (3%)
  starting transfers between devices  6.22 us (1%)
    another operation x24, other arithmetic, shards_body(): diag = lax.linalg.cholesky(work[lo:hi, lo:hi], symmetrize_input=False)  99.5 us
    another operation x16, other arithmetic, shards_body(): inverse = lax.linalg.triangular_solve(diag, eye, left_side=True, lower=True)  90.1 us
    all_to_all x1, waiting for transfers between devices, shards_body(): lax.all_to_all(jnp.concatenate([send_slabs, regular], axis=2), 'panel', s...  71.3 us
    all_gather x1, waiting for transfers between devices, shards_body(): gathered = lax.all_gather(my_slab, ('leaf', 'panel'), axis=0, tiled=False)  66.1 us
    all_to_all x1, blocking collectives, shards_body(): lax.all_to_all(slab_rows.reshape(leaf_count, height, slab), 'leaf', split...  34.9 us
    unnamed x72, local copies, waits for them, and re-layouts  24 us
    dot_general x7, matrix products, shards_body(): jnp.dot(below, below[:pivot_span - hi].T, precision=high)  18.8 us
    dot_general x2, matrix products, child_update(): lax.dot_general(own_panel, panel_all[first:first + count], (((1,), (1,)),...  11.7 us
  transfers between devices with their start and end apart: 3, of which 2 were waited for; matrix products, arithmetic and copies ran while one was open for 50% of the time, Pallas kernels for 0%

profile of v8, /device:TPU:1, one launch (start us, length us, event | category | flops | bytes accessed | tf_op | source)
XLA Modules:
  0.0 520.3 jit_solution(16496310734824956868)
XLA Ops:
  7.4 6.7 %fusion.23 = f32[256,1024]{1,0:T(8,128)S(1)} fusion(bf16[1,2048,4096]{2,1,0:T(8,128)(2,1)} %param.23, s32[]{:T(128)S(6)} %select_n.103, f32[256,2048]{1,0:T(8,128)} %bitcast.148), kind=kOutput, calls=%fused_computation.37 | convolution fusion | flops 2147745792 | bytes 12582916 | tf_op jit(solution)/shard_map/dot_general | solution.py:40
  14.1 2.3 copy-done.29
  16.4 5.0 fusion.28
  23.6 1.7 pad_maximum_fusion.1
  25.3 2.1 convolution_bitcast_fusion.1
  27.4 2.7 reshape_reshape.6
  30.1 1.4 copy.45
  32.4 3.7 convolution_bitcast_fusion
  36.1 5.6 %reshape_reshape.7 = f32[256,8,512]{2,1,0:T(8,128)} reshape(f32[256,16,256]{2,1,0:T(8,128)} %convolution_bitcast_fusion) | data formatting | bytes 8388608 | tf_op jit(solution)/shard_map/reshape;reshape | solution.py:58
  41.7 4.7 copy.44
  46.6 3.2 pad_maximum_fusion
  49.8 6.0 %all-to-all-start = ((f32[8,256,768]{2,1,0:T(8,128)}), f32[8,256,768]{2,1,0:T(8,128)}, u32[]{:S(2)}, u32[]{:S(2)}) async-start(f32[8,256,768]{2,1,0:T(8,128)} %pad_maximum_fusion), calls=%async_computation | async-start | bytes 12582912 | tf_op jit(solution)/shard_map/all_to_all | solution.py:67
  55.8 71.3 %all-to-all-done = f32[8,256,768]{2,1,0:T(8,128)} async-done(((f32[8,256,768]{2,1,0:T(8,128)}), f32[8,256,768]{2,1,0:T(8,128)}, u32[]{:S(2)}, u32[]{:S(2)}) %all-to-all-start) | async-done | bytes 6291488 | tf_op jit(solution)/shard_map/all_to_all | solution.py:67
  127.1 1.7 fusion.97
  131.3 34.9 %all_to_all.10 = f32[16,256,128]{2,1,0:T(8,128)S(1)} all-to-all(f32[16,256,128]{2,1,0:T(8,128)S(1)} %copy.20), channel_id=1, replica_groups=mesh['leaf'=16,'panel'=8] {'leaf'}, dimensions={0} | all-to-all | bytes 4194304 | tf_op jit(solution)/shard_map/all_to_all | solution.py:79
  167.6 2.9 slice.423
  170.6 2.4 copy.31
  173.0 5.0 fusion
  178.0 8.3 %copy.26 = f32[16,256,512]{2,1,0:T(8,128)} copy(f32[16,256,512]{2,0,1:T(8,128)S(1)} %fusion) | data formatting | bytes 16777216 | tf_op jit(solution)/shard_map/ft,tbc->fbc/dot_general | solution.py:84
  187.0 66.1 %all-gather.3.cloned.1.call-done = f32[32768,128]{1,0:T(8,128)} async-done(((f32[256,128]{1,0:T(8,128)}), f32[32768,128]{1,0:T(8,128)}) %all-gather.3.cloned.1.call-update) | async-done | bytes 16777232 | tf_op jit(solution)/shard_map/all_gather | solution.py:89
  253.1 1.3 dynamic-slice_bitcast_fusion.1
  255.1 1.8 dynamic-slice_bitcast_fusion
  258.0 2.5 slice.384
  260.6 2.4 copy.21
  265.1 11.7 %custom-call.20 = f32[128,128]{1,0:T(8,128)S(1)} custom-call(f32[128,128]{1,0:T(8,128)S(1)} %slice.385), custom_call_target="Cholesky" | custom-call | tf_op jit(solution)/shard_map/cholesky/custom-call.1 | solution.py:108
  277.4 1.3 select_bitcast_fusion.7
  278.7 10.2 %custom-call.21 = f32[1,128,128]{1,2,0:T(8,128)S(1)} custom-call(f32[1,128,128]{2,1,0:T(8,128)S(1)} %get-tuple-element.105), custom_call_target="InvertDiagBlocksLowerTriangular" | custom-call | tf_op jit(solution)/shard_map/triangular_solve/custom-call.0 | solution.py:110
  289.2 3.2 constant_dynamic-update-slice_fusion
  293.6 3.0 slice_add_fusion
  296.6 2.5 copy-done.1
  299.2 11.7 %custom-call.22 = f32[128,128]{1,0:T(8,128)S(1)} custom-call(f32[128,128]{1,0:T(8,128)S(1)} %slice.389), custom_call_target="Cholesky" | custom-call | tf_op jit(solution)/shard_map/cholesky/custom-call.1 | solution.py:108
  311.6 1.3 select_bitcast_fusion.6
  312.8 9.9 %custom-call.23 = f32[1,128,128]{1,2,0:T(8,128)S(1)} custom-call(f32[1,128,128]{2,1,0:T(8,128)S(1)} %get-tuple-element.103), custom_call_target="InvertDiagBlocksLowerTriangular" | custom-call | tf_op jit(solution)/shard_map/triangular_solve/custom-call.0 | solution.py:110
  323.1 1.6 fusion.45
  324.7 4.5 slice_add_fusion.1
  329.2 2.1 copy-done.2
  331.4 11.7 %custom-call.24 = f32[128,128]{1,0:T(8,128)S(1)} custom-call(f32[128,128]{1,0:T(8,128)S(1)} %slice.393), custom_call_target="Cholesky" | custom-call | tf_op jit(solution)/shard_map/cholesky/custom-call.1 | solution.py:108
  343.7 1.3 select_bitcast_fusion.5
  345.0 9.8 %custom-call.25 = f32[1,128,128]{1,2,0:T(8,128)S(1)} custom-call(f32[1,128,128]{2,1,0:T(8,128)S(1)} %get-tuple-element.101), custom_call_target="InvertDiagBlocksLowerTriangular" | custom-call | tf_op jit(solution)/shard_map/triangular_solve/custom-call.0 | solution.py:110
  355.1 1.6 fusion.47
  356.7 4.1 slice_add_fusion.2
  360.8 1.8 copy-done.3
  362.6 11.9 %custom-call.26 = f32[128,128]{1,0:T(8,128)S(1)} custom-call(f32[128,128]{1,0:T(8,128)S(1)} %slice.397), custom_call_target="Cholesky" | custom-call | tf_op jit(solution)/shard_map/cholesky/custom-call.1 | solution.py:108
  375.2 1.3 select_bitcast_fusion.4
  376.5 9.8 %custom-call.27 = f32[1,128,128]{1,2,0:T(8,128)S(1)} custom-call(f32[1,128,128]{2,1,0:T(8,128)S(1)} %get-tuple-element.99), custom_call_target="InvertDiagBlocksLowerTriangular" | custom-call | tf_op jit(solution)/shard_map/triangular_solve/custom-call.0 | solution.py:110
  386.6 1.5 fusion.49
  389.1 3.0 fusion.10
  392.1 11.7 %custom-call.28 = f32[128,128]{1,0:T(8,128)S(1)} custom-call(f32[128,128]{1,0:T(8,128)S(1)} %slice.401), custom_call_target="Cholesky" | custom-call | tf_op jit(solution)/shard_map/cholesky/custom-call.1 | solution.py:108
  404.5 1.3 select_bitcast_fusion.3
  405.7 10.3 %custom-call.29 = f32[1,128,128]{1,2,0:T(8,128)S(1)} custom-call(f32[1,128,128]{2,1,0:T(8,128)S(1)} %get-tuple-element.97), custom_call_target="InvertDiagBlocksLowerTriangular" | custom-call | tf_op jit(solution)/shard_map/triangular_solve/custom-call.0 | solution.py:110
  418.9 11.7 %custom-call.30 = f32[128,128]{1,0:T(8,128)S(1)} custom-call(f32[128,128]{1,0:T(8,128)S(1)} %slice.405), custom_call_target="Cholesky" | custom-call | tf_op jit(solution)/shard_map/cholesky/custom-call.1 | solution.py:108
  431.2 1.3 select_bitcast_fusion.2
  432.5 9.8 %custom-call.31 = f32[1,128,128]{1,2,0:T(8,128)S(1)} custom-call(f32[1,128,128]{2,1,0:T(8,128)S(1)} %get-tuple-element.95), custom_call_target="InvertDiagBlocksLowerTriangular" | custom-call | tf_op jit(solution)/shard_map/triangular_solve/custom-call.0 | solution.py:110
  442.6 1.5 fusion.53
  444.9 1.8 fusion.22
  447.8 11.9 %custom-call.32 = f32[128,128]{1,0:T(8,128)S(1)} custom-call(f32[128,128]{1,0:T(8,128)S(1)} %slice.409), custom_call_target="Cholesky" | custom-call | tf_op jit(solution)/shard_map/cholesky/custom-call.1 | solution.py:108
  461.5 9.8 %custom-call.33 = f32[1,128,128]{1,2,0:T(8,128)S(1)} custom-call(f32[1,128,128]{2,1,0:T(8,128)S(1)} %get-tuple-element.93), custom_call_target="InvertDiagBlocksLowerTriangular" | custom-call | tf_op jit(solution)/shard_map/triangular_solve/custom-call.0 | solution.py:110
  471.6 1.4 fusion.55
  473.0 1.6 fusion.42
  475.4 11.7 %custom-call.34 = f32[128,128]{1,0:T(8,128)S(1)} custom-call(f32[128,128]{1,0:T(8,128)S(1)} %slice.413), custom_call_target="Cholesky" | custom-call | tf_op jit(solution)/shard_map/cholesky/custom-call.1 | solution.py:108
  487.8 1.2 select_bitcast_fusion
  489.1 10.4 %custom-call.35 = f32[1,128,128]{1,2,0:T(8,128)} custom-call(f32[1,128,128]{2,1,0:T(8,128)S(1)} %get-tuple-element.91), custom_call_target="InvertDiagBlocksLowerTriangular" | custom-call | tf_op jit(solution)/shard_map/triangular_solve/custom-call.0 | solution.py:110
  507.3 1.7 copy-done.18
  509.1 3.5 fusion.39
  (153 shorter events, 34.5 us)
Async XLA Ops:
  7.4 9.1 %copy-start.29 = (bf16[1,2048,4096]{2,1,0:T(8,128)(2,1)S(1)}, bf16[1,2048,4096]{2,1,0:T(8,128)(2,1)}, u32[]{:S(2)}) copy-start(bf16[1,2048,4096]{2,1,0:T(8,128)(2,1)} %param.23) | copy-start | bytes 50331652
  16.4 6.7 %copy-start.17 = (f32[256,1024]{1,0:T(8,128)}, f32[256,1024]{1,0:T(8,128)S(1)}, u32[]{:S(2)}) copy-start(f32[256,1024]{1,0:T(8,128)S(1)} %fusion.23) | copy-start | bytes 3145732
  16.4 5.7 %copy-start.20 = (f32[256,512]{1,0:T(8,128)S(1)}, f32[256,512]{1,0:T(8,128)}, u32[]{:S(2)}) copy-start(f32[256,512]{1,0:T(8,128)} %param.24) | copy-start | bytes 1572868
  22.1 3.2 copy-start.28
  41.7 4.7 copy-start.22
  49.8 77.3 %all-to-all-start = ((f32[8,256,768]{2,1,0:T(8,128)}), f32[8,256,768]{2,1,0:T(8,128)}, u32[]{:S(2)}, u32[]{:S(2)}) async-start(f32[8,256,768]{2,1,0:T(8,128)} %pad_maximum_fusion), calls=%async_computation | async-start | bytes 12582912 | tf_op jit(solution)/shard_map/all_to_all | solution.py:67
  55.8 197.3 %all-gather.3.cloned.1.call-start = ((), (), s32[]{:S(2)}) async-start(), calls=%async_computation.4 | async-start | bytes 16908288 | tf_op jit(solution)/shard_map/all_gather | solution.py:89
  131.3 35.9 %copy-start.21 = (f32[256,512]{1,0:T(8,128)S(1)}, f32[256,512]{1,0:T(8,128)}, u32[]{:S(2)}) copy-start(f32[256,512]{1,0:T(8,128)} %param.24) | copy-start | bytes 1572868
  167.0 342.1 %reduce-scatter.2.cloned.1.call-start = ((), (), s32[]{:S(2)}) async-start(), calls=%async_computation.3 | async-start | bytes 8912896 | tf_op jit(solution)/shard_map/reduce_scatter | solution.py:85
  263.0 2.0 copy-start
  293.6 3.0 copy-start.4
  296.6 2.5 copy-start.1
  329.2 2.1 copy-start.2
  356.7 4.1 copy-start.6
  360.8 1.8 copy-start.3
  388.1 1.0 copy-start.8
  416.7 0.9 copy-start.11
  417.6 1.2 copy-start.10
  418.8 80.7 %slice-start = ((f32[1664,128]{1,0:T(8,128)}), f32[896,128]{1,0:T(8,128)S(1)}, s32[]{:S(2)}) async-start(f32[1664,128]{1,0:T(8,128)} %copy-done.4), calls=%async_computation.5 | async-start | bytes 917504 | tf_op jit(solution)/shard_map/slice | solution.py:118
  418.8 80.7 %copy-start.25 = (f32[128,128]{1,0:T(8,128)S(1)}, f32[128,128]{1,0:T(8,128)}, u32[]{:S(2)}) copy-start(f32[128,128]{1,0:T(8,128)} %get-tuple-element.106) | copy-start | bytes 196612
  442.6 56.9 %copy-start.5 = (f32[1664,128]{1,0:T(8,128)S(1)}, f32[1664,128]{1,0:T(8,128)}, u32[]{:S(2)}) copy-start(f32[1664,128]{1,0:T(8,128)} %copy-done.4) | copy-start | bytes 2555908
  444.1 0.8 copy-start.13
  446.8 1.0 copy-start.19
  447.7 53.1 %slice-start.1 = ((f32[1408,128]{1,0:T(8,128)}), f32[640,128]{1,0:T(8,128)S(1)}, s32[]{:S(2)}) async-start(f32[1408,128]{1,0:T(8,128)} %copy-done.6), calls=%async_computation.6 | async-start | bytes 655360 | tf_op jit(solution)/shard_map/slice | solution.py:118
  473.0 26.5 %copy-start.15 = (f32[896,128]{1,0:T(8,128)}, f32[896,128]{1,0:T(8,128)S(1)}, u32[]{:S(2)}) copy-start(f32[896,128]{1,0:T(8,128)S(1)} %fusion.55) | copy-start | bytes 1376260
  473.0 30.1 %slice-start.2 = ((f32[1152,128]{1,0:T(8,128)}), f32[384,128]{1,0:T(8,128)S(1)}, s32[]{:S(2)}) async-start(f32[1152,128]{1,0:T(8,128)} %copy-done.11), calls=%async_computation.7 | async-start | bytes 393216 | tf_op jit(solution)/shard_map/slice | solution.py:118
  474.6 0.8 copy-start.23
  499.5 6.8 %copy-start.26 = (f32[128,128]{1,0:T(8,128)S(1)}, f32[128,128]{1,0:T(8,128)}, u32[]{:S(2)}) copy-start(f32[128,128]{1,0:T(8,128)} %get-tuple-element.92) | copy-start | bytes 196612
  499.6 5.6 %slice-start.3 = ((f32[896,128]{1,0:T(8,128)}), f32[128,128]{1,0:T(8,128)S(1)}, s32[]{:S(2)}) async-start(f32[896,128]{1,0:T(8,128)} %copy-done.15), calls=%async_computation.8 | async-start | bytes 131072 | tf_op jit(solution)/shard_map/slice | solution.py:118
  499.6 6.8 %copy-start.27 = (f32[1,128,128]{1,2,0:T(8,128)S(1)}, f32[1,128,128]{1,2,0:T(8,128)}, u32[]{:S(2)}) copy-start(f32[1,128,128]{1,2,0:T(8,128)} %custom-call.35) | copy-start | bytes 196612
  499.6 7.1 %copy-start.7 = (f32[1408,128]{1,0:T(8,128)S(1)}, f32[1408,128]{1,0:T(8,128)}, u32[]{:S(2)}) copy-start(f32[1408,128]{1,0:T(8,128)} %copy-done.6) | copy-start | bytes 2162692
  499.7 7.1 %copy-start.9 = (f32[1280,128]{1,0:T(8,128)S(1)}, f32[1280,128]{1,0:T(8,128)}, u32[]{:S(2)}) copy-start(f32[1280,128]{1,0:T(8,128)} %copy-done.8) | copy-start | bytes 1966084
  499.7 7.1 %copy-start.12 = (f32[1152,128]{1,0:T(8,128)S(1)}, f32[1152,128]{1,0:T(8,128)}, u32[]{:S(2)}) copy-start(f32[1152,128]{1,0:T(8,128)} %copy-done.11) | copy-start | bytes 1769476
  499.8 7.1 %copy-start.14 = (f32[1024,128]{1,0:T(8,128)S(1)}, f32[1024,128]{1,0:T(8,128)}, u32[]{:S(2)}) copy-start(f32[1024,128]{1,0:T(8,128)} %copy-done.13) | copy-start | bytes 1572868
  499.8 7.1 %copy-start.16 = (f32[896,128]{1,0:T(8,128)S(1)}, f32[896,128]{1,0:T(8,128)}, u32[]{:S(2)}) copy-start(f32[896,128]{1,0:T(8,128)} %copy-done.15) | copy-start | bytes 1376260
  500.9 6.1 %copy-start.24 = (f32[896,128]{1,0:T(8,128)S(1)}, f32[896,128]{1,0:T(8,128)}, u32[]{:S(2)}) copy-start(f32[896,128]{1,0:T(8,128)} %copy-done.23) | copy-start | bytes 1376260
  507.3 1.7 copy-start.18
Sparse Core Ops, SparseCore 0:
  167.1 85.9 all-gather.2
Sparse Core Ops, SparseCore 1:
  186.4 102.7 reduce-scatter.1

commit v9 on v7

--- a/solution.py
+++ b/solution.py
@@ -73,7 +73,11 @@
     slab_sources = jnp.concatenate([moved_slabs[:, :, :slab], parent_slab[None]], axis=0)
     slab_rows = jnp.einsum("ft,tbc->fbc", picked, slab_sources, precision=highest)
     slab_rows = slab_rows.reshape(leaf_count * height, slab)
-    my_slab = lax.psum_scatter(slab_rows, "leaf", scatter_dimension=0, tiled=True)
+    slab_rows = slab_rows + 0.0 * regular[0, 0, 0]
+    pieces = lax.all_to_all(
+        slab_rows.reshape(leaf_count, height, slab), "leaf", split_axis=0, concat_axis=0, tiled=True
+    )
+    my_slab = jnp.sum(pieces, axis=0)
     sources = jnp.concatenate([moved, parent_front[None]], axis=0)
     summed = jnp.einsum("ft,tbc->fbc", picked, sources, precision=highest)
     front_block = lax.psum_scatter(
@@ -100,7 +104,6 @@
     for k in range(blocks):
         lo, hi = k * FACTOR_TILE, (k + 1) * FACTOR_TILE
         diag = lax.linalg.cholesky(work[lo:hi, lo:hi], symmetrize_input=False)
-        diag = jnp.tril(diag)
         inverse = lax.linalg.triangular_solve(diag, eye, left_side=True, lower=True)
         below = jnp.dot(work[hi:, lo:hi], inverse.T, precision=high)
         if hi < pivot_span:
@@ -113,7 +116,7 @@
             )
         )
         solved.append(below[pivot_span - hi :])
-    factor = jnp.concatenate(factor_cols, axis=1)
+    factor = jnp.tril(jnp.concatenate(factor_cols, axis=1))
     solved = jnp.concatenate(solved, axis=1)
 
     factor_rows = lax.dynamic_slice_in_dim(

time: 529 us -> 462 us (0.87)
  waiting for transfers between devices: 174 us -> 73.5 us
  blocking collectives: 0 us -> 34.7 us
    reduce_scatter x1 -> x0, waiting for transfers between devices: 73.9 us -> none  [shards_body(): lax.psum_scatter(slab_rows, 'leaf', scatter_dimension=0, tiled=True)]
    all_to_all x0 -> x1, blocking collectives: none -> 34.7 us  [shards_body(): lax.all_to_all(slab_rows.reshape(leaf_count, height, slab), 'leaf', split...]
    all_to_all x1, waiting for transfers between devices: 26.2 us -> 1.48 us  [shards_body(): lax.all_to_all(send_slabs, 'panel', split_axis=0, concat_axis=0, tiled=True)]
    all_to_all x1, waiting for transfers between devices: 74.1 us -> 55.3 us  [shards_body(): lax.all_to_all(regular, 'panel', split_axis=0, concat_axis=0, tiled=True)]
    all_gather x1, waiting for transfers between devices: 0.02 us -> 16.7 us  [shards_body(): gathered = lax.all_gather(my_slab, ('leaf', 'panel'), axis=0, tiled=False)]
    unnamed x65 -> x67, local copies, waits for them, and re-layouts: 19.3 us -> 20.5 us
  transfers between devices with their start and end apart: 5 -> 4, of which waited for: 3 -> 3; matrix products, arithmetic and copies ran while one was open for 55% -> 62% of each run, Pallas kernels for 0% -> 0%
where the time goes in v9:
time: 462 us; the launch traced here: 456 us
  other arithmetic  199 us (43%)
  waiting for transfers between devices  73.5 us (16%)
  local copies, waits for them, and re-layouts  60.2 us (13%)
  matrix products  58 us (13%)
  blocking collectives  34.7 us (8%)
  between operations  17.4 us (4%)
  starting transfers between devices  13.2 us (3%)
    another operation x24, other arithmetic, shards_body(): diag = lax.linalg.cholesky(work[lo:hi, lo:hi], symmetrize_input=False)  99.5 us
    another operation x16, other arithmetic, shards_body(): inverse = lax.linalg.triangular_solve(diag, eye, left_side=True, lower=True)  90.1 us
    all_to_all x1, waiting for transfers between devices, shards_body(): lax.all_to_all(regular, 'panel', split_axis=0, concat_axis=0, tiled=True)  55.3 us
    all_to_all x1, blocking collectives, shards_body(): lax.all_to_all(slab_rows.reshape(leaf_count, height, slab), 'leaf', split...  34.7 us
    unnamed x67, local copies, waits for them, and re-layouts  20.5 us
    dot_general x7, matrix products, shards_body(): jnp.dot(below, below[:pivot_span - hi].T, precision=high)  19 us
    all_gather x1, waiting for transfers between devices, shards_body(): gathered = lax.all_gather(my_slab, ('leaf', 'panel'), axis=0, tiled=False)  16.7 us
    dot_general x2, matrix products, child_update(): lax.dot_general(own_panel, panel_all[first:first + count], (((1,), (1,)),...  13.2 us
  transfers between devices with their start and end apart: 4, of which 3 were waited for; matrix products, arithmetic and copies ran while one was open for 62% of the time, Pallas kernels for 0%

profile of v9, /device:TPU:1, one launch (start us, length us, event | category | flops | bytes accessed | tf_op | source)
XLA Modules:
  0.0 456.3 jit_solution(5584932075871754959)
XLA Ops:
  10.1 6.6 %fusion.26 = f32[256,1024]{1,0:T(8,128)S(1)} fusion(bf16[1,2048,4096]{2,1,0:T(8,128)(2,1)} %param.23, s32[]{:T(128)S(6)} %select_n.82, f32[256,2048]{1,0:T(8,128)} %bitcast.150), kind=kOutput, calls=%fused_computation.38 | convolution fusion | flops 2147745792 | bytes 12582916 | tf_op jit(solution)/shard_map/dot_general | solution.py:40
  20.1 1.5 pad_maximum_fusion
  21.6 6.0 %all-to-all-start = ((f32[8,256,256]{2,1,0:T(8,128)}), f32[8,256,256]{2,1,0:T(8,128)S(1)}, u32[]{:S(2)}, u32[]{:S(2)}) async-start(f32[8,256,256]{2,1,0:T(8,128)} %pad_maximum_fusion), calls=%async_computation | async-start | bytes 4194304 | tf_op jit(solution)/shard_map/all_to_all | solution.py:67
  28.1 6.6 %fusion.31 = f32[256,1024]{1,0:T(8,128)S(1)} fusion(bf16[1,2048,4096]{2,1,0:T(8,128)(2,1)} %param.23, s32[]{:T(128)S(6)} %select_n.82, f32[256,2048]{1,0:T(8,128)} %bitcast.151), kind=kOutput, calls=%fused_computation.39 | convolution fusion | flops 2147745792 | bytes 12582916 | tf_op jit(solution)/shard_map/dot_general | solution.py:40
  35.7 3.7 convolution_bitcast_fusion
  39.4 5.2 %reshape_reshape.7 = f32[256,8,512]{2,1,0:T(8,128)} reshape(f32[256,16,256]{2,1,0:T(8,128)} %convolution_bitcast_fusion) | data formatting | bytes 8388608 | tf_op jit(solution)/shard_map/reshape;reshape | solution.py:58
  44.6 4.6 %copy.43 = f32[256,8,512]{2,0,1:T(8,128)S(1)} copy(f32[256,8,512]{2,1,0:T(8,128)} %reshape_reshape.7) | data formatting | bytes 8388608 | tf_op jit(solution)/shard_map/reshape;reshape | solution.py:58
  49.2 1.9 copy-done.3
  52.3 1.5 all-to-all-done
  54.5 1.3 fusion.22
  56.5 34.7 %all_to_all.15 = f32[16,256,128]{2,1,0:T(8,128)S(1)} all-to-all(f32[16,256,128]{2,1,0:T(8,128)S(1)} %copy.20), channel_id=1, replica_groups=mesh['leaf'=16,'panel'=8] {'leaf'}, dimensions={0} | all-to-all | bytes 4194304 | tf_op jit(solution)/shard_map/all_to_all | solution.py:77
  91.9 6.6 %all-to-all-start.2 = ((f32[8,256,512]{2,1,0:T(8,128)}), f32[8,256,512]{2,1,0:T(8,128)}, u32[]{:S(2)}, u32[]{:S(2)}) async-start(f32[8,256,512]{2,1,0:T(8,128)} %bitcast.136), calls=%async_computation.2 | async-start | bytes 8388608 | tf_op jit(solution)/shard_map/all_to_all | solution.py:68
  99.1 55.3 %all-to-all-done.2 = f32[8,256,512]{2,1,0:T(8,128)} async-done(((f32[8,256,512]{2,1,0:T(8,128)}), f32[8,256,512]{2,1,0:T(8,128)}, u32[]{:S(2)}, u32[]{:S(2)}) %all-to-all-start.2) | async-done | bytes 4194336 | tf_op jit(solution)/shard_map/all_to_all | solution.py:68
  154.4 4.6 %copy.25 = f32[8,256,512]{2,0,1:T(8,128)S(1)} copy(f32[8,256,512]{2,1,0:T(8,128)} %all-to-all-done.2) | data formatting | bytes 8388608 | tf_op jit(solution)/shard_map/all_to_all | solution.py:68
  159.1 5.0 %fusion = f32[16,256,512]{2,0,1:T(8,128)S(1)} fusion(f32[1,256,512]{2,0,1:T(1,128)S(1)} %broadcast_in_dim.58, f32[8,256,512]{2,0,1:T(8,128)S(1)} %copy.25, pred[16,1]{1,0:T(8,128)(4,1)S(1)} %iota_compare_fusion.11, pred[16,8]{1,0:T(8,128)(4,1)S(1)} %fusion.85), kind=kOutput, calls=%fused_computation | convolution fusion | flops 227672208 | bytes 13107344 | tf_op jit(solution)/shard_map/ft,tbc->fbc/dot_general | solution.py:82
  164.1 8.5 %copy.26 = f32[16,256,512]{2,1,0:T(8,128)} copy(f32[16,256,512]{2,0,1:T(8,128)S(1)} %fusion) | data formatting | bytes 16777216 | tf_op jit(solution)/shard_map/ft,tbc->fbc/dot_general | solution.py:82
  173.2 16.7 %all-gather.3.cloned.1.call-done = f32[32768,128]{1,0:T(8,128)} async-done(((f32[256,128]{1,0:T(8,128)}), f32[32768,128]{1,0:T(8,128)}) %all-gather.3.cloned.1.call-update) | async-done | bytes 16777232 | tf_op jit(solution)/shard_map/all_gather | solution.py:87
  189.9 1.3 dynamic-slice_bitcast_fusion.1
  191.8 1.8 dynamic-slice_bitcast_fusion
  193.6 1.2 copy.23
  194.8 2.7 slice.382
  197.6 2.4 copy.21
  202.1 11.7 %custom-call.20 = f32[128,128]{1,0:T(8,128)S(1)} custom-call(f32[128,128]{1,0:T(8,128)S(1)} %slice.383), custom_call_target="Cholesky" | custom-call | tf_op jit(solution)/shard_map/cholesky/custom-call.1 | solution.py:106
  214.5 1.3 select_bitcast_fusion.7
  215.7 10.2 %custom-call.21 = f32[1,128,128]{1,2,0:T(8,128)S(1)} custom-call(f32[1,128,128]{2,1,0:T(8,128)S(1)} %get-tuple-element.105), custom_call_target="InvertDiagBlocksLowerTriangular" | custom-call | tf_op jit(solution)/shard_map/triangular_solve/custom-call.0 | solution.py:107
  226.2 3.3 constant_dynamic-update-slice_fusion
  230.7 3.0 slice_add_fusion
  233.7 2.5 copy-done.1
  236.3 11.7 %custom-call.22 = f32[128,128]{1,0:T(8,128)S(1)} custom-call(f32[128,128]{1,0:T(8,128)S(1)} %slice.387), custom_call_target="Cholesky" | custom-call | tf_op jit(solution)/shard_map/cholesky/custom-call.1 | solution.py:106
  248.7 1.3 select_bitcast_fusion.6
  249.9 9.8 %custom-call.23 = f32[1,128,128]{1,2,0:T(8,128)S(1)} custom-call(f32[1,128,128]{2,1,0:T(8,128)S(1)} %get-tuple-element.103), custom_call_target="InvertDiagBlocksLowerTriangular" | custom-call | tf_op jit(solution)/shard_map/triangular_solve/custom-call.0 | solution.py:107
  260.2 1.6 fusion.48
  261.8 4.5 slice_add_fusion.1
  266.4 2.1 copy-done.2
  268.5 11.7 %custom-call.24 = f32[128,128]{1,0:T(8,128)S(1)} custom-call(f32[128,128]{1,0:T(8,128)S(1)} %slice.391), custom_call_target="Cholesky" | custom-call | tf_op jit(solution)/shard_map/cholesky/custom-call.1 | solution.py:106
  280.9 1.3 select_bitcast_fusion.5
  282.2 9.8 %custom-call.25 = f32[1,128,128]{1,2,0:T(8,128)S(1)} custom-call(f32[1,128,128]{2,1,0:T(8,128)S(1)} %get-tuple-element.101), custom_call_target="InvertDiagBlocksLowerTriangular" | custom-call | tf_op jit(solution)/shard_map/triangular_solve/custom-call.0 | solution.py:107
  292.3 1.6 fusion.50
  293.8 4.1 slice_add_fusion.2
  298.0 1.8 copy-done.4
  299.7 11.9 %custom-call.26 = f32[128,128]{1,0:T(8,128)S(1)} custom-call(f32[128,128]{1,0:T(8,128)S(1)} %slice.395), custom_call_target="Cholesky" | custom-call | tf_op jit(solution)/shard_map/cholesky/custom-call.1 | solution.py:106
  312.3 1.3 select_bitcast_fusion.4
  313.6 9.8 %custom-call.27 = f32[1,128,128]{1,2,0:T(8,128)S(1)} custom-call(f32[1,128,128]{2,1,0:T(8,128)S(1)} %get-tuple-element.99), custom_call_target="InvertDiagBlocksLowerTriangular" | custom-call | tf_op jit(solution)/shard_map/triangular_solve/custom-call.0 | solution.py:107
  323.7 1.5 fusion.52
  326.2 3.0 fusion.10
  329.2 11.7 %custom-call.28 = f32[128,128]{1,0:T(8,128)S(1)} custom-call(f32[128,128]{1,0:T(8,128)S(1)} %slice.399), custom_call_target="Cholesky" | custom-call | tf_op jit(solution)/shard_map/cholesky/custom-call.1 | solution.py:106
  341.6 1.3 select_bitcast_fusion.3
  342.9 10.2 %custom-call.29 = f32[1,128,128]{1,2,0:T(8,128)S(1)} custom-call(f32[1,128,128]{2,1,0:T(8,128)S(1)} %get-tuple-element.97), custom_call_target="InvertDiagBlocksLowerTriangular" | custom-call | tf_op jit(solution)/shard_map/triangular_solve/custom-call.0 | solution.py:107
  354.7 1.2 copy-done.11
  355.9 11.7 %custom-call.30 = f32[128,128]{1,0:T(8,128)S(1)} custom-call(f32[128,128]{1,0:T(8,128)S(1)} %slice.403), custom_call_target="Cholesky" | custom-call | tf_op jit(solution)/shard_map/cholesky/custom-call.1 | solution.py:106
  368.3 1.3 select_bitcast_fusion.2
  369.6 9.8 %custom-call.31 = f32[1,128,128]{1,2,0:T(8,128)S(1)} custom-call(f32[1,128,128]{2,1,0:T(8,128)S(1)} %get-tuple-element.95), custom_call_target="InvertDiagBlocksLowerTriangular" | custom-call | tf_op jit(solution)/shard_map/triangular_solve/custom-call.0 | solution.py:107
  379.7 1.5 fusion.56
  381.2 2.0 fusion.25
  384.3 11.9 %custom-call.32 = f32[128,128]{1,0:T(8,128)S(1)} custom-call(f32[128,128]{1,0:T(8,128)S(1)} %slice.407), custom_call_target="Cholesky" | custom-call | tf_op jit(solution)/shard_map/cholesky/custom-call.1 | solution.py:106
  396.8 1.2 select_bitcast_fusion.1
  398.1 9.8 %custom-call.33 = f32[1,128,128]{1,2,0:T(8,128)S(1)} custom-call(f32[1,128,128]{2,1,0:T(8,128)S(1)} %get-tuple-element.93), custom_call_target="InvertDiagBlocksLowerTriangular" | custom-call | tf_op jit(solution)/shard_map/triangular_solve/custom-call.0 | solution.py:107
  408.2 1.4 fusion.58
  409.6 1.5 fusion.45
  412.0 11.7 %custom-call.34 = f32[128,128]{1,0:T(8,128)S(1)} custom-call(f32[128,128]{1,0:T(8,128)S(1)} %slice.411), custom_call_target="Cholesky" | custom-call | tf_op jit(solution)/shard_map/cholesky/custom-call.1 | solution.py:106
  424.4 1.3 select_bitcast_fusion
  425.7 10.4 %custom-call.35 = f32[1,128,128]{1,2,0:T(8,128)} custom-call(f32[1,128,128]{2,1,0:T(8,128)S(1)} %get-tuple-element.91), custom_call_target="InvertDiagBlocksLowerTriangular" | custom-call | tf_op jit(solution)/shard_map/triangular_solve/custom-call.0 | solution.py:107
  443.2 1.6 copy-done.18
  445.1 3.5 fusion.42
  (152 shorter events, 33.4 us)
Async XLA Ops:
  10.1 7.1 %copy-start.27 = (s32[1,8]{1,0:T(1,128)S(1)}, s32[1,8]{1,0:T(1,128)}, u32[]{:S(2)}) copy-start(s32[1,8]{1,0:T(1,128)} %param.25) | copy-start | bytes 100
  21.6 32.2 %all-to-all-start = ((f32[8,256,256]{2,1,0:T(8,128)}), f32[8,256,256]{2,1,0:T(8,128)S(1)}, u32[]{:S(2)}, u32[]{:S(2)}) async-start(f32[8,256,256]{2,1,0:T(8,128)} %pad_maximum_fusion), calls=%async_computation | async-start | bytes 4194304 | tf_op jit(solution)/shard_map/all_to_all | solution.py:67
  27.6 162.3 %all-gather.3.cloned.1.call-start = ((), (), s32[]{:S(2)}) async-start(), calls=%async_computation.5 | async-start | bytes 16908288 | tf_op jit(solution)/shard_map/all_gather | solution.py:87
  49.2 1.9 copy-start.3
  91.9 6.8 %copy-start.20 = (f32[256,512]{1,0:T(8,128)S(1)}, f32[256,512]{1,0:T(8,128)}, u32[]{:S(2)}) copy-start(f32[256,512]{1,0:T(8,128)} %param.24) | copy-start | bytes 1572868
  91.9 62.5 %all-to-all-start.2 = ((f32[8,256,512]{2,1,0:T(8,128)}), f32[8,256,512]{2,1,0:T(8,128)}, u32[]{:S(2)}, u32[]{:S(2)}) async-start(f32[8,256,512]{2,1,0:T(8,128)} %bitcast.136), calls=%async_computation.2 | async-start | bytes 8388608 | tf_op jit(solution)/shard_map/all_to_all | solution.py:68
  98.6 346.6 %reduce-scatter.2.cloned.1.call-start = ((), (), s32[]{:S(2)}) async-start(), calls=%async_computation.4 | async-start | bytes 8912896 | tf_op jit(solution)/shard_map/reduce_scatter | solution.py:83
  200.0 2.1 copy-start
  230.7 3.0 copy-start.5
  233.7 2.5 copy-start.1
  266.4 2.1 copy-start.2
  293.8 4.1 copy-start.7
  297.9 1.8 copy-start.4
  325.2 1.0 copy-start.9
  353.8 0.9 copy-start.12
  354.7 1.2 copy-start.11
  379.7 56.4 %slice-start = ((f32[1664,128]{1,0:T(8,128)}), f32[896,128]{1,0:T(8,128)S(1)}, s32[]{:S(2)}) async-start(f32[1664,128]{1,0:T(8,128)} %copy-done.5), calls=%async_computation.6 | async-start | bytes 917504 | tf_op jit(solution)/shard_map/slice | solution.py:115
  379.7 56.4 %copy-start.23 = (f32[128,128]{1,0:T(8,128)S(1)}, f32[128,128]{1,0:T(8,128)}, u32[]{:S(2)}) copy-start(f32[128,128]{1,0:T(8,128)} %get-tuple-element.106) | copy-start | bytes 196612
  381.2 26.7 %copy-start.14 = (f32[1024,128]{1,0:T(8,128)}, f32[1024,128]{1,0:T(8,128)S(1)}, u32[]{:S(2)}) copy-start(f32[1024,128]{1,0:T(8,128)S(1)} %fusion.56) | copy-start | bytes 1572868
  381.2 55.0 %copy-start.6 = (f32[1664,128]{1,0:T(8,128)S(1)}, f32[1664,128]{1,0:T(8,128)}, u32[]{:S(2)}) copy-start(f32[1664,128]{1,0:T(8,128)} %copy-done.5) | copy-start | bytes 2555908
  383.3 1.0 copy-start.19
  408.2 29.3 %slice-start.1 = ((f32[1408,128]{1,0:T(8,128)}), f32[640,128]{1,0:T(8,128)S(1)}, s32[]{:S(2)}) async-start(f32[1408,128]{1,0:T(8,128)} %copy-done.7), calls=%async_computation.7 | async-start | bytes 655360 | tf_op jit(solution)/shard_map/slice | solution.py:115
  409.6 26.6 %copy-start.16 = (f32[896,128]{1,0:T(8,128)}, f32[896,128]{1,0:T(8,128)S(1)}, u32[]{:S(2)}) copy-start(f32[896,128]{1,0:T(8,128)S(1)} %fusion.58) | copy-start | bytes 1376260
  411.2 0.8 copy-start.21
  412.0 27.8 %slice-start.2 = ((f32[1152,128]{1,0:T(8,128)}), f32[384,128]{1,0:T(8,128)S(1)}, s32[]{:S(2)}) async-start(f32[1152,128]{1,0:T(8,128)} %copy-done.12), calls=%async_computation.8 | async-start | bytes 393216 | tf_op jit(solution)/shard_map/slice | solution.py:115
  424.4 16.5 %slice-start.3 = ((f32[1024,128]{1,0:T(8,128)}), f32[256,128]{1,0:T(8,128)S(1)}, s32[]{:S(2)}) async-start(f32[1024,128]{1,0:T(8,128)} %copy-done.14), calls=%async_computation.9 | async-start | bytes 262144 | tf_op jit(solution)/shard_map/slice | solution.py:115
  436.2 5.8 %copy-start.24 = (f32[128,128]{1,0:T(8,128)S(1)}, f32[128,128]{1,0:T(8,128)}, u32[]{:S(2)}) copy-start(f32[128,128]{1,0:T(8,128)} %get-tuple-element.94) | copy-start | bytes 196612
  436.2 6.0 %copy-start.25 = (f32[128,128]{1,0:T(8,128)S(1)}, f32[128,128]{1,0:T(8,128)}, u32[]{:S(2)}) copy-start(f32[128,128]{1,0:T(8,128)} %get-tuple-element.92) | copy-start | bytes 196612
  436.3 5.7 %slice-start.4 = ((f32[896,128]{1,0:T(8,128)}), f32[128,128]{1,0:T(8,128)S(1)}, s32[]{:S(2)}) async-start(f32[896,128]{1,0:T(8,128)} %copy-done.16), calls=%async_computation.10 | async-start | bytes 131072 | tf_op jit(solution)/shard_map/slice | solution.py:115
  436.3 6.0 %copy-start.26 = (f32[1,128,128]{1,2,0:T(8,128)S(1)}, f32[1,128,128]{1,2,0:T(8,128)}, u32[]{:S(2)}) copy-start(f32[1,128,128]{1,2,0:T(8,128)} %custom-call.35) | copy-start | bytes 196612
  436.3 6.3 %copy-start.8 = (f32[1408,128]{1,0:T(8,128)S(1)}, f32[1408,128]{1,0:T(8,128)}, u32[]{:S(2)}) copy-start(f32[1408,128]{1,0:T(8,128)} %copy-done.7) | copy-start | bytes 2162692
  436.4 6.2 %copy-start.10 = (f32[1280,128]{1,0:T(8,128)S(1)}, f32[1280,128]{1,0:T(8,128)}, u32[]{:S(2)}) copy-start(f32[1280,128]{1,0:T(8,128)} %copy-done.9) | copy-start | bytes 1966084
  436.4 6.3 %copy-start.13 = (f32[1152,128]{1,0:T(8,128)S(1)}, f32[1152,128]{1,0:T(8,128)}, u32[]{:S(2)}) copy-start(f32[1152,128]{1,0:T(8,128)} %copy-done.12) | copy-start | bytes 1769476
  437.5 5.3 %copy-start.15 = (f32[1024,128]{1,0:T(8,128)S(1)}, f32[1024,128]{1,0:T(8,128)}, u32[]{:S(2)}) copy-start(f32[1024,128]{1,0:T(8,128)} %copy-done.14) | copy-start | bytes 1572868
  438.6 4.2 copy-start.17
  439.8 3.1 copy-start.22
  443.2 1.7 copy-start.18
Sparse Core Ops, SparseCore 0:
  92.0 97.7 all-gather.2
Sparse Core Ops, SparseCore 1:
  172.6 84.5 reduce-scatter.1
